TPU v7x, 128 devices: a whole 4x4x4 slice. The times are simulated.
128 devices in a mesh: tm: 2 (over core), space: 64 (over z, y, x).
Axes of the slice: x: 4, y: 4, z: 4, core: 2. Of those that a mesh axis runs over, the one named last changes fastest.
Arguments:
- increment_start: float32 [2, 8, 2048, 1024], P('tm', None, 'space'), may hold values from -6 to 6
- dual_model_start: float32 [2, 8, 2048, 1024], P('tm', None, 'space'), may hold values from -6 to 6
- dual_obs_start: bfloat16 [2, 1024, 128], P('tm', 'space'), may hold values from -6 to 6
- model_rhs: float32 [2, 8, 2048, 1024], P('tm', None, 'space'), may hold values from -6 to 6
- err_var: float32 [2, 8, 2048, 1024], P('tm', None, 'space'), may hold values from 0.2 to 2
- decays: float32 [2, 8, 2048, 1024], P('tm', None, 'space'), may hold values from 0.1 to 0.95
- scaling: float32 [8, 2048, 1024], P(None, 'space'), may hold values from 0.5 to 1
- diffusion: float32 [8], replicated, may hold values from 0.05 to 0.24
- owners: int32 [2, 1024], P('tm', 'space'), may hold values from 0 to 63, as said below
- tile_cols: int32 [2, 1024, 128], P('tm', 'space'), may hold values from 0 to 32767, as said below
- jacobian: bfloat16 [2, 1024, 128, 1024], P('tm', 'space'), may hold values from -0.1875 to 0.1875
- innovation: bfloat16 [2, 1024, 128], P('tm', 'space'), may hold values from -6 to 6
- obs_var: bfloat16 [2, 1024, 128], P('tm', 'space'), may hold values from 0.5 to 4
Outputs:
- dual_model: float32 [2, 8, 2048, 1024], P('tm', None, 'space')
- dual_obs: float32 [2, 1024, 128], P('tm', 'space')
- increment: float32 [2, 8, 2048, 1024], P('tm', None, 'space')
Inputs may be any that keep to these rules, and one draw needn't show every extreme that they name: `owners`: in each subwindow at most 2 of the 16 tiles of one device name the same owner, and one owner is named exactly 2 times by the tiles of every device. All 128 cells of a tile lie in one latitude row: tile_cols[k, t, c] // 1024 is the same for every c.
All inputs are finite; a program needn't handle non-finite values.
Results may differ from a plain program's by a relative error of at most 0.0042.
The roundings to bfloat16 on the way count: a program that leaves them out, or rounds other values in their place, can miss the bound.
Values may be sent and summed in bfloat16 or wider, within the bound.
No kernel may reach another device: no remote copies, remote signals or barrier semaphores. Data moves between devices by JAX's collectives and lax.ppermute only.
A program may use at most 256 MiB of HBM per device.

v0:
```python
import jax
import jax.numpy as jnp
from jax import lax
from jax.sharding import PartitionSpec as P

SUBSTEPS = 2
ITERS = 2
LANES = 128


def with_halo(cells, axis, dim, width):
    count = lax.axis_size(axis)
    ends = count - 1
    head = lax.slice_in_dim(cells, 0, width, axis=dim)
    tail = lax.slice_in_dim(cells, cells.shape[dim] - width, cells.shape[dim], axis=dim)
    return jnp.concatenate(
        [
            lax.ppermute(tail, axis, [(i, i + 1) for i in range(ends)]),
            cells,
            lax.ppermute(head, axis, [(i + 1, i) for i in range(ends)]),
        ],
        axis=dim,
    )


def shifted(value, axis, by):
    length = lax.axis_size(axis)
    pairs = [(i, i + by) for i in range(length) if 0 <= i + by < length]
    return lax.ppermute(value, axis, pairs)


def model_apply(current, scaling_ext, diff_coef):
    for step in range(SUBSTEPS):
        gain = scaling_ext[:, step : scaling_ext.shape[1] - step]
        scaled = gain * current
        inner = scaled[:, 1:-1]
        laplace = (
            scaled[:, 2:]
            + scaled[:, :-2]
            + jnp.roll(inner, 1, 2)
            + jnp.roll(inner, -1, 2)
            - 4.0 * inner
        )
        current = gain[:, 1:-1] * (inner + diff_coef * laplace)
    return current


def gather_cols(fields, row_oh, col_oh, group_mask):
    levels, row_count, col_count = fields.shape
    slots, lanes, touched = col_oh.shape
    groups = col_count // lanes
    lines = jnp.einsum(
        "sr,lrc->slc", row_oh, fields.astype(jnp.bfloat16), preferred_element_type=jnp.float32
    ).astype(jnp.bfloat16)
    lines = lines.reshape(slots, levels, groups, lanes)
    picked = jnp.einsum("slab,sbj->slaj", lines, col_oh, preferred_element_type=jnp.float32)
    picked = jnp.sum(picked * group_mask[:, None, :, :], axis=2)
    return picked.astype(jnp.bfloat16)


def spread_cols(values, row_oh, col_oh, group_mask, levels, col_count):
    slots, lanes, touched = col_oh.shape
    groups = col_count // lanes
    row_count = row_oh.shape[1]
    grads = values.reshape(slots, levels, 1, touched)
    placed = grads * group_mask[:, None, :, :].astype(jnp.bfloat16)
    lines = jnp.einsum("slaj,sbj->slab", placed, col_oh, preferred_element_type=jnp.float32)
    total = jnp.einsum(
        "sr,slab->lrab", row_oh, lines.astype(jnp.bfloat16), preferred_element_type=jnp.float32
    )
    return total.reshape(levels, row_count, groups * lanes)


def on_device(
    increment_start,
    dual_model_start,
    dual_obs_start,
    model_rhs,
    err_var,
    decays,
    scaling,
    diffusion,
    owners,
    tile_cols,
    jacobian,
    innovation,
    obs_var,
):
    increment = increment_start[0]
    dual_model = dual_model_start[0]
    rhs_field = model_rhs[0]
    err_field = err_var[0]
    decay_field = decays[0]
    owner_list = owners[0]
    cell_index = tile_cols[0]
    observed = innovation[0].astype(jnp.float32)
    obs_error = obs_var[0].astype(jnp.float32)
    obs_dual = dual_obs_start[0].astype(jnp.float32)
    levels, row_count, col_count = increment.shape
    tiles_here, orows, touch_levels = jacobian.shape[1:]
    touched = touch_levels // levels
    owners_count = lax.axis_size("space")
    tm_count = lax.axis_size("tm")
    tm_here = lax.axis_index("tm")
    capacity = max(2, 2 * tiles_here // owners_count)
    slots_all = owners_count * capacity
    groups = col_count // LANES
    diff_coef = diffusion[:, None, None]

    jac_tiles = jacobian[0]

    one_hot = (owner_list[:, None] == jnp.arange(owners_count, dtype=jnp.int32)[None, :]).astype(
        jnp.int32
    )
    earlier_count = jnp.cumsum(one_hot, axis=0) - one_hot
    slot_rank = jnp.sum(earlier_count * one_hot, axis=1)
    position = owner_list * capacity + slot_rank
    slot_oh = (position[:, None] == jnp.arange(slots_all, dtype=jnp.int32)[None, :]).astype(
        jnp.bfloat16
    )
    packed_cells = jnp.zeros((slots_all, touched), jnp.int32).at[position].set(cell_index)
    requests = lax.all_to_all(
        packed_cells.reshape(owners_count, capacity, touched),
        "space",
        split_axis=0,
        concat_axis=0,
        tiled=True,
    ).reshape(slots_all, touched)
    req_rows = requests[:, 0] // col_count
    req_cols = requests % col_count
    row_oh = (req_rows[:, None] == jnp.arange(row_count, dtype=jnp.int32)[None, :])
    col_oh = (
        (req_cols % LANES)[:, None, :] == jnp.arange(LANES, dtype=jnp.int32)[None, :, None]
    ).astype(jnp.bfloat16)
    group_mask = (
        (req_cols // LANES)[:, None, :] == jnp.arange(groups, dtype=jnp.int32)[None, :, None]
    ).astype(jnp.float32)

    scaling_ext = None
    is_first = (tm_here == 0).astype(jnp.float32)
    is_last = (tm_here == tm_count - 1).astype(jnp.float32)

    for repeat in range(ITERS):
        wanted = gather_cols(increment, row_oh.astype(jnp.bfloat16), col_oh, group_mask)
        tile_grad = jnp.einsum(
            "toj,to->tj", jac_tiles, obs_dual.astype(jnp.bfloat16), preferred_element_type=jnp.float32
        ).astype(jnp.bfloat16)
        sent_grad = jnp.einsum(
            "ts,tjl->slj",
            slot_oh,
            tile_grad.reshape(tiles_here, touched, levels),
            preferred_element_type=jnp.float32,
        ).astype(jnp.bfloat16)
        both = jnp.stack(
            [
                wanted.reshape(owners_count, capacity * levels, touched),
                sent_grad.reshape(owners_count, capacity * levels, touched),
            ],
            axis=1,
        )
        got = lax.all_to_all(both, "space", split_axis=0, concat_axis=0, tiled=True)
        got_cols = got[:, 0].reshape(slots_all, touch_levels)
        got_grad = got[:, 1].reshape(slots_all, touch_levels)
        own_cols = jnp.einsum(
            "ts,slj->tjl",
            slot_oh,
            got_cols.reshape(slots_all, levels, touched),
            preferred_element_type=jnp.float32,
        ).astype(jnp.bfloat16).reshape(tiles_here, touch_levels)
        obs_image = jnp.einsum(
            "toj,tj->to", jac_tiles, own_cols, preferred_element_type=jnp.float32
        )
        adjoint_field = spread_cols(
            got_grad, row_oh.astype(jnp.bfloat16), col_oh, group_mask, levels, col_count
        )

        if tm_count == 2:
            chosen = jnp.where(tm_here == 0, increment, dual_model)
            if scaling_ext is None:
                both_ext = with_halo(jnp.stack([scaling, chosen]), "space", 2, SUBSTEPS)
                scaling_ext, chosen_ext = both_ext[0], both_ext[1]
            else:
                chosen_ext = with_halo(chosen, "space", 1, SUBSTEPS)
            applied = model_apply(chosen_ext, scaling_ext, diff_coef)
            other = lax.ppermute(applied, "tm", [(0, 1), (1, 0)])
            forward = other * (1.0 - is_first)
            backward = other * (1.0 - is_last)
            r_dual = -(dual_model - backward) - adjoint_field
            upward = r_dual + shifted(decay_field * r_dual, "tm", -1)
        else:
            if scaling_ext is None:
                scaling_ext = with_halo(scaling, "space", 1, SUBSTEPS)
            stacked = jnp.stack([increment, dual_model]).reshape(2 * levels, row_count, col_count)
            applied = model_apply(
                with_halo(stacked, "space", 1, SUBSTEPS),
                jnp.concatenate([scaling_ext, scaling_ext]),
                jnp.concatenate([diff_coef, diff_coef]),
            )
            forward = shifted(applied[:levels], "tm", 1)
            backward = shifted(applied[levels:], "tm", -1)
            r_dual = -(dual_model - backward) - adjoint_field
            upward = r_dual + shifted(decay_field * r_dual, "tm", -1)

        obs_dual = obs_dual + (observed - obs_error * obs_dual - obs_image) / obs_error
        r_model = rhs_field - err_field * dual_model - (increment - forward)
        source = r_model - err_field * upward
        along = source
        along = source + decay_field * shifted(along, "tm", 1)
        dual_model = dual_model + upward
        increment = increment + along
    return (dual_model[None], obs_dual[None], increment[None])


def solution(mesh):
    in_specs = (
        P("tm", None, "space", None),
        P("tm", None, "space", None),
        P("tm", "space", None),
        P("tm", None, "space", None),
        P("tm", None, "space", None),
        P("tm", None, "space", None),
        P(None, "space", None),
        P(),
        P("tm", "space"),
        P("tm", "space", None),
        P("tm", "space", None, None),
        P("tm", "space", None),
        P("tm", "space", None),
    )
    out_specs = (P("tm", None, "space", None), P("tm", "space", None), P("tm", None, "space", None))
    return jax.shard_map(
        on_device, mesh=mesh, in_specs=in_specs, out_specs=out_specs, check_vma=False
    )
```

profile of v0, /device:TPU:1, one launch (start us, length us, event | category | flops | bytes accessed | tf_op | source)
XLA Modules:
  0.0 144.1 jit_solution(13807751908596036649)
XLA Ops:
  0.7 1.5 %broadcast_select_fusion.1 = f32[1,8,32,1024]{3,2,1,0:T(8,128)S(1)} fusion(f32[1,8,32,1024]{3,2,1,0:T(8,128)} %param.13, f32[1,8,32,1024]{3,2,1,0:T(8,128)} %param.14, pred[]{:T(512)S(6)} %eq.87), kind=kLoop, calls=%fused_computation.115 | loop fusion | flops 262144 | bytes 3145729 | tf_op jit(solution)/shard_map/jit(_where)/select_n | solution.py:178
  3.0 4.6 %collective-permute-start = (f32[2,8,2,1024]{3,2,1,0:T(2,128)}, f32[2,8,2,1024]{3,2,1,0:T(2,128)}, u32[]{:S(2)}, u32[]{:S(2)}) collective-permute-start(f32[2,8,2,1024]{3,2,1,0:T(2,128)} %get-tuple-element.8), channel_id=1, source_target_pairs={{0,1},{1,2},{2,3},{3,4},{4,5},{5,6},{6,7},{7,8},{8,9},{9,10},{10,1... | collective-permute-start | bytes 393224 | tf_op jit(solution)/shard_map/ppermute | solution.py:18
  10.5 11.5 %all-to-all-start = ((s32[64,2,128]{2,1,0:T(2,128)}), s32[64,2,128]{2,1,0:T(2,128)S(1)}, u32[]{:S(2)}, u32[]{:S(2)}) async-start(s32[64,2,128]{2,1,0:T(2,128)} %bitcast.9), calls=%async_computation | async-start | bytes 131072 | tf_op jit(solution)/shard_map/all_to_all | solution.py:122
  22.0 2.8 %fusion.15 = bf16[16,1,1024]{2,1,0:T(2,128)(2,1)S(1)} fusion(bf16[1,16,128,1024]{3,2,1,0:T(8,128)(2,1)} %param.23, bf16[16,128,1]{1,0,2:T(8,128)(2,1)S(1)} %bitcast.269), kind=kOutput, calls=%fused_computation.13 | convolution fusion | flops 4194304 | bytes 4231168 | tf_op jit(solution)/shard_map/toj,to->tj/dot_general | solution.py:145
  26.3 4.1 %all-to-all-done = s32[64,2,128]{2,1,0:T(2,128)S(1)} async-done(((s32[64,2,128]{2,1,0:T(2,128)}), s32[64,2,128]{2,1,0:T(2,128)S(1)}, u32[]{:S(2)}, u32[]{:S(2)}) %all-to-all-start) | async-done | bytes 65568 | tf_op jit(solution)/shard_map/all_to_all | solution.py:122
  32.8 3.0 %multiply_reduce_fusion.1 = bf16[128,8,128]{2,1,0:T(8,128)(2,1)S(1)} fusion(f32[128,8,128]{2,1,0:T(8,128)S(1)} %get-tuple-element.32, s32[128,128]{1,0:T(8,128)S(1)} %get-tuple-element.35, bf16[128,8,8,128]{3,2,0,1:T(8,128)(2,1)S(1)} %bitcast.253), kind=kOutput, calls=%fused_computation.16 | convolution fusion | flops 272498688 | bytes 2949120 | tf_op jit(solution)/shard_map/slab,sbj->slaj/dot_general | solution.py:56
  36.8 5.9 %all-to-all-start.1 = ((bf16[64,2,16,128]{3,2,1,0:T(8,128)(2,1)}), bf16[64,2,16,128]{3,2,1,0:T(8,128)(2,1)}, u32[]{:S(2)}, u32[]{:S(2)}) async-start(bf16[64,2,16,128]{3,2,1,0:T(8,128)(2,1)} %copy.49), calls=%async_computation.1 | async-start | bytes 1048576 | tf_op jit(solution)/shard_map/all_to_all | solution.py:161
  42.7 1.4 pad_maximum_fusion
  47.9 1.7 %fusion.79 = f32[8,32,1024]{2,1,0:T(8,128)} fusion(f32[8,34,1024]{2,1,0:T(8,128)S(1)} %multiply_multiply_fusion.1, f32[8,32,1023]{2,1,0:T(8,128)S(1)} %get-tuple-element.19, f32[8,32,1]{2,1,0:T(8,128)S(1)} %get-tuple-element.21, f32[8,32,1]{2,1,0:T(8,128)S(1)} %get-tuple-element.20, f32[8,32,1023]{2,1,0:T(8,128)S(1)} %get-tuple-element.18, ...), kind=kLoop, calls=%fused_computation.77 | loop fusion | flops 2621440 | bytes 7340064 | tf_op jit(solution)/shard_map/mul | solution.py:44
  49.5 2.2 %collective-permute-start.2 = (f32[8,32,1024]{2,1,0:T(8,128)}, f32[8,32,1024]{2,1,0:T(8,128)}, u32[]{:S(2)}, u32[]{:S(2)}) collective-permute-start(f32[8,32,1024]{2,1,0:T(8,128)} %fusion.79), channel_id=1, source_target_pairs={{0,64},{64,0},{1,65},{65,1},{2,66},{66,2},{3,67},{67,3},{4,68},{68... | collective-permute-start | bytes 3145736 | tf_op jit(solution)/shard_map/ppermute | solution.py:185
  51.8 1.9 %all-to-all-done.1 = bf16[64,2,16,128]{3,2,1,0:T(8,128)(2,1)} async-done(((bf16[64,2,16,128]{3,2,1,0:T(8,128)(2,1)}), bf16[64,2,16,128]{3,2,1,0:T(8,128)(2,1)}, u32[]{:S(2)}, u32[]{:S(2)}) %all-to-all-start.1) | async-done | bytes 524320 | tf_op jit(solution)/shard_map/all_to_all | solution.py:161
  53.7 1.8 %fusion.153 = (bf16[64,1,16,128]{3,2,1,0:T(8,128)(2,1)}, bf16[64,1,16,128]{3,2,1,0:T(8,128)(2,1)S(1)}) fusion(bf16[64,2,16,128]{3,2,1,0:T(8,128)(2,1)} %all-to-all-done.1), kind=kLoop, calls=%fused_computation.192 | loop fusion | bytes 1048576 | tf_op jit(solution)/shard_map/slice | solution.py:162
  55.4 2.9 %fusion.29 = bf16[128,8,8,128]{3,2,1,0:T(8,128)(2,1)S(1)} fusion(s32[128,128]{1,0:T(8,128)S(1)} %get-tuple-element.35, bf16[128,8,128]{2,1,0:T(8,128)(2,1)S(1)} %copy-done.19, bf16[128,8,128]{2,1,0:T(8,128)(2,1)S(1)} %bitcast.265), kind=kOutput, calls=%fused_computation.32 | convolution fusion | flops 272629760 | bytes 2686976 | tf_op jit(solution)/shard_map/slaj,sbj->slab/dot_general | solution.py:67
  59.9 2.7 %bitcast_multiply_fusion.7 = f32[8,32,1024]{2,1,0:T(8,128)} fusion(f32[1,8,32,1024]{3,2,1,0:T(8,128)S(1)} %copy-done.8, f32[8,8,4,8,128]{4,3,2,1,0:T(8,128)S(1)} %fusion.47, f32[8,32,1024]{2,1,0:T(8,128)} %collective-permute-done.2, f32[]{:T(128)S(6)} %sub.85, f32[1,8,32,1024]{3,2,1,0:T(8,128)S(1)} %copy-done.5), kind=kLoop, calls=%fused_computation.91 | loop fusion | flops 1310720 | bytes 5242884 | tf_op jit(solution)/shard_map/mul | solution.py:189
  62.6 6.1 %collective-permute-start.3 = (f32[8,32,1024]{2,1,0:T(8,128)}, f32[8,32,1024]{2,1,0:T(8,128)}, u32[]{:S(2)}, u32[]{:S(2)}) collective-permute-start(f32[8,32,1024]{2,1,0:T(8,128)} %bitcast_multiply_fusion.7), channel_id=1, source_target_pairs={{64,0},{65,1},{66,2},{67,3},{68,4},{69,5},{70,6},{71,7},{72,8},{73... | collective-permute-start | bytes 3145736 | tf_op jit(solution)/shard_map/ppermute | solution.py:29
  71.9 4.4 %fusion.82 = f32[8,32,1024]{2,1,0:T(8,128)} fusion(f32[1,8,32,1024]{3,2,1,0:T(8,128)} %param.17, f32[1,8,32,1024]{3,2,1,0:T(8,128)} %param.16, f32[1,8,32,1024]{3,2,1,0:T(8,128)S(1)} %copy-done.4, f32[1,8,32,1024]{3,2,1,0:T(8,128)S(1)} %copy-done.5, f32[8,32,1024]{2,1,0:T(8,128)} %collective-permute-done.2, f32[]{:T(128)S(6)} %sub.92, ...), kind=kLoop, calls=%fused_computation.84 | loop fusion | flops 3145728 | bytes 8388616 | tf_op jit(solution)/shard_map/sub | solution.py:206
  76.4 1.4 collective-permute-start.4
  81.4 4.6 %broadcast_select_fusion = (f32[8,32,1024]{2,1,0:T(8,128)S(1)}, f32[8,32,1024]{2,1,0:T(8,128)S(1)}, f32[8,32,1024]{2,1,0:T(8,128)}) fusion(pred[]{:T(512)S(6)} %eq.87, f32[8,32,1024]{2,1,0:T(8,128)} %fusion.82, f32[8,32,1024]{2,1,0:T(8,128)} %collective-permute-done.4, f32[1,8,32,1024]{3,2,1,0:T(8,128)} %param.18, f32[1,8,32,1024]{3,2,1,0:T(8,128)S(1)} %copy-done.4, ...), kind=kLoop, calls=%fused_computation.114 | loop fusion | flops 2621440 | bytes 11534341 | tf_op jit(solution)/shard_map/jit(_where)/select_n | solution.py:178
  87.7 3.0 %multiply_reduce_fusion = bf16[128,8,128]{2,1,0:T(8,128)(2,1)S(1)} fusion(f32[128,8,128]{2,1,0:T(8,128)S(1)} %copy-done.18, s32[128,128]{1,0:T(8,128)S(1)} %get-tuple-element.35, bf16[128,8,8,128]{3,2,0,1:T(8,128)(2,1)S(1)} %bitcast.254), kind=kOutput, calls=%fused_computation.15 | convolution fusion | flops 272498688 | bytes 2949120 | tf_op jit(solution)/shard_map/slab,sbj->slaj/dot_general | solution.py:56
  91.4 2.8 %collective-permute-start.5 = (f32[8,2,1024]{2,1,0:T(2,128)}, f32[8,2,1024]{2,1,0:T(2,128)}, u32[]{:S(2)}, u32[]{:S(2)}) collective-permute-start(f32[8,2,1024]{2,1,0:T(2,128)} %get-tuple-element.26), channel_id=1, source_target_pairs={{0,1},{1,2},{2,3},{3,4},{4,5},{5,6},{6,7},{7,8},{8,9},{9,10},{10,1... | collective-permute-start | bytes 196616 | tf_op jit(solution)/shard_map/ppermute | solution.py:18
  96.5 8.8 %all-to-all-start.2 = ((bf16[64,2,16,128]{3,2,1,0:T(8,128)(2,1)}), bf16[64,2,16,128]{3,2,1,0:T(8,128)(2,1)}, u32[]{:S(2)}, u32[]{:S(2)}) async-start(bf16[64,2,16,128]{3,2,1,0:T(8,128)(2,1)} %copy.58), calls=%async_computation.2 | async-start | bytes 1048576 | tf_op jit(solution)/shard_map/all_to_all | solution.py:161
  105.3 1.7 %maximum_multiply_fusion = f32[8,36,1024]{2,1,0:T(8,128)S(1)} fusion(f32[8,2,1024]{2,1,0:T(2,128)} %collective-permute-done.6, f32[8,32,1024]{2,1,0:T(8,128)S(1)} %copy-done.12, f32[8,2,1024]{2,1,0:T(2,128)} %collective-permute-done.5, f32[2,8,36,1024]{3,2,1,0:T(8,128)} %copy-done.3), kind=kLoop, calls=%fused_computation.53 | loop fusion | flops 884736 | bytes 3538944 | tf_op jit(solution)/shard_map/mul | solution.py:35
  109.3 1.7 %fusion.73 = f32[8,32,1024]{2,1,0:T(8,128)} fusion(f32[8,34,1024]{2,1,0:T(8,128)S(1)} %multiply_multiply_fusion, f32[8,32,1023]{2,1,0:T(8,128)S(1)} %get-tuple-element.11, f32[8,32,1]{2,1,0:T(8,128)S(1)} %get-tuple-element.13, f32[8,32,1]{2,1,0:T(8,128)S(1)} %get-tuple-element.12, f32[8,32,1023]{2,1,0:T(8,128)S(1)} %get-tuple-element.10, ...), kind=kLoop, calls=%fused_computation.70 | loop fusion | flops 2621440 | bytes 7340064 | tf_op jit(solution)/shard_map/mul | solution.py:44
  111.0 2.7 %collective-permute-start.7 = (f32[8,32,1024]{2,1,0:T(8,128)}, f32[8,32,1024]{2,1,0:T(8,128)}, u32[]{:S(2)}, u32[]{:S(2)}) collective-permute-start(f32[8,32,1024]{2,1,0:T(8,128)} %fusion.73), channel_id=1, source_target_pairs={{0,64},{64,0},{1,65},{65,1},{2,66},{66,2},{3,67},{67,3},{4,68},{68... | collective-permute-start | bytes 3145736 | tf_op jit(solution)/shard_map/ppermute | solution.py:185
  113.7 2.4 %all-to-all-done.2 = bf16[64,2,16,128]{3,2,1,0:T(8,128)(2,1)} async-done(((bf16[64,2,16,128]{3,2,1,0:T(8,128)(2,1)}), bf16[64,2,16,128]{3,2,1,0:T(8,128)(2,1)}, u32[]{:S(2)}, u32[]{:S(2)}) %all-to-all-start.2) | async-done | bytes 524320 | tf_op jit(solution)/shard_map/all_to_all | solution.py:161
  117.1 3.8 %fusion.34 = bf16[128,8,8,128]{3,2,1,0:T(8,128)(2,1)S(1)} fusion(s32[128,128]{1,0:T(8,128)S(1)} %get-tuple-element.35, bf16[128,8,128]{2,1,0:T(8,128)(2,1)S(1)} %bitcast.264, bf16[128,8,128]{2,1,0:T(8,128)(2,1)} %get-tuple-element.33), kind=kOutput, calls=%fused_computation.33 | convolution fusion | flops 272629760 | bytes 2686976 | tf_op jit(solution)/shard_map/slaj,sbj->slab/dot_general | solution.py:67
  122.5 1.7 %bitcast_multiply_fusion.5 = f32[8,32,1024]{2,1,0:T(8,128)S(1)} fusion(f32[1,8,32,1024]{3,2,1,0:T(8,128)S(1)} %copy-done.9, f32[8,8,4,8,128]{4,3,2,1,0:T(8,128)S(1)} %fusion.50, f32[8,32,1024]{2,1,0:T(8,128)S(1)} %copy-done.10, f32[8,32,1024]{2,1,0:T(8,128)} %collective-permute-done.7, f32[]{:T(128)S(6)} %sub.85), kind=kLoop, calls=%fused_computation.89 | loop fusion | flops 1310720 | bytes 5242884 | tf_op jit(solution)/shard_map/mul | solution.py:189
  124.3 5.7 %collective-permute-start.8 = (f32[8,32,1024]{2,1,0:T(8,128)S(1)}, f32[8,32,1024]{2,1,0:T(8,128)S(1)}, u32[]{:S(2)}, u32[]{:S(2)}) collective-permute-start(f32[8,32,1024]{2,1,0:T(8,128)S(1)} %bitcast_multiply_fusion.5), channel_id=1, source_target_pairs={{64,0},{65,1},{66,2},{67,3},{68,4},{69,5},{70,6},{71,7},{72,8},{73... | collective-permute-start | bytes 3145736 | tf_op jit(solution)/shard_map/ppermute | solution.py:29
  130.0 2.2 %collective-permute-done.8 = f32[8,32,1024]{2,1,0:T(8,128)S(1)} collective-permute-done((f32[8,32,1024]{2,1,0:T(8,128)S(1)}, f32[8,32,1024]{2,1,0:T(8,128)S(1)}, u32[]{:S(2)}, u32[]{:S(2)}) %collective-permute-start.8) | collective-permute-done | bytes 1048608 | tf_op jit(solution)/shard_map/ppermute | solution.py:29
  132.2 3.3 %fusion.85 = (f32[8,32,1024]{2,1,0:T(8,128)}, f32[1,8,32,1024]{3,2,1,0:T(8,128)}) fusion(f32[8,32,1024]{2,1,0:T(8,128)S(1)} %copy-done.10, f32[1,8,32,1024]{3,2,1,0:T(8,128)S(1)} %copy-done.13, f32[1,8,32,1024]{3,2,1,0:T(8,128)S(1)} %copy-done.14, f32[8,32,1024]{2,1,0:T(8,128)S(1)} %get-tuple-element.4, f32[8,32,1024]{2,1,0:T(8,128)} %collective-permute-done.7, ...), kind=kLoop, calls=%fused_computation.87 | loop fusion | flops 3407872 | bytes 9437192 | tf_op jit(solution)/shard_map/sub | solution.py:206
  137.4 3.4 %fusion.9 = f32[16,1,128]{2,1,0:T(1,128)S(1)} fusion(bf16[16,1024,1]{1,2,0:T(2,128)(2,1)S(1)} %copy.72, bf16[1,16,128,1024]{3,2,1,0:T(8,128)(2,1)} %param.23), kind=kOutput, calls=%fused_computation.7 | convolution fusion | flops 4194304 | bytes 4235264 | tf_op jit(solution)/shard_map/toj,tj->to/dot_general | solution.py:170
  141.4 2.7 %fusion.90 = f32[1,8,32,1024]{3,2,1,0:T(8,128)} fusion(f32[8,32,1024]{2,1,0:T(8,128)S(1)} %get-tuple-element.4, f32[8,32,1024]{2,1,0:T(8,128)} %get-tuple-element.6, f32[8,32,1024]{2,1,0:T(8,128)S(1)} %collective-permute-done.9, f32[1,8,32,1024]{3,2,1,0:T(8,128)S(1)} %copy-done.9), kind=kLoop, calls=%fused_computation.96 | loop fusion | flops 786432 | bytes 5242880 | tf_op jit(solution)/shard_map/broadcast_in_dim | solution.py:211
  (130 shorter events, 32.4 us)
Async XLA Ops:
  0.6 8.6 %copy-start = (s32[1,16,128]{2,1,0:T(8,128)S(1)}, s32[1,16,128]{2,1,0:T(8,128)}, u32[]{:S(2)}) copy-start(s32[1,16,128]{2,1,0:T(8,128)} %param.22) | copy-start | bytes 24580
  2.1 6.8 %copy-start.32 = (s32[1,16]{1,0:T(1,128)S(1)}, s32[1,16]{1,0:T(1,128)}, u32[]{:S(2)}) copy-start(s32[1,16]{1,0:T(1,128)} %param.21) | copy-start | bytes 196
  2.1 19.9 %copy-start.20 = (bf16[1,16,128]{2,1,0:T(8,128)(2,1)S(1)}, bf16[1,16,128]{2,1,0:T(8,128)(2,1)}, u32[]{:S(2)}) copy-start(bf16[1,16,128]{2,1,0:T(8,128)(2,1)} %param.15) | copy-start | bytes 12292
  3.0 39.7 %collective-permute-start = (f32[2,8,2,1024]{3,2,1,0:T(2,128)}, f32[2,8,2,1024]{3,2,1,0:T(2,128)}, u32[]{:S(2)}, u32[]{:S(2)}) collective-permute-start(f32[2,8,2,1024]{3,2,1,0:T(2,128)} %get-tuple-element.8), channel_id=1, source_target_pairs={{0,1},{1,2},{2,3},{3,4},{4,5},{5,6},{6,7},{7,8},{8,9},{9,10},{10,1... | collective-permute-start | bytes 393224 | tf_op jit(solution)/shard_map/ppermute | solution.py:18
  7.6 35.1 %collective-permute-start.1 = (f32[2,8,2,1024]{3,2,1,0:T(2,128)}, f32[2,8,2,1024]{3,2,1,0:T(2,128)}, u32[]{:S(2)}, u32[]{:S(2)}) collective-permute-start(f32[2,8,2,1024]{3,2,1,0:T(2,128)} %get-tuple-element.9), channel_id=1, source_target_pairs={{1,0},{2,1},{3,2},{4,3},{5,4},{6,5},{7,6},{8,7},{9,8},{10,9},{11,1... | collective-permute-start | bytes 393224 | tf_op jit(solution)/shard_map/ppermute | solution.py:20
  10.5 20.0 %all-to-all-start = ((s32[64,2,128]{2,1,0:T(2,128)}), s32[64,2,128]{2,1,0:T(2,128)S(1)}, u32[]{:S(2)}, u32[]{:S(2)}) async-start(s32[64,2,128]{2,1,0:T(2,128)} %bitcast.9), calls=%async_computation | async-start | bytes 131072 | tf_op jit(solution)/shard_map/all_to_all | solution.py:122
  22.0 46.7 %copy-start.29 = (s32[16]{0:T(128)}, s32[16]{0:T(128)S(1)}, u32[]{:S(2)}) copy-start(s32[16]{0:T(128)S(1)} %multiply_add_fusion) | copy-start | bytes 196
  24.9 5.8 %copy-start.4 = (f32[1,8,32,1024]{3,2,1,0:T(8,128)S(1)}, f32[1,8,32,1024]{3,2,1,0:T(8,128)}, u32[]{:S(2)}) copy-start(f32[1,8,32,1024]{3,2,1,0:T(8,128)} %param.13) | copy-start | bytes 3145732
  30.7 27.7 %copy-start.24 = (s32[128]{0:T(128)}, s32[128]{0:T(128)S(1)}, u32[]{:S(2)}) copy-start(s32[128]{0:T(128)S(1)} %fusion.106) | copy-start | bytes 1540
  32.8 3.0 %copy-start.17 = (f32[128,8,128]{2,1,0:T(8,128)}, f32[128,8,128]{2,1,0:T(8,128)S(1)}, u32[]{:S(2)}) copy-start(f32[128,8,128]{2,1,0:T(8,128)S(1)} %get-tuple-element.32) | copy-start | bytes 1572868
  32.8 3.0 %copy-start.16 = (bf16[128,8,128]{2,1,0:T(8,128)(2,1)S(1)}, bf16[128,8,128]{2,1,0:T(8,128)(2,1)}, u32[]{:S(2)}) copy-start(bf16[128,8,128]{2,1,0:T(8,128)(2,1)} %copy.48) | copy-start | bytes 786436
  36.8 16.9 %all-to-all-start.1 = ((bf16[64,2,16,128]{3,2,1,0:T(8,128)(2,1)}), bf16[64,2,16,128]{3,2,1,0:T(8,128)(2,1)}, u32[]{:S(2)}, u32[]{:S(2)}) async-start(bf16[64,2,16,128]{3,2,1,0:T(8,128)(2,1)} %copy.49), calls=%async_computation.1 | async-start | bytes 1048576 | tf_op jit(solution)/shard_map/all_to_all | solution.py:161
  47.8 7.6 %copy-start.19 = (bf16[128,8,128]{2,1,0:T(8,128)(2,1)S(1)}, bf16[128,8,128]{2,1,0:T(8,128)(2,1)}, u32[]{:S(2)}) copy-start(bf16[128,8,128]{2,1,0:T(8,128)(2,1)} %get-tuple-element.33) | copy-start | bytes 786436
  49.5 10.2 %collective-permute-start.2 = (f32[8,32,1024]{2,1,0:T(8,128)}, f32[8,32,1024]{2,1,0:T(8,128)}, u32[]{:S(2)}, u32[]{:S(2)}) collective-permute-start(f32[8,32,1024]{2,1,0:T(8,128)} %fusion.79), channel_id=1, source_target_pairs={{0,64},{64,0},{1,65},{65,1},{2,66},{66,2},{3,67},{67,3},{4,68},{68... | collective-permute-start | bytes 3145736 | tf_op jit(solution)/shard_map/ppermute | solution.py:185
  59.7 2.9 %copy-start.7 = (f32[8,8,4,8,128]{4,3,2,1,0:T(8,128)}, f32[8,8,4,8,128]{4,3,2,1,0:T(8,128)S(1)}, u32[]{:S(2)}) copy-start(f32[8,8,4,8,128]{4,3,2,1,0:T(8,128)S(1)} %fusion.47) | copy-start | bytes 3145732
  62.6 9.3 %collective-permute-start.3 = (f32[8,32,1024]{2,1,0:T(8,128)}, f32[8,32,1024]{2,1,0:T(8,128)}, u32[]{:S(2)}, u32[]{:S(2)}) collective-permute-start(f32[8,32,1024]{2,1,0:T(8,128)} %bitcast_multiply_fusion.7), channel_id=1, source_target_pairs={{64,0},{65,1},{66,2},{67,3},{68,4},{69,5},{70,6},{71,7},{72,8},{73... | collective-permute-start | bytes 3145736 | tf_op jit(solution)/shard_map/ppermute | solution.py:29
  71.9 5.9 %copy-start.2 = (bf16[1,16,128,1024]{3,2,1,0:T(8,128)(2,1)S(1)}, bf16[1,16,128,1024]{3,2,1,0:T(8,128)(2,1)}, u32[]{:S(2)}) copy-start(bf16[1,16,128,1024]{3,2,1,0:T(8,128)(2,1)} %param.23) | copy-start | bytes 12582916
  76.4 5.0 %collective-permute-start.4 = (f32[8,32,1024]{2,1,0:T(8,128)}, f32[8,32,1024]{2,1,0:T(8,128)}, u32[]{:S(2)}, u32[]{:S(2)}) collective-permute-start(f32[8,32,1024]{2,1,0:T(8,128)} %fusion.82), channel_id=1, source_target_pairs={{0,64},{1,65},{2,66},{3,67},{4,68},{5,69},{6,70},{7,71},{8,72},{9,... | collective-permute-start | bytes 3145736 | tf_op jit(solution)/shard_map/ppermute | solution.py:29
  80.4 5.5 %copy-start.25 = (s32[128]{0:T(128)S(1)}, s32[128]{0:T(128)}, u32[]{:S(2)}) copy-start(s32[128]{0:T(128)} %copy-done.24) | copy-start | bytes 1540
  85.9 4.8 %copy-start.11 = (f32[8,32,1024]{2,1,0:T(8,128)}, f32[8,32,1024]{2,1,0:T(8,128)S(1)}, u32[]{:S(2)}) copy-start(f32[8,32,1024]{2,1,0:T(8,128)S(1)} %get-tuple-element.3) | copy-start | bytes 3145732
  91.4 13.8 %collective-permute-start.5 = (f32[8,2,1024]{2,1,0:T(2,128)}, f32[8,2,1024]{2,1,0:T(2,128)}, u32[]{:S(2)}, u32[]{:S(2)}) collective-permute-start(f32[8,2,1024]{2,1,0:T(2,128)} %get-tuple-element.26), channel_id=1, source_target_pairs={{0,1},{1,2},{2,3},{3,4},{4,5},{5,6},{6,7},{7,8},{8,9},{9,10},{10,1... | collective-permute-start | bytes 196616 | tf_op jit(solution)/shard_map/ppermute | solution.py:18
  94.3 11.0 %collective-permute-start.6 = (f32[8,2,1024]{2,1,0:T(2,128)S(1)}, f32[8,2,1024]{2,1,0:T(2,128)}, u32[]{:S(2)}, u32[]{:S(2)}) collective-permute-start(f32[8,2,1024]{2,1,0:T(2,128)S(1)} %get-tuple-element.27), channel_id=1, source_target_pairs={{1,0},{2,1},{3,2},{4,3},{5,4},{6,5},{7,6},{8,7},{9,8},{10,9},{11,1... | collective-permute-start | bytes 196616 | tf_op jit(solution)/shard_map/ppermute | solution.py:20
  95.6 9.7 %copy-start.12 = (f32[8,32,1024]{2,1,0:T(8,128)S(1)}, f32[8,32,1024]{2,1,0:T(8,128)}, u32[]{:S(2)}) copy-start(f32[8,32,1024]{2,1,0:T(8,128)} %copy-done.11) | copy-start | bytes 3145732
  96.5 19.6 %all-to-all-start.2 = ((bf16[64,2,16,128]{3,2,1,0:T(8,128)(2,1)}), bf16[64,2,16,128]{3,2,1,0:T(8,128)(2,1)}, u32[]{:S(2)}, u32[]{:S(2)}) async-start(bf16[64,2,16,128]{3,2,1,0:T(8,128)(2,1)} %copy.58), calls=%async_computation.2 | async-start | bytes 1048576 | tf_op jit(solution)/shard_map/all_to_all | solution.py:161
  111.0 11.3 %collective-permute-start.7 = (f32[8,32,1024]{2,1,0:T(8,128)}, f32[8,32,1024]{2,1,0:T(8,128)}, u32[]{:S(2)}, u32[]{:S(2)}) collective-permute-start(f32[8,32,1024]{2,1,0:T(8,128)} %fusion.73), channel_id=1, source_target_pairs={{0,64},{64,0},{1,65},{65,1},{2,66},{66,2},{3,67},{67,3},{4,68},{68... | collective-permute-start | bytes 3145736 | tf_op jit(solution)/shard_map/ppermute | solution.py:185
  117.1 3.8 %copy-start.26 = (s32[128]{0:T(128)S(1)}, s32[128]{0:T(128)}, u32[]{:S(2)}) copy-start(s32[128]{0:T(128)} %copy-done.24) | copy-start | bytes 1540
  122.5 9.6 %copy-start.13 = (f32[1,8,32,1024]{3,2,1,0:T(8,128)S(1)}, f32[1,8,32,1024]{3,2,1,0:T(8,128)}, u32[]{:S(2)}) copy-start(f32[1,8,32,1024]{3,2,1,0:T(8,128)} %param.17) | copy-start | bytes 3145732
  122.5 9.6 %copy-start.14 = (f32[1,8,32,1024]{3,2,1,0:T(8,128)S(1)}, f32[1,8,32,1024]{3,2,1,0:T(8,128)}, u32[]{:S(2)}) copy-start(f32[1,8,32,1024]{3,2,1,0:T(8,128)} %param.16) | copy-start | bytes 3145732
  124.3 12.5 %copy-start.31 = (s32[16]{0:T(128)S(1)}, s32[16]{0:T(128)}, u32[]{:S(2)}) copy-start(s32[16]{0:T(128)} %copy-done.29) | copy-start | bytes 196
  124.3 7.9 %collective-permute-start.8 = (f32[8,32,1024]{2,1,0:T(8,128)S(1)}, f32[8,32,1024]{2,1,0:T(8,128)S(1)}, u32[]{:S(2)}, u32[]{:S(2)}) collective-permute-start(f32[8,32,1024]{2,1,0:T(8,128)S(1)} %bitcast_multiply_fusion.5), channel_id=1, source_target_pairs={{64,0},{65,1},{66,2},{67,3},{68,4},{69,5},{70,6},{71,7},{72,8},{73... | collective-permute-start | bytes 3145736 | tf_op jit(solution)/shard_map/ppermute | solution.py:29
  135.5 5.9 %collective-permute-start.9 = (f32[8,32,1024]{2,1,0:T(8,128)}, f32[8,32,1024]{2,1,0:T(8,128)S(1)}, u32[]{:S(2)}, u32[]{:S(2)}) collective-permute-start(f32[8,32,1024]{2,1,0:T(8,128)} %get-tuple-element.6), channel_id=1, source_target_pairs={{0,64},{1,65},{2,66},{3,67},{4,68},{5,69},{6,70},{7,71},{8,72},{9,... | collective-permute-start | bytes 3145736 | tf_op jit(solution)/shard_map/ppermute | solution.py:29
  137.4 3.4 %copy-start.23 = (bf16[1,16,128]{2,1,0:T(8,128)(2,1)S(1)}, bf16[1,16,128]{2,1,0:T(8,128)(2,1)}, u32[]{:S(2)}) copy-start(bf16[1,16,128]{2,1,0:T(8,128)(2,1)} %param.24) | copy-start | bytes 12292
  (14 other events, 21.6 us)
where the time goes:
time: 145 us; the launch traced here: 144 us
  starting transfers between devices  55.6 us (38%)
  other arithmetic  32.3 us (22%)
  matrix products  27 us (19%)
  local copies, waits for them, and re-layouts  16.3 us (11%)
  waiting for transfers between devices  11.5 us (8%)
    all_to_all x2, starting transfers between devices, on_device(): got = lax.all_to_all(both, 'space', split_axis=0, concat_axis=0, tiled=True)  14.7 us
    ppermute x4, starting transfers between devices, shifted(): return lax.ppermute(value, axis, pairs)  14.4 us
    all_to_all x1, starting transfers between devices, on_device(): lax.all_to_all(packed_cells.reshape(owners_count, capacity, touched), 'sp...  11.5 us
    sub x2, other arithmetic, on_device(): source = r_model - err_field * upward  7.76 us
    ppermute x2, starting transfers between devices, with_halo(): lax.ppermute(tail, axis, [(i, i + 1) for i in range(ends)])  7.42 us
    dot_general x2, matrix products, spread_cols(): jnp.einsum('slaj,sbj->slab', placed, col_oh, preferred_element_type=jnp.f...  6.71 us
    dot_general x2, matrix products, gather_cols(): jnp.einsum('slab,sbj->slaj', lines, col_oh, preferred_element_type=jnp.fl...  6.02 us
    select_n x2, other arithmetic, on_device(): chosen = jnp.where(tm_here == 0, increment, dual_model)  6.02 us
  transfers between devices with their start and end apart: 13, of which 5 were waited for; matrix products, arithmetic and copies ran while one was open for 32% of the time, Pallas kernels for 0%

commit v1 on v0

--- a/solution.py
+++ b/solution.py
@@ -68,7 +68,7 @@
     total = jnp.einsum(
         "sr,slab->lrab", row_oh, lines.astype(jnp.bfloat16), preferred_element_type=jnp.float32
     )
-    return total.reshape(levels, row_count, groups * lanes)
+    return lax.optimization_barrier(total.reshape(levels, row_count, groups * lanes))
 
 
 def on_device(

time: 145 us -> 148 us (1.021)
  local copies, waits for them, and re-layouts: 16.3 us -> 19.4 us
    unnamed x68, local copies, waits for them, and re-layouts: 3.32 us -> 6.13 us
where the time goes in v1:
time: 148 us; the launch traced here: 147 us
  starting transfers between devices  55.6 us (38%)
  other arithmetic  32.5 us (22%)
  matrix products  27 us (18%)
  local copies, waits for them, and re-layouts  19.4 us (13%)
  waiting for transfers between devices  11.5 us (8%)
    all_to_all x2, starting transfers between devices, on_device(): got = lax.all_to_all(both, 'space', split_axis=0, concat_axis=0, tiled=True)  14.5 us
    ppermute x4, starting transfers between devices, shifted(): return lax.ppermute(value, axis, pairs)  14.4 us
    all_to_all x1, starting transfers between devices, on_device(): lax.all_to_all(packed_cells.reshape(owners_count, capacity, touched), 'sp...  11.5 us
    sub x2, other arithmetic, on_device(): source = r_model - err_field * upward  7.93 us
    ppermute x2, starting transfers between devices, with_halo(): lax.ppermute(tail, axis, [(i, i + 1) for i in range(ends)])  7.64 us
    dot_general x2, matrix products, spread_cols(): jnp.einsum('slaj,sbj->slab', placed, col_oh, preferred_element_type=jnp.f...  6.71 us
    unnamed x68, local copies, waits for them, and re-layouts  6.13 us
    select_n x2, other arithmetic, on_device(): chosen = jnp.where(tm_here == 0, increment, dual_model)  6.11 us
  transfers between devices with their start and end apart: 13, of which 5 were waited for; matrix products, arithmetic and copies ran while one was open for 32% of the time, Pallas kernels for 0%

profile of v1, /device:TPU:1, one launch (start us, length us, event | category | flops | bytes accessed | tf_op | source)
XLA Modules:
  0.0 147.3 jit_solution(2475448315279114461)
XLA Ops:
  0.7 1.5 broadcast_select_fusion.1
  3.0 4.6 %collective-permute-start = (f32[2,8,2,1024]{3,2,1,0:T(2,128)}, f32[2,8,2,1024]{3,2,1,0:T(2,128)}, u32[]{:S(2)}, u32[]{:S(2)}) collective-permute-start(f32[2,8,2,1024]{3,2,1,0:T(2,128)} %get-tuple-element.8), channel_id=1, source_target_pairs={{0,1},{1,2},{2,3},{3,4},{4,5},{5,6},{6,7},{7,8},{8,9},{9,10},{10,1... | collective-permute-start | bytes 393224 | tf_op jit(solution)/shard_map/ppermute | solution.py:18
  10.5 11.5 %all-to-all-start = ((s32[64,2,128]{2,1,0:T(2,128)}), s32[64,2,128]{2,1,0:T(2,128)S(1)}, u32[]{:S(2)}, u32[]{:S(2)}) async-start(s32[64,2,128]{2,1,0:T(2,128)} %bitcast.9), calls=%async_computation | async-start | bytes 131072 | tf_op jit(solution)/shard_map/all_to_all | solution.py:122
  22.0 2.8 %fusion.15 = bf16[16,1,1024]{2,1,0:T(2,128)(2,1)S(1)} fusion(bf16[1,16,128,1024]{3,2,1,0:T(8,128)(2,1)} %param.23, bf16[16,128,1]{1,0,2:T(8,128)(2,1)S(1)} %bitcast.263), kind=kOutput, calls=%fused_computation.13 | convolution fusion | flops 4194304 | bytes 4231168 | tf_op jit(solution)/shard_map/toj,to->tj/dot_general | solution.py:145
  26.3 4.1 %all-to-all-done = s32[64,2,128]{2,1,0:T(2,128)S(1)} async-done(((s32[64,2,128]{2,1,0:T(2,128)}), s32[64,2,128]{2,1,0:T(2,128)S(1)}, u32[]{:S(2)}, u32[]{:S(2)}) %all-to-all-start) | async-done | bytes 65568 | tf_op jit(solution)/shard_map/all_to_all | solution.py:122
  32.8 3.0 %multiply_reduce_fusion.1 = bf16[128,8,128]{2,1,0:T(8,128)(2,1)S(1)} fusion(f32[128,8,128]{2,1,0:T(8,128)S(1)} %get-tuple-element.32, s32[128,128]{1,0:T(8,128)S(1)} %get-tuple-element.35, bf16[128,8,8,128]{3,2,0,1:T(8,128)(2,1)S(1)} %bitcast.247), kind=kOutput, calls=%fused_computation.16 | convolution fusion | flops 272498688 | bytes 2949120 | tf_op jit(solution)/shard_map/slab,sbj->slaj/dot_general | solution.py:56
  36.8 5.9 %all-to-all-start.1 = ((bf16[64,2,16,128]{3,2,1,0:T(8,128)(2,1)}), bf16[64,2,16,128]{3,2,1,0:T(8,128)(2,1)}, u32[]{:S(2)}, u32[]{:S(2)}) async-start(bf16[64,2,16,128]{3,2,1,0:T(8,128)(2,1)} %copy.49), calls=%async_computation.1 | async-start | bytes 1048576 | tf_op jit(solution)/shard_map/all_to_all | solution.py:161
  47.9 1.7 %fusion.79 = f32[8,32,1024]{2,1,0:T(8,128)} fusion(f32[8,34,1024]{2,1,0:T(8,128)S(1)} %multiply_multiply_fusion.1, f32[8,32,1023]{2,1,0:T(8,128)S(1)} %get-tuple-element.19, f32[8,32,1]{2,1,0:T(8,128)S(1)} %get-tuple-element.21, f32[8,32,1]{2,1,0:T(8,128)S(1)} %get-tuple-element.20, f32[8,32,1023]{2,1,0:T(8,128)S(1)} %get-tuple-element.18, ...), kind=kLoop, calls=%fused_computation.77 | loop fusion | flops 2621440 | bytes 7340064 | tf_op jit(solution)/shard_map/mul | solution.py:44
  49.5 2.2 %collective-permute-start.2 = (f32[8,32,1024]{2,1,0:T(8,128)}, f32[8,32,1024]{2,1,0:T(8,128)}, u32[]{:S(2)}, u32[]{:S(2)}) collective-permute-start(f32[8,32,1024]{2,1,0:T(8,128)} %fusion.79), channel_id=1, source_target_pairs={{0,64},{64,0},{1,65},{65,1},{2,66},{66,2},{3,67},{67,3},{4,68},{68... | collective-permute-start | bytes 3145736 | tf_op jit(solution)/shard_map/ppermute | solution.py:185
  51.8 1.9 %all-to-all-done.1 = bf16[64,2,16,128]{3,2,1,0:T(8,128)(2,1)} async-done(((bf16[64,2,16,128]{3,2,1,0:T(8,128)(2,1)}), bf16[64,2,16,128]{3,2,1,0:T(8,128)(2,1)}, u32[]{:S(2)}, u32[]{:S(2)}) %all-to-all-start.1) | async-done | bytes 524320 | tf_op jit(solution)/shard_map/all_to_all | solution.py:161
  53.7 1.8 %fusion.154 = (bf16[64,1,16,128]{3,2,1,0:T(8,128)(2,1)}, bf16[64,1,16,128]{3,2,1,0:T(8,128)(2,1)S(1)}) fusion(bf16[64,2,16,128]{3,2,1,0:T(8,128)(2,1)} %all-to-all-done.1), kind=kLoop, calls=%fused_computation.194 | loop fusion | bytes 1048576 | tf_op jit(solution)/shard_map/slice | solution.py:162
  55.4 2.9 %fusion.29 = bf16[128,8,8,128]{3,2,1,0:T(8,128)(2,1)S(1)} fusion(s32[128,128]{1,0:T(8,128)S(1)} %get-tuple-element.35, bf16[128,8,128]{2,1,0:T(8,128)(2,1)S(1)} %copy-done.19, bf16[128,8,128]{2,1,0:T(8,128)(2,1)S(1)} %bitcast.259), kind=kOutput, calls=%fused_computation.32 | convolution fusion | flops 272629760 | bytes 2686976 | tf_op jit(solution)/shard_map/slaj,sbj->slab/dot_general | solution.py:67
  59.8 1.4 copy-done.5
  61.6 2.5 %bitcast_multiply_fusion.7 = f32[8,32,1024]{2,1,0:T(8,128)} fusion(f32[1,8,32,1024]{3,2,1,0:T(8,128)S(1)} %copy-done.8, f32[8,32,1024]{2,1,0:T(8,128)S(1)} %bitcast.238, f32[8,32,1024]{2,1,0:T(8,128)} %collective-permute-done.2, f32[]{:T(128)S(6)} %sub.85, f32[1,8,32,1024]{3,2,1,0:T(8,128)S(1)} %copy-done.5), kind=kLoop, calls=%fused_computation.91 | loop fusion | flops 1310720 | bytes 5242884 | tf_op jit(solution)/shard_map/mul | solution.py:189
  64.1 6.1 %collective-permute-start.3 = (f32[8,32,1024]{2,1,0:T(8,128)}, f32[8,32,1024]{2,1,0:T(8,128)}, u32[]{:S(2)}, u32[]{:S(2)}) collective-permute-start(f32[8,32,1024]{2,1,0:T(8,128)} %bitcast_multiply_fusion.7), channel_id=1, source_target_pairs={{64,0},{65,1},{66,2},{67,3},{68,4},{69,5},{70,6},{71,7},{72,8},{73... | collective-permute-start | bytes 3145736 | tf_op jit(solution)/shard_map/ppermute | solution.py:29
  73.5 4.5 %fusion.82 = f32[8,32,1024]{2,1,0:T(8,128)} fusion(f32[1,8,32,1024]{3,2,1,0:T(8,128)} %param.17, f32[1,8,32,1024]{3,2,1,0:T(8,128)} %param.16, f32[1,8,32,1024]{3,2,1,0:T(8,128)S(1)} %copy-done.4, f32[1,8,32,1024]{3,2,1,0:T(8,128)S(1)} %copy-done.5, f32[8,32,1024]{2,1,0:T(8,128)} %collective-permute-done.2, f32[]{:T(128)S(6)} %sub.92, ...), kind=kLoop, calls=%fused_computation.84 | loop fusion | flops 3145728 | bytes 8388616 | tf_op jit(solution)/shard_map/sub | solution.py:206
  78.0 1.4 collective-permute-start.4
  83.0 4.6 %broadcast_select_fusion = (f32[8,32,1024]{2,1,0:T(8,128)S(1)}, f32[8,32,1024]{2,1,0:T(8,128)S(1)}, f32[8,32,1024]{2,1,0:T(8,128)}) fusion(pred[]{:T(512)S(6)} %eq.87, f32[8,32,1024]{2,1,0:T(8,128)} %fusion.82, f32[8,32,1024]{2,1,0:T(8,128)} %collective-permute-done.4, f32[1,8,32,1024]{3,2,1,0:T(8,128)} %param.18, f32[1,8,32,1024]{3,2,1,0:T(8,128)S(1)} %copy-done.4, ...), kind=kLoop, calls=%fused_computation.116 | loop fusion | flops 2621440 | bytes 11534341 | tf_op jit(solution)/shard_map/jit(_where)/select_n | solution.py:178
  89.4 3.0 %multiply_reduce_fusion = bf16[128,8,128]{2,1,0:T(8,128)(2,1)S(1)} fusion(f32[128,8,128]{2,1,0:T(8,128)S(1)} %copy-done.18, s32[128,128]{1,0:T(8,128)S(1)} %get-tuple-element.35, bf16[128,8,8,128]{3,2,0,1:T(8,128)(2,1)S(1)} %bitcast.248), kind=kOutput, calls=%fused_computation.15 | convolution fusion | flops 272498688 | bytes 2949120 | tf_op jit(solution)/shard_map/slab,sbj->slaj/dot_general | solution.py:56
  93.1 3.0 %collective-permute-start.5 = (f32[8,2,1024]{2,1,0:T(2,128)}, f32[8,2,1024]{2,1,0:T(2,128)}, u32[]{:S(2)}, u32[]{:S(2)}) collective-permute-start(f32[8,2,1024]{2,1,0:T(2,128)} %get-tuple-element.26), channel_id=1, source_target_pairs={{0,1},{1,2},{2,3},{3,4},{4,5},{5,6},{6,7},{7,8},{8,9},{9,10},{10,1... | collective-permute-start | bytes 196616 | tf_op jit(solution)/shard_map/ppermute | solution.py:18
  98.4 8.6 %all-to-all-start.2 = ((bf16[64,2,16,128]{3,2,1,0:T(8,128)(2,1)}), bf16[64,2,16,128]{3,2,1,0:T(8,128)(2,1)}, u32[]{:S(2)}, u32[]{:S(2)}) async-start(bf16[64,2,16,128]{3,2,1,0:T(8,128)(2,1)} %copy.58), calls=%async_computation.2 | async-start | bytes 1048576 | tf_op jit(solution)/shard_map/all_to_all | solution.py:161
  107.0 1.7 %maximum_multiply_fusion = f32[8,36,1024]{2,1,0:T(8,128)S(1)} fusion(f32[8,2,1024]{2,1,0:T(2,128)} %collective-permute-done.6, f32[8,32,1024]{2,1,0:T(8,128)S(1)} %copy-done.12, f32[8,2,1024]{2,1,0:T(2,128)} %collective-permute-done.5, f32[2,8,36,1024]{3,2,1,0:T(8,128)} %copy-done.3), kind=kLoop, calls=%fused_computation.53 | loop fusion | flops 884736 | bytes 3538944 | tf_op jit(solution)/shard_map/mul | solution.py:35
  111.0 1.7 %fusion.73 = f32[8,32,1024]{2,1,0:T(8,128)} fusion(f32[8,34,1024]{2,1,0:T(8,128)S(1)} %multiply_multiply_fusion, f32[8,32,1023]{2,1,0:T(8,128)S(1)} %get-tuple-element.11, f32[8,32,1]{2,1,0:T(8,128)S(1)} %get-tuple-element.13, f32[8,32,1]{2,1,0:T(8,128)S(1)} %get-tuple-element.12, f32[8,32,1023]{2,1,0:T(8,128)S(1)} %get-tuple-element.10, ...), kind=kLoop, calls=%fused_computation.70 | loop fusion | flops 2621440 | bytes 7340064 | tf_op jit(solution)/shard_map/mul | solution.py:44
  112.7 2.7 %collective-permute-start.7 = (f32[8,32,1024]{2,1,0:T(8,128)}, f32[8,32,1024]{2,1,0:T(8,128)}, u32[]{:S(2)}, u32[]{:S(2)}) collective-permute-start(f32[8,32,1024]{2,1,0:T(8,128)} %fusion.73), channel_id=1, source_target_pairs={{0,64},{64,0},{1,65},{65,1},{2,66},{66,2},{3,67},{67,3},{4,68},{68... | collective-permute-start | bytes 3145736 | tf_op jit(solution)/shard_map/ppermute | solution.py:185
  115.4 2.4 %all-to-all-done.2 = bf16[64,2,16,128]{3,2,1,0:T(8,128)(2,1)} async-done(((bf16[64,2,16,128]{3,2,1,0:T(8,128)(2,1)}), bf16[64,2,16,128]{3,2,1,0:T(8,128)(2,1)}, u32[]{:S(2)}, u32[]{:S(2)}) %all-to-all-start.2) | async-done | bytes 524320 | tf_op jit(solution)/shard_map/all_to_all | solution.py:161
  118.8 3.8 %fusion.34 = bf16[128,8,8,128]{3,2,1,0:T(8,128)(2,1)S(1)} fusion(s32[128,128]{1,0:T(8,128)S(1)} %get-tuple-element.35, bf16[128,8,128]{2,1,0:T(8,128)(2,1)S(1)} %bitcast.258, bf16[128,8,128]{2,1,0:T(8,128)(2,1)} %get-tuple-element.33), kind=kOutput, calls=%fused_computation.33 | convolution fusion | flops 272629760 | bytes 2686976 | tf_op jit(solution)/shard_map/slaj,sbj->slab/dot_general | solution.py:67
  125.5 1.8 %bitcast_multiply_fusion.5 = f32[8,32,1024]{2,1,0:T(8,128)S(1)} fusion(f32[1,8,32,1024]{3,2,1,0:T(8,128)S(1)} %copy-done.9, f32[8,32,1024]{2,1,0:T(8,128)S(1)} %bitcast.241, f32[8,32,1024]{2,1,0:T(8,128)S(1)} %copy-done.10, f32[8,32,1024]{2,1,0:T(8,128)} %collective-permute-done.7, f32[]{:T(128)S(6)} %sub.85), kind=kLoop, calls=%fused_computation.89 | loop fusion | flops 1310720 | bytes 5242884 | tf_op jit(solution)/shard_map/mul | solution.py:189
  127.4 5.7 %collective-permute-start.8 = (f32[8,32,1024]{2,1,0:T(8,128)S(1)}, f32[8,32,1024]{2,1,0:T(8,128)S(1)}, u32[]{:S(2)}, u32[]{:S(2)}) collective-permute-start(f32[8,32,1024]{2,1,0:T(8,128)S(1)} %bitcast_multiply_fusion.5), channel_id=1, source_target_pairs={{64,0},{65,1},{66,2},{67,3},{68,4},{69,5},{70,6},{71,7},{72,8},{73... | collective-permute-start | bytes 3145736 | tf_op jit(solution)/shard_map/ppermute | solution.py:29
  133.0 2.2 %collective-permute-done.8 = f32[8,32,1024]{2,1,0:T(8,128)S(1)} collective-permute-done((f32[8,32,1024]{2,1,0:T(8,128)S(1)}, f32[8,32,1024]{2,1,0:T(8,128)S(1)}, u32[]{:S(2)}, u32[]{:S(2)}) %collective-permute-start.8) | collective-permute-done | bytes 1048608 | tf_op jit(solution)/shard_map/ppermute | solution.py:29
  135.2 3.4 %fusion.85 = (f32[8,32,1024]{2,1,0:T(8,128)}, f32[1,8,32,1024]{3,2,1,0:T(8,128)}) fusion(f32[8,32,1024]{2,1,0:T(8,128)S(1)} %copy-done.10, f32[1,8,32,1024]{3,2,1,0:T(8,128)S(1)} %copy-done.13, f32[1,8,32,1024]{3,2,1,0:T(8,128)S(1)} %copy-done.14, f32[8,32,1024]{2,1,0:T(8,128)S(1)} %get-tuple-element.4, f32[8,32,1024]{2,1,0:T(8,128)} %collective-permute-done.7, ...), kind=kLoop, calls=%fused_computation.87 | loop fusion | flops 3407872 | bytes 9437192 | tf_op jit(solution)/shard_map/sub | solution.py:206
  140.6 3.4 %fusion.9 = f32[16,1,128]{2,1,0:T(1,128)S(1)} fusion(bf16[16,1024,1]{1,2,0:T(2,128)(2,1)S(1)} %copy.72, bf16[1,16,128,1024]{3,2,1,0:T(8,128)(2,1)} %param.23), kind=kOutput, calls=%fused_computation.7 | convolution fusion | flops 4194304 | bytes 4235264 | tf_op jit(solution)/shard_map/toj,tj->to/dot_general | solution.py:170
  144.6 2.7 %fusion.90 = f32[1,8,32,1024]{3,2,1,0:T(8,128)} fusion(f32[8,32,1024]{2,1,0:T(8,128)S(1)} %get-tuple-element.4, f32[8,32,1024]{2,1,0:T(8,128)} %get-tuple-element.6, f32[8,32,1024]{2,1,0:T(8,128)S(1)} %collective-permute-done.9, f32[1,8,32,1024]{3,2,1,0:T(8,128)S(1)} %copy-done.9), kind=kLoop, calls=%fused_computation.96 | loop fusion | flops 786432 | bytes 5242880 | tf_op jit(solution)/shard_map/broadcast_in_dim | solution.py:211
  (132 shorter events, 35.3 us)
Async XLA Ops:
  0.6 8.6 %copy-start = (s32[1,16,128]{2,1,0:T(8,128)S(1)}, s32[1,16,128]{2,1,0:T(8,128)}, u32[]{:S(2)}) copy-start(s32[1,16,128]{2,1,0:T(8,128)} %param.22) | copy-start | bytes 24580
  2.1 6.8 %copy-start.32 = (s32[1,16]{1,0:T(1,128)S(1)}, s32[1,16]{1,0:T(1,128)}, u32[]{:S(2)}) copy-start(s32[1,16]{1,0:T(1,128)} %param.21) | copy-start | bytes 196
  2.1 19.9 %copy-start.20 = (bf16[1,16,128]{2,1,0:T(8,128)(2,1)S(1)}, bf16[1,16,128]{2,1,0:T(8,128)(2,1)}, u32[]{:S(2)}) copy-start(bf16[1,16,128]{2,1,0:T(8,128)(2,1)} %param.15) | copy-start | bytes 12292
  3.0 39.7 %collective-permute-start = (f32[2,8,2,1024]{3,2,1,0:T(2,128)}, f32[2,8,2,1024]{3,2,1,0:T(2,128)}, u32[]{:S(2)}, u32[]{:S(2)}) collective-permute-start(f32[2,8,2,1024]{3,2,1,0:T(2,128)} %get-tuple-element.8), channel_id=1, source_target_pairs={{0,1},{1,2},{2,3},{3,4},{4,5},{5,6},{6,7},{7,8},{8,9},{9,10},{10,1... | collective-permute-start | bytes 393224 | tf_op jit(solution)/shard_map/ppermute | solution.py:18
  7.6 35.1 %collective-permute-start.1 = (f32[2,8,2,1024]{3,2,1,0:T(2,128)}, f32[2,8,2,1024]{3,2,1,0:T(2,128)}, u32[]{:S(2)}, u32[]{:S(2)}) collective-permute-start(f32[2,8,2,1024]{3,2,1,0:T(2,128)} %get-tuple-element.9), channel_id=1, source_target_pairs={{1,0},{2,1},{3,2},{4,3},{5,4},{6,5},{7,6},{8,7},{9,8},{10,9},{11,1... | collective-permute-start | bytes 393224 | tf_op jit(solution)/shard_map/ppermute | solution.py:20
  10.5 20.0 %all-to-all-start = ((s32[64,2,128]{2,1,0:T(2,128)}), s32[64,2,128]{2,1,0:T(2,128)S(1)}, u32[]{:S(2)}, u32[]{:S(2)}) async-start(s32[64,2,128]{2,1,0:T(2,128)} %bitcast.9), calls=%async_computation | async-start | bytes 131072 | tf_op jit(solution)/shard_map/all_to_all | solution.py:122
  22.0 48.2 %copy-start.29 = (s32[16]{0:T(128)}, s32[16]{0:T(128)S(1)}, u32[]{:S(2)}) copy-start(s32[16]{0:T(128)S(1)} %multiply_add_fusion) | copy-start | bytes 196
  24.9 5.8 %copy-start.4 = (f32[1,8,32,1024]{3,2,1,0:T(8,128)S(1)}, f32[1,8,32,1024]{3,2,1,0:T(8,128)}, u32[]{:S(2)}) copy-start(f32[1,8,32,1024]{3,2,1,0:T(8,128)} %param.13) | copy-start | bytes 3145732
  30.7 27.7 %copy-start.24 = (s32[128]{0:T(128)}, s32[128]{0:T(128)S(1)}, u32[]{:S(2)}) copy-start(s32[128]{0:T(128)S(1)} %fusion.107) | copy-start | bytes 1540
  32.8 3.0 %copy-start.17 = (f32[128,8,128]{2,1,0:T(8,128)}, f32[128,8,128]{2,1,0:T(8,128)S(1)}, u32[]{:S(2)}) copy-start(f32[128,8,128]{2,1,0:T(8,128)S(1)} %get-tuple-element.32) | copy-start | bytes 1572868
  32.8 3.0 %copy-start.16 = (bf16[128,8,128]{2,1,0:T(8,128)(2,1)S(1)}, bf16[128,8,128]{2,1,0:T(8,128)(2,1)}, u32[]{:S(2)}) copy-start(bf16[128,8,128]{2,1,0:T(8,128)(2,1)} %copy.48) | copy-start | bytes 786436
  36.8 16.9 %all-to-all-start.1 = ((bf16[64,2,16,128]{3,2,1,0:T(8,128)(2,1)}), bf16[64,2,16,128]{3,2,1,0:T(8,128)(2,1)}, u32[]{:S(2)}, u32[]{:S(2)}) async-start(bf16[64,2,16,128]{3,2,1,0:T(8,128)(2,1)} %copy.49), calls=%async_computation.1 | async-start | bytes 1048576 | tf_op jit(solution)/shard_map/all_to_all | solution.py:161
  47.8 7.6 %copy-start.19 = (bf16[128,8,128]{2,1,0:T(8,128)(2,1)S(1)}, bf16[128,8,128]{2,1,0:T(8,128)(2,1)}, u32[]{:S(2)}) copy-start(bf16[128,8,128]{2,1,0:T(8,128)(2,1)} %get-tuple-element.33) | copy-start | bytes 786436
  49.5 10.3 %collective-permute-start.2 = (f32[8,32,1024]{2,1,0:T(8,128)}, f32[8,32,1024]{2,1,0:T(8,128)}, u32[]{:S(2)}, u32[]{:S(2)}) collective-permute-start(f32[8,32,1024]{2,1,0:T(8,128)} %fusion.79), channel_id=1, source_target_pairs={{0,64},{64,0},{1,65},{65,1},{2,66},{66,2},{3,67},{67,3},{4,68},{68... | collective-permute-start | bytes 3145736 | tf_op jit(solution)/shard_map/ppermute | solution.py:185
  59.8 4.3 %copy-start.7 = (f32[8,8,4,8,128]{4,3,1,2,0:T(8,128)}, f32[8,8,4,8,128]{4,3,1,2,0:T(8,128)S(1)}, u32[]{:S(2)}) copy-start(f32[8,8,4,8,128]{4,3,1,2,0:T(8,128)S(1)} %copy.111) | copy-start | bytes 3145732
  64.1 9.3 %collective-permute-start.3 = (f32[8,32,1024]{2,1,0:T(8,128)}, f32[8,32,1024]{2,1,0:T(8,128)}, u32[]{:S(2)}, u32[]{:S(2)}) collective-permute-start(f32[8,32,1024]{2,1,0:T(8,128)} %bitcast_multiply_fusion.7), channel_id=1, source_target_pairs={{64,0},{65,1},{66,2},{67,3},{68,4},{69,5},{70,6},{71,7},{72,8},{73... | collective-permute-start | bytes 3145736 | tf_op jit(solution)/shard_map/ppermute | solution.py:29
  73.4 6.0 %copy-start.2 = (bf16[1,16,128,1024]{3,2,1,0:T(8,128)(2,1)S(1)}, bf16[1,16,128,1024]{3,2,1,0:T(8,128)(2,1)}, u32[]{:S(2)}) copy-start(bf16[1,16,128,1024]{3,2,1,0:T(8,128)(2,1)} %param.23) | copy-start | bytes 12582916
  78.0 5.0 %collective-permute-start.4 = (f32[8,32,1024]{2,1,0:T(8,128)}, f32[8,32,1024]{2,1,0:T(8,128)}, u32[]{:S(2)}, u32[]{:S(2)}) collective-permute-start(f32[8,32,1024]{2,1,0:T(8,128)} %fusion.82), channel_id=1, source_target_pairs={{0,64},{1,65},{2,66},{3,67},{4,68},{5,69},{6,70},{7,71},{8,72},{9,... | collective-permute-start | bytes 3145736 | tf_op jit(solution)/shard_map/ppermute | solution.py:29
  82.1 5.6 %copy-start.25 = (s32[128]{0:T(128)S(1)}, s32[128]{0:T(128)}, u32[]{:S(2)}) copy-start(s32[128]{0:T(128)} %copy-done.24) | copy-start | bytes 1540
  87.6 4.8 %copy-start.11 = (f32[8,32,1024]{2,1,0:T(8,128)}, f32[8,32,1024]{2,1,0:T(8,128)S(1)}, u32[]{:S(2)}) copy-start(f32[8,32,1024]{2,1,0:T(8,128)S(1)} %get-tuple-element.3) | copy-start | bytes 3145732
  93.1 13.8 %collective-permute-start.5 = (f32[8,2,1024]{2,1,0:T(2,128)}, f32[8,2,1024]{2,1,0:T(2,128)}, u32[]{:S(2)}, u32[]{:S(2)}) collective-permute-start(f32[8,2,1024]{2,1,0:T(2,128)} %get-tuple-element.26), channel_id=1, source_target_pairs={{0,1},{1,2},{2,3},{3,4},{4,5},{5,6},{6,7},{7,8},{8,9},{9,10},{10,1... | collective-permute-start | bytes 196616 | tf_op jit(solution)/shard_map/ppermute | solution.py:18
  96.2 10.8 %collective-permute-start.6 = (f32[8,2,1024]{2,1,0:T(2,128)S(1)}, f32[8,2,1024]{2,1,0:T(2,128)}, u32[]{:S(2)}, u32[]{:S(2)}) collective-permute-start(f32[8,2,1024]{2,1,0:T(2,128)S(1)} %get-tuple-element.27), channel_id=1, source_target_pairs={{1,0},{2,1},{3,2},{4,3},{5,4},{6,5},{7,6},{8,7},{9,8},{10,9},{11,1... | collective-permute-start | bytes 196616 | tf_op jit(solution)/shard_map/ppermute | solution.py:20
  97.5 9.5 %copy-start.12 = (f32[8,32,1024]{2,1,0:T(8,128)S(1)}, f32[8,32,1024]{2,1,0:T(8,128)}, u32[]{:S(2)}) copy-start(f32[8,32,1024]{2,1,0:T(8,128)} %copy-done.11) | copy-start | bytes 3145732
  98.4 19.4 %all-to-all-start.2 = ((bf16[64,2,16,128]{3,2,1,0:T(8,128)(2,1)}), bf16[64,2,16,128]{3,2,1,0:T(8,128)(2,1)}, u32[]{:S(2)}, u32[]{:S(2)}) async-start(bf16[64,2,16,128]{3,2,1,0:T(8,128)(2,1)} %copy.58), calls=%async_computation.2 | async-start | bytes 1048576 | tf_op jit(solution)/shard_map/all_to_all | solution.py:161
  112.7 11.4 %collective-permute-start.7 = (f32[8,32,1024]{2,1,0:T(8,128)}, f32[8,32,1024]{2,1,0:T(8,128)}, u32[]{:S(2)}, u32[]{:S(2)}) collective-permute-start(f32[8,32,1024]{2,1,0:T(8,128)} %fusion.73), channel_id=1, source_target_pairs={{0,64},{64,0},{1,65},{65,1},{2,66},{66,2},{3,67},{67,3},{4,68},{68... | collective-permute-start | bytes 3145736 | tf_op jit(solution)/shard_map/ppermute | solution.py:185
  118.8 3.8 %copy-start.26 = (s32[128]{0:T(128)S(1)}, s32[128]{0:T(128)}, u32[]{:S(2)}) copy-start(s32[128]{0:T(128)} %copy-done.24) | copy-start | bytes 1540
  125.5 9.7 %copy-start.13 = (f32[1,8,32,1024]{3,2,1,0:T(8,128)S(1)}, f32[1,8,32,1024]{3,2,1,0:T(8,128)}, u32[]{:S(2)}) copy-start(f32[1,8,32,1024]{3,2,1,0:T(8,128)} %param.17) | copy-start | bytes 3145732
  125.5 9.7 %copy-start.14 = (f32[1,8,32,1024]{3,2,1,0:T(8,128)S(1)}, f32[1,8,32,1024]{3,2,1,0:T(8,128)}, u32[]{:S(2)}) copy-start(f32[1,8,32,1024]{3,2,1,0:T(8,128)} %param.16) | copy-start | bytes 3145732
  127.4 12.6 %copy-start.31 = (s32[16]{0:T(128)S(1)}, s32[16]{0:T(128)}, u32[]{:S(2)}) copy-start(s32[16]{0:T(128)} %copy-done.29) | copy-start | bytes 196
  127.4 7.9 %collective-permute-start.8 = (f32[8,32,1024]{2,1,0:T(8,128)S(1)}, f32[8,32,1024]{2,1,0:T(8,128)S(1)}, u32[]{:S(2)}, u32[]{:S(2)}) collective-permute-start(f32[8,32,1024]{2,1,0:T(8,128)S(1)} %bitcast_multiply_fusion.5), channel_id=1, source_target_pairs={{64,0},{65,1},{66,2},{67,3},{68,4},{69,5},{70,6},{71,7},{72,8},{73... | collective-permute-start | bytes 3145736 | tf_op jit(solution)/shard_map/ppermute | solution.py:29
  138.7 5.9 %collective-permute-start.9 = (f32[8,32,1024]{2,1,0:T(8,128)}, f32[8,32,1024]{2,1,0:T(8,128)S(1)}, u32[]{:S(2)}, u32[]{:S(2)}) collective-permute-start(f32[8,32,1024]{2,1,0:T(8,128)} %get-tuple-element.6), channel_id=1, source_target_pairs={{0,64},{1,65},{2,66},{3,67},{4,68},{5,69},{6,70},{7,71},{8,72},{9,... | collective-permute-start | bytes 3145736 | tf_op jit(solution)/shard_map/ppermute | solution.py:29
  140.6 3.4 %copy-start.23 = (bf16[1,16,128]{2,1,0:T(8,128)(2,1)S(1)}, bf16[1,16,128]{2,1,0:T(8,128)(2,1)}, u32[]{:S(2)}) copy-start(bf16[1,16,128]{2,1,0:T(8,128)(2,1)} %param.24) | copy-start | bytes 12292
  (14 other events, 22.0 us)

commit v2 on v1

--- a/solution.py
+++ b/solution.py
@@ -62,13 +62,15 @@
     slots, lanes, touched = col_oh.shape
     groups = col_count // lanes
     row_count = row_oh.shape[1]
-    grads = values.reshape(slots, levels, 1, touched)
-    placed = grads * group_mask[:, None, :, :].astype(jnp.bfloat16)
-    lines = jnp.einsum("slaj,sbj->slab", placed, col_oh, preferred_element_type=jnp.float32)
-    total = jnp.einsum(
-        "sr,slab->lrab", row_oh, lines.astype(jnp.bfloat16), preferred_element_type=jnp.float32
-    )
-    return lax.optimization_barrier(total.reshape(levels, row_count, groups * lanes))
+    grads = values.reshape(slots, 1, levels, touched)
+    placed = grads * group_mask[:, :, None, :].astype(jnp.bfloat16)
+    lines = jnp.einsum("salj,sbj->salb", placed, col_oh, preferred_element_type=jnp.float32)
+    lines = lines.astype(jnp.bfloat16)
+    parts = [
+        jnp.einsum("sr,slb->lrb", row_oh, lines[:, a], preferred_element_type=jnp.float32)
+        for a in range(groups)
+    ]
+    return jnp.concatenate(parts, axis=2)
 
 
 def on_device(

time: 148 us -> 146 us (0.986)
  starting transfers between devices: 55.6 us -> 59.4 us
  waiting for transfers between devices: 11.5 us -> 7.71 us
  matrix products: 27 us -> 24.6 us
  other arithmetic: 32.5 us -> 34.5 us
  local copies, waits for them, and re-layouts: 19.4 us -> 17.5 us
    all_to_all x2, starting transfers between devices: 14.5 us -> 19.3 us  [on_device(): got = lax.all_to_all(both, 'space', split_axis=0, concat_axis=0, tiled=True)]
    all_to_all x1, waiting for transfers between devices: 4.12 us -> 0.01 us  [on_device(): lax.all_to_all(packed_cells.reshape(owners_count, capacity, touched), 'sp...]
    unnamed x68, local copies, waits for them, and re-layouts: 6.13 us -> 3.69 us
    dot_general x2, matrix products: 3.5 us -> 1.31 us  [on_device(): jnp.einsum('toj,to->tj', jac_tiles, obs_dual.astype(jnp.bfloat16), prefer...]
    dot_general x4 -> x18, matrix products: 9.35 us -> 9.22 us  [the longest x2 6.71 us: spread_cols(): jnp.einsum('salj,sbj->salb', placed, col_oh, preferred_element_type=jnp.f...]
  transfers between devices with their start and end apart: 13 -> 13, of which waited for: 5 -> 4; matrix products, arithmetic and copies ran while one was open for 32% -> 32% of each run, Pallas kernels for 0% -> 0%
where the time goes in v2:
time: 146 us; the launch traced here: 145 us
  starting transfers between devices  59.4 us (41%)
  other arithmetic  34.5 us (24%)
  matrix products  24.6 us (17%)
  local copies, waits for them, and re-layouts  17.5 us (12%)
  waiting for transfers between devices  7.71 us (5%)
    all_to_all x2, starting transfers between devices, on_device(): got = lax.all_to_all(both, 'space', split_axis=0, concat_axis=0, tiled=True)  19.3 us
    ppermute x4, starting transfers between devices, shifted(): return lax.ppermute(value, axis, pairs)  14.3 us
    all_to_all x1, starting transfers between devices, on_device(): lax.all_to_all(packed_cells.reshape(owners_count, capacity, touched), 'sp...  12.1 us
    sub x2, other arithmetic, on_device(): source = r_model - err_field * upward  7.93 us
    dot_general x2, matrix products, spread_cols(): jnp.einsum('salj,sbj->salb', placed, col_oh, preferred_element_type=jnp.f...  6.71 us
    ppermute x2, starting transfers between devices, with_halo(): lax.ppermute(tail, axis, [(i, i + 1) for i in range(ends)])  6.38 us
    select_n x2, other arithmetic, on_device(): chosen = jnp.where(tm_here == 0, increment, dual_model)  6.17 us
    dot_general x2, matrix products, gather_cols(): jnp.einsum('slab,sbj->slaj', lines, col_oh, preferred_element_type=jnp.fl...  6.02 us
  transfers between devices with their start and end apart: 13, of which 4 were waited for; matrix products, arithmetic and copies ran while one was open for 32% of the time, Pallas kernels for 0%

profile of v2, /device:TPU:1, one launch (start us, length us, event | category | flops | bytes accessed | tf_op | source)
XLA Modules:
  0.0 145.1 jit_solution(4438720054296929644)
XLA Ops:
  4.1 12.1 %all-to-all-start = ((s32[64,2,128]{2,1,0:T(2,128)}), s32[64,2,128]{2,1,0:T(2,128)S(1)}, u32[]{:S(2)}, u32[]{:S(2)}) async-start(s32[64,2,128]{2,1,0:T(2,128)} %bitcast.9), calls=%async_computation | async-start | bytes 131072 | tf_op jit(solution)/shard_map/all_to_all | solution.py:124
  16.3 1.5 %broadcast_select_fusion.1 = f32[1,8,32,1024]{3,2,1,0:T(8,128)S(1)} fusion(f32[1,8,32,1024]{3,2,1,0:T(8,128)} %param.13, f32[1,8,32,1024]{3,2,1,0:T(8,128)} %param.14, pred[]{:T(512)S(6)} %eq.88), kind=kLoop, calls=%fused_computation.141 | loop fusion | flops 262144 | bytes 3145729 | tf_op jit(solution)/shard_map/jit(_where)/select_n | solution.py:180
  18.6 3.6 %collective-permute-start = (f32[2,8,2,1024]{3,2,1,0:T(2,128)}, f32[2,8,2,1024]{3,2,1,0:T(2,128)}, u32[]{:S(2)}, u32[]{:S(2)}) collective-permute-start(f32[2,8,2,1024]{3,2,1,0:T(2,128)} %get-tuple-element.24), channel_id=1, source_target_pairs={{0,1},{1,2},{2,3},{3,4},{4,5},{5,6},{6,7},{7,8},{8,9},{9,10},{10,1... | collective-permute-start | bytes 393224 | tf_op jit(solution)/shard_map/ppermute | solution.py:18
  22.2 1.3 collective-permute-start.1
  28.1 3.0 %multiply_reduce_fusion.1 = bf16[128,8,128]{2,1,0:T(8,128)(2,1)S(1)} fusion(f32[128,8,128]{2,1,0:T(8,128)S(1)} %get-tuple-element.48, s32[128,128]{1,0:T(8,128)S(1)} %get-tuple-element.51, bf16[128,8,8,128]{3,2,0,1:T(8,128)(2,1)S(1)} %bitcast.336), kind=kOutput, calls=%fused_computation.16 | convolution fusion | flops 272498688 | bytes 2949120 | tf_op jit(solution)/shard_map/slab,sbj->slaj/dot_general | solution.py:56
  32.0 10.5 %all-to-all-start.1 = ((bf16[64,2,16,128]{3,2,1,0:T(8,128)(2,1)}), bf16[64,2,16,128]{3,2,1,0:T(8,128)(2,1)}, u32[]{:S(2)}, u32[]{:S(2)}) async-start(bf16[64,2,16,128]{3,2,1,0:T(8,128)(2,1)} %copy.91), calls=%async_computation.1 | async-start | bytes 1048576 | tf_op jit(solution)/shard_map/all_to_all | solution.py:163
  42.5 1.4 pad_maximum_fusion
  47.6 1.7 %fusion.85 = f32[8,32,1024]{2,1,0:T(8,128)} fusion(f32[8,34,1024]{2,1,0:T(8,128)S(1)} %multiply_multiply_fusion.1, f32[8,32,1023]{2,1,0:T(8,128)S(1)} %get-tuple-element.35, f32[8,32,1]{2,1,0:T(8,128)S(1)} %get-tuple-element.37, f32[8,32,1]{2,1,0:T(8,128)S(1)} %get-tuple-element.36, f32[8,32,1023]{2,1,0:T(8,128)S(1)} %get-tuple-element.34, ...), kind=kLoop, calls=%fused_computation.101 | loop fusion | flops 2621440 | bytes 7340064 | tf_op jit(solution)/shard_map/mul | solution.py:44
  49.3 2.1 %collective-permute-start.2 = (f32[8,32,1024]{2,1,0:T(8,128)}, f32[8,32,1024]{2,1,0:T(8,128)}, u32[]{:S(2)}, u32[]{:S(2)}) collective-permute-start(f32[8,32,1024]{2,1,0:T(8,128)} %fusion.85), channel_id=1, source_target_pairs={{0,64},{64,0},{1,65},{65,1},{2,66},{66,2},{3,67},{67,3},{4,68},{68... | collective-permute-start | bytes 3145736 | tf_op jit(solution)/shard_map/ppermute | solution.py:187
  51.4 2.2 %all-to-all-done.1 = bf16[64,2,16,128]{3,2,1,0:T(8,128)(2,1)} async-done(((bf16[64,2,16,128]{3,2,1,0:T(8,128)(2,1)}), bf16[64,2,16,128]{3,2,1,0:T(8,128)(2,1)}, u32[]{:S(2)}, u32[]{:S(2)}) %all-to-all-start.1) | async-done | bytes 524320 | tf_op jit(solution)/shard_map/all_to_all | solution.py:163
  53.5 1.8 %fusion.203 = (bf16[64,1,16,128]{3,2,1,0:T(8,128)(2,1)}, bf16[64,1,16,128]{3,2,1,0:T(8,128)(2,1)S(1)}) fusion(bf16[64,2,16,128]{3,2,1,0:T(8,128)(2,1)} %all-to-all-done.1), kind=kLoop, calls=%fused_computation.263 | loop fusion | bytes 1048576 | tf_op jit(solution)/shard_map/slice | solution.py:164
  55.4 2.9 %fusion.25 = bf16[128,8,8,128]{3,2,1,0:T(8,128)(2,1)S(1)} fusion(s32[128,128]{1,0:T(8,128)S(1)} %get-tuple-element.51, bf16[128,8,128]{2,1,0:T(8,128)(2,1)S(1)} %copy-done.20, bf16[128,8,128]{2,1,0:T(8,128)(2,1)S(1)} %bitcast.348), kind=kOutput, calls=%fused_computation.28 | convolution fusion | flops 272629760 | bytes 2686976 | tf_op jit(solution)/shard_map/salj,sbj->salb/dot_general | solution.py:67
  60.3 2.5 %bitcast_multiply_fusion.7 = f32[8,32,1024]{2,1,0:T(8,128)} fusion(f32[1,8,32,1024]{3,2,1,0:T(8,128)S(1)} %copy-done.8, f32[8,32,1024]{2,1,0:T(8,128)S(1)} %fusion.64, f32[8,32,1024]{2,1,0:T(8,128)} %collective-permute-done.2, f32[]{:T(128)S(6)} %sub.85, f32[1,8,32,1024]{3,2,1,0:T(8,128)S(1)} %copy-done.6), kind=kLoop, calls=%fused_computation.115 | loop fusion | flops 1310720 | bytes 5242884 | tf_op jit(solution)/shard_map/mul | solution.py:191
  62.9 6.0 %collective-permute-start.3 = (f32[8,32,1024]{2,1,0:T(8,128)}, f32[8,32,1024]{2,1,0:T(8,128)}, u32[]{:S(2)}, u32[]{:S(2)}) collective-permute-start(f32[8,32,1024]{2,1,0:T(8,128)} %bitcast_multiply_fusion.7), channel_id=1, source_target_pairs={{64,0},{65,1},{66,2},{67,3},{68,4},{69,5},{70,6},{71,7},{72,8},{73... | collective-permute-start | bytes 3145736 | tf_op jit(solution)/shard_map/ppermute | solution.py:29
  72.1 4.5 %fusion.88 = f32[8,32,1024]{2,1,0:T(8,128)} fusion(f32[1,8,32,1024]{3,2,1,0:T(8,128)} %param.17, f32[1,8,32,1024]{3,2,1,0:T(8,128)} %param.16, f32[1,8,32,1024]{3,2,1,0:T(8,128)S(1)} %copy-done.5, f32[1,8,32,1024]{3,2,1,0:T(8,128)S(1)} %copy-done.6, f32[8,32,1024]{2,1,0:T(8,128)} %collective-permute-done.2, f32[]{:T(128)S(6)} %sub.92, ...), kind=kLoop, calls=%fused_computation.108 | loop fusion | flops 3145728 | bytes 8388616 | tf_op jit(solution)/shard_map/sub | solution.py:208
  76.6 1.4 collective-permute-start.4
  81.6 4.6 %broadcast_select_fusion = (f32[8,32,1024]{2,1,0:T(8,128)S(1)}, f32[8,32,1024]{2,1,0:T(8,128)S(1)}, f32[8,32,1024]{2,1,0:T(8,128)}) fusion(pred[]{:T(512)S(6)} %eq.88, f32[8,32,1024]{2,1,0:T(8,128)} %fusion.88, f32[8,32,1024]{2,1,0:T(8,128)} %collective-permute-done.4, f32[1,8,32,1024]{3,2,1,0:T(8,128)} %param.18, f32[1,8,32,1024]{3,2,1,0:T(8,128)S(1)} %copy-done.5, ...), kind=kLoop, calls=%fused_computation.140 | loop fusion | flops 2621440 | bytes 11534341 | tf_op jit(solution)/shard_map/jit(_where)/select_n | solution.py:180
  88.1 3.0 %multiply_reduce_fusion = bf16[128,8,128]{2,1,0:T(8,128)(2,1)S(1)} fusion(f32[128,8,128]{2,1,0:T(8,128)S(1)} %copy-done.19, s32[128,128]{1,0:T(8,128)S(1)} %get-tuple-element.51, bf16[128,8,8,128]{3,2,0,1:T(8,128)(2,1)S(1)} %bitcast.337), kind=kOutput, calls=%fused_computation.15 | convolution fusion | flops 272498688 | bytes 2949120 | tf_op jit(solution)/shard_map/slab,sbj->slaj/dot_general | solution.py:56
  91.8 2.8 %collective-permute-start.5 = (f32[8,2,1024]{2,1,0:T(2,128)}, f32[8,2,1024]{2,1,0:T(2,128)}, u32[]{:S(2)}, u32[]{:S(2)}) collective-permute-start(f32[8,2,1024]{2,1,0:T(2,128)} %get-tuple-element.42), channel_id=1, source_target_pairs={{0,1},{1,2},{2,3},{3,4},{4,5},{5,6},{6,7},{7,8},{8,9},{9,10},{10,1... | collective-permute-start | bytes 196616 | tf_op jit(solution)/shard_map/ppermute | solution.py:18
  96.8 8.8 %all-to-all-start.2 = ((bf16[64,2,16,128]{3,2,1,0:T(8,128)(2,1)}), bf16[64,2,16,128]{3,2,1,0:T(8,128)(2,1)}, u32[]{:S(2)}, u32[]{:S(2)}) async-start(bf16[64,2,16,128]{3,2,1,0:T(8,128)(2,1)} %copy.106), calls=%async_computation.2 | async-start | bytes 1048576 | tf_op jit(solution)/shard_map/all_to_all | solution.py:163
  105.6 1.7 %maximum_multiply_fusion = f32[8,36,1024]{2,1,0:T(8,128)S(1)} fusion(f32[8,2,1024]{2,1,0:T(2,128)} %collective-permute-done.6, f32[8,32,1024]{2,1,0:T(8,128)S(1)} %copy-done.13, f32[8,2,1024]{2,1,0:T(2,128)} %collective-permute-done.5, f32[2,8,36,1024]{3,2,1,0:T(8,128)} %copy-done.4), kind=kLoop, calls=%fused_computation.47 | loop fusion | flops 884736 | bytes 3538944 | tf_op jit(solution)/shard_map/mul | solution.py:35
  109.6 1.7 %fusion.79 = f32[8,32,1024]{2,1,0:T(8,128)} fusion(f32[8,34,1024]{2,1,0:T(8,128)S(1)} %multiply_multiply_fusion, f32[8,32,1023]{2,1,0:T(8,128)S(1)} %get-tuple-element.27, f32[8,32,1]{2,1,0:T(8,128)S(1)} %get-tuple-element.29, f32[8,32,1]{2,1,0:T(8,128)S(1)} %get-tuple-element.28, f32[8,32,1023]{2,1,0:T(8,128)S(1)} %get-tuple-element.26, ...), kind=kLoop, calls=%fused_computation.94 | loop fusion | flops 2621440 | bytes 7340064 | tf_op jit(solution)/shard_map/mul | solution.py:44
  111.3 2.7 %collective-permute-start.7 = (f32[8,32,1024]{2,1,0:T(8,128)}, f32[8,32,1024]{2,1,0:T(8,128)}, u32[]{:S(2)}, u32[]{:S(2)}) collective-permute-start(f32[8,32,1024]{2,1,0:T(8,128)} %fusion.79), channel_id=1, source_target_pairs={{0,64},{64,0},{1,65},{65,1},{2,66},{66,2},{3,67},{67,3},{4,68},{68... | collective-permute-start | bytes 3145736 | tf_op jit(solution)/shard_map/ppermute | solution.py:187
  114.0 2.4 %all-to-all-done.2 = bf16[64,2,16,128]{3,2,1,0:T(8,128)(2,1)} async-done(((bf16[64,2,16,128]{3,2,1,0:T(8,128)(2,1)}), bf16[64,2,16,128]{3,2,1,0:T(8,128)(2,1)}, u32[]{:S(2)}, u32[]{:S(2)}) %all-to-all-start.2) | async-done | bytes 524320 | tf_op jit(solution)/shard_map/all_to_all | solution.py:163
  117.4 3.8 %fusion.30 = bf16[128,8,8,128]{3,2,1,0:T(8,128)(2,1)S(1)} fusion(s32[128,128]{1,0:T(8,128)S(1)} %get-tuple-element.51, bf16[128,8,128]{2,1,0:T(8,128)(2,1)S(1)} %bitcast.347, bf16[128,8,128]{2,1,0:T(8,128)(2,1)} %get-tuple-element.49), kind=kOutput, calls=%fused_computation.29 | convolution fusion | flops 272629760 | bytes 2686976 | tf_op jit(solution)/shard_map/salj,sbj->salb/dot_general | solution.py:67
  123.4 1.8 %bitcast_multiply_fusion.5 = f32[8,32,1024]{2,1,0:T(8,128)S(1)} fusion(f32[1,8,32,1024]{3,2,1,0:T(8,128)S(1)} %copy-done.9, f32[8,32,1024]{2,1,0:T(8,128)S(1)} %fusion.56, f32[8,32,1024]{2,1,0:T(8,128)S(1)} %copy-done.11, f32[8,32,1024]{2,1,0:T(8,128)} %collective-permute-done.7, f32[]{:T(128)S(6)} %sub.85), kind=kLoop, calls=%fused_computation.113 | loop fusion | flops 1310720 | bytes 5242884 | tf_op jit(solution)/shard_map/mul | solution.py:191
  125.2 5.7 %collective-permute-start.8 = (f32[8,32,1024]{2,1,0:T(8,128)S(1)}, f32[8,32,1024]{2,1,0:T(8,128)S(1)}, u32[]{:S(2)}, u32[]{:S(2)}) collective-permute-start(f32[8,32,1024]{2,1,0:T(8,128)S(1)} %bitcast_multiply_fusion.5), channel_id=1, source_target_pairs={{64,0},{65,1},{66,2},{67,3},{68,4},{69,5},{70,6},{71,7},{72,8},{73... | collective-permute-start | bytes 3145736 | tf_op jit(solution)/shard_map/ppermute | solution.py:29
  130.9 2.2 %collective-permute-done.8 = f32[8,32,1024]{2,1,0:T(8,128)S(1)} collective-permute-done((f32[8,32,1024]{2,1,0:T(8,128)S(1)}, f32[8,32,1024]{2,1,0:T(8,128)S(1)}, u32[]{:S(2)}, u32[]{:S(2)}) %collective-permute-start.8) | collective-permute-done | bytes 1048608 | tf_op jit(solution)/shard_map/ppermute | solution.py:29
  133.1 3.4 %fusion.91 = (f32[8,32,1024]{2,1,0:T(8,128)}, f32[1,8,32,1024]{3,2,1,0:T(8,128)}) fusion(f32[8,32,1024]{2,1,0:T(8,128)S(1)} %copy-done.11, f32[1,8,32,1024]{3,2,1,0:T(8,128)S(1)} %copy-done.14, f32[1,8,32,1024]{3,2,1,0:T(8,128)S(1)} %copy-done.15, f32[8,32,1024]{2,1,0:T(8,128)S(1)} %get-tuple-element.4, f32[8,32,1024]{2,1,0:T(8,128)} %collective-permute-done.7, ...), kind=kLoop, calls=%fused_computation.111 | loop fusion | flops 3407872 | bytes 9437192 | tf_op jit(solution)/shard_map/sub | solution.py:208
  136.5 1.3 collective-permute-start.9
  138.4 3.4 %fusion.9 = f32[16,1,128]{2,1,0:T(1,128)S(1)} fusion(bf16[16,1024,1]{1,2,0:T(2,128)(2,1)S(1)} %copy.125, bf16[1,16,128,1024]{3,2,1,0:T(8,128)(2,1)} %param.23), kind=kOutput, calls=%fused_computation.7 | convolution fusion | flops 4194304 | bytes 4235264 | tf_op jit(solution)/shard_map/toj,tj->to/dot_general | solution.py:172
  142.5 2.7 %fusion.96 = f32[1,8,32,1024]{3,2,1,0:T(8,128)} fusion(f32[8,32,1024]{2,1,0:T(8,128)S(1)} %get-tuple-element.4, f32[8,32,1024]{2,1,0:T(8,128)} %get-tuple-element.6, f32[8,32,1024]{2,1,0:T(8,128)S(1)} %collective-permute-done.9, f32[1,8,32,1024]{3,2,1,0:T(8,128)S(1)} %copy-done.9), kind=kLoop, calls=%fused_computation.120 | loop fusion | flops 786432 | bytes 5242880 | tf_op jit(solution)/shard_map/broadcast_in_dim | solution.py:213
  (146 shorter events, 33.4 us)
Async XLA Ops:
  4.1 13.7 %copy-start.16 = (f32[8,32,1024]{2,1,0:T(8,128)S(1)}, f32[8,32,1024]{2,1,0:T(8,128)}, u32[]{:S(2)}) copy-start(f32[8,32,1024]{2,1,0:T(8,128)} %param.19) | copy-start | bytes 3145732
  4.1 21.5 %all-to-all-start = ((s32[64,2,128]{2,1,0:T(2,128)}), s32[64,2,128]{2,1,0:T(2,128)S(1)}, u32[]{:S(2)}, u32[]{:S(2)}) async-start(s32[64,2,128]{2,1,0:T(2,128)} %bitcast.9), calls=%async_computation | async-start | bytes 131072 | tf_op jit(solution)/shard_map/all_to_all | solution.py:124
  16.3 7.3 %copy-start.2 = (bf16[1,16,128,1024]{3,2,1,0:T(8,128)(2,1)S(1)}, bf16[1,16,128,1024]{3,2,1,0:T(8,128)(2,1)}, u32[]{:S(2)}) copy-start(bf16[1,16,128,1024]{3,2,1,0:T(8,128)(2,1)} %param.23) | copy-start | bytes 12582916
  17.8 5.7 %copy-start.32 = (s32[1,16]{1,0:T(1,128)S(1)}, s32[1,16]{1,0:T(1,128)}, u32[]{:S(2)}) copy-start(s32[1,16]{1,0:T(1,128)} %param.21) | copy-start | bytes 196
  17.8 5.7 %copy-start.21 = (bf16[1,16,128]{2,1,0:T(8,128)(2,1)S(1)}, bf16[1,16,128]{2,1,0:T(8,128)(2,1)}, u32[]{:S(2)}) copy-start(bf16[1,16,128]{2,1,0:T(8,128)(2,1)} %param.15) | copy-start | bytes 12292
  18.6 23.8 %collective-permute-start = (f32[2,8,2,1024]{3,2,1,0:T(2,128)}, f32[2,8,2,1024]{3,2,1,0:T(2,128)}, u32[]{:S(2)}, u32[]{:S(2)}) collective-permute-start(f32[2,8,2,1024]{3,2,1,0:T(2,128)} %get-tuple-element.24), channel_id=1, source_target_pairs={{0,1},{1,2},{2,3},{3,4},{4,5},{5,6},{6,7},{7,8},{8,9},{9,10},{10,1... | collective-permute-start | bytes 393224 | tf_op jit(solution)/shard_map/ppermute | solution.py:18
  22.2 20.3 %collective-permute-start.1 = (f32[2,8,2,1024]{3,2,1,0:T(2,128)}, f32[2,8,2,1024]{3,2,1,0:T(2,128)}, u32[]{:S(2)}, u32[]{:S(2)}) collective-permute-start(f32[2,8,2,1024]{3,2,1,0:T(2,128)} %get-tuple-element.25), channel_id=1, source_target_pairs={{1,0},{2,1},{3,2},{4,3},{5,4},{6,5},{7,6},{8,7},{9,8},{10,9},{11,1... | collective-permute-start | bytes 393224 | tf_op jit(solution)/shard_map/ppermute | solution.py:20
  28.0 3.0 %copy-start.18 = (f32[128,8,128]{2,1,0:T(8,128)}, f32[128,8,128]{2,1,0:T(8,128)S(1)}, u32[]{:S(2)}) copy-start(f32[128,8,128]{2,1,0:T(8,128)S(1)} %get-tuple-element.48) | copy-start | bytes 1572868
  28.1 3.0 %copy-start.17 = (bf16[128,8,128]{2,1,0:T(8,128)(2,1)S(1)}, bf16[128,8,128]{2,1,0:T(8,128)(2,1)}, u32[]{:S(2)}) copy-start(bf16[128,8,128]{2,1,0:T(8,128)(2,1)} %copy.90) | copy-start | bytes 786436
  32.0 21.6 %all-to-all-start.1 = ((bf16[64,2,16,128]{3,2,1,0:T(8,128)(2,1)}), bf16[64,2,16,128]{3,2,1,0:T(8,128)(2,1)}, u32[]{:S(2)}, u32[]{:S(2)}) async-start(bf16[64,2,16,128]{3,2,1,0:T(8,128)(2,1)} %copy.91), calls=%async_computation.1 | async-start | bytes 1048576 | tf_op jit(solution)/shard_map/all_to_all | solution.py:163
  47.6 7.7 %copy-start.20 = (bf16[128,8,128]{2,1,0:T(8,128)(2,1)S(1)}, bf16[128,8,128]{2,1,0:T(8,128)(2,1)}, u32[]{:S(2)}) copy-start(bf16[128,8,128]{2,1,0:T(8,128)(2,1)} %get-tuple-element.49) | copy-start | bytes 786436
  49.3 10.7 %collective-permute-start.2 = (f32[8,32,1024]{2,1,0:T(8,128)}, f32[8,32,1024]{2,1,0:T(8,128)}, u32[]{:S(2)}, u32[]{:S(2)}) collective-permute-start(f32[8,32,1024]{2,1,0:T(8,128)} %fusion.85), channel_id=1, source_target_pairs={{0,64},{64,0},{1,65},{65,1},{2,66},{66,2},{3,67},{67,3},{4,68},{68... | collective-permute-start | bytes 3145736 | tf_op jit(solution)/shard_map/ppermute | solution.py:187
  59.9 2.9 %copy-start.10 = (f32[8,32,1024]{2,1,0:T(8,128)}, f32[8,32,1024]{2,1,0:T(8,128)S(1)}, u32[]{:S(2)}) copy-start(f32[8,32,1024]{2,1,0:T(8,128)S(1)} %fusion.64) | copy-start | bytes 3145732
  59.9 8.9 %copy-start.29 = (s32[16]{0:T(128)S(1)}, s32[16]{0:T(128)}, u32[]{:S(2)}) copy-start(s32[16]{0:T(128)} %copy-done.28) | copy-start | bytes 196
  62.9 9.2 %collective-permute-start.3 = (f32[8,32,1024]{2,1,0:T(8,128)}, f32[8,32,1024]{2,1,0:T(8,128)}, u32[]{:S(2)}, u32[]{:S(2)}) collective-permute-start(f32[8,32,1024]{2,1,0:T(8,128)} %bitcast_multiply_fusion.7), channel_id=1, source_target_pairs={{64,0},{65,1},{66,2},{67,3},{68,4},{69,5},{70,6},{71,7},{72,8},{73... | collective-permute-start | bytes 3145736 | tf_op jit(solution)/shard_map/ppermute | solution.py:29
  72.1 6.0 %copy-start.3 = (bf16[1,16,128,1024]{3,2,1,0:T(8,128)(2,1)S(1)}, bf16[1,16,128,1024]{3,2,1,0:T(8,128)(2,1)}, u32[]{:S(2)}) copy-start(bf16[1,16,128,1024]{3,2,1,0:T(8,128)(2,1)} %param.23) | copy-start | bytes 12582916
  76.6 2.6 %copy-start.24 = (bf16[1,16,128]{2,1,0:T(8,128)(2,1)S(1)}, bf16[1,16,128]{2,1,0:T(8,128)(2,1)}, u32[]{:S(2)}) copy-start(bf16[1,16,128]{2,1,0:T(8,128)(2,1)} %param.24) | copy-start | bytes 12292
  76.6 5.0 %collective-permute-start.4 = (f32[8,32,1024]{2,1,0:T(8,128)}, f32[8,32,1024]{2,1,0:T(8,128)}, u32[]{:S(2)}, u32[]{:S(2)}) collective-permute-start(f32[8,32,1024]{2,1,0:T(8,128)} %fusion.88), channel_id=1, source_target_pairs={{0,64},{1,65},{2,66},{3,67},{4,68},{5,69},{6,70},{7,71},{8,72},{9,... | collective-permute-start | bytes 3145736 | tf_op jit(solution)/shard_map/ppermute | solution.py:29
  86.3 4.8 %copy-start.12 = (f32[8,32,1024]{2,1,0:T(8,128)}, f32[8,32,1024]{2,1,0:T(8,128)S(1)}, u32[]{:S(2)}) copy-start(f32[8,32,1024]{2,1,0:T(8,128)S(1)} %get-tuple-element.3) | copy-start | bytes 3145732
  91.8 13.8 %collective-permute-start.5 = (f32[8,2,1024]{2,1,0:T(2,128)}, f32[8,2,1024]{2,1,0:T(2,128)}, u32[]{:S(2)}, u32[]{:S(2)}) collective-permute-start(f32[8,2,1024]{2,1,0:T(2,128)} %get-tuple-element.42), channel_id=1, source_target_pairs={{0,1},{1,2},{2,3},{3,4},{4,5},{5,6},{6,7},{7,8},{8,9},{9,10},{10,1... | collective-permute-start | bytes 196616 | tf_op jit(solution)/shard_map/ppermute | solution.py:18
  94.6 11.0 %collective-permute-start.6 = (f32[8,2,1024]{2,1,0:T(2,128)S(1)}, f32[8,2,1024]{2,1,0:T(2,128)}, u32[]{:S(2)}, u32[]{:S(2)}) collective-permute-start(f32[8,2,1024]{2,1,0:T(2,128)S(1)} %get-tuple-element.43), channel_id=1, source_target_pairs={{1,0},{2,1},{3,2},{4,3},{5,4},{6,5},{7,6},{8,7},{9,8},{10,9},{11,1... | collective-permute-start | bytes 196616 | tf_op jit(solution)/shard_map/ppermute | solution.py:20
  95.9 9.7 %copy-start.13 = (f32[8,32,1024]{2,1,0:T(8,128)S(1)}, f32[8,32,1024]{2,1,0:T(8,128)}, u32[]{:S(2)}) copy-start(f32[8,32,1024]{2,1,0:T(8,128)} %copy-done.12) | copy-start | bytes 3145732
  96.8 19.6 %all-to-all-start.2 = ((bf16[64,2,16,128]{3,2,1,0:T(8,128)(2,1)}), bf16[64,2,16,128]{3,2,1,0:T(8,128)(2,1)}, u32[]{:S(2)}, u32[]{:S(2)}) async-start(bf16[64,2,16,128]{3,2,1,0:T(8,128)(2,1)} %copy.106), calls=%async_computation.2 | async-start | bytes 1048576 | tf_op jit(solution)/shard_map/all_to_all | solution.py:163
  111.3 11.7 %collective-permute-start.7 = (f32[8,32,1024]{2,1,0:T(8,128)}, f32[8,32,1024]{2,1,0:T(8,128)}, u32[]{:S(2)}, u32[]{:S(2)}) collective-permute-start(f32[8,32,1024]{2,1,0:T(8,128)} %fusion.79), channel_id=1, source_target_pairs={{0,64},{64,0},{1,65},{65,1},{2,66},{66,2},{3,67},{67,3},{4,68},{68... | collective-permute-start | bytes 3145736 | tf_op jit(solution)/shard_map/ppermute | solution.py:187
  123.4 9.7 %copy-start.14 = (f32[1,8,32,1024]{3,2,1,0:T(8,128)S(1)}, f32[1,8,32,1024]{3,2,1,0:T(8,128)}, u32[]{:S(2)}) copy-start(f32[1,8,32,1024]{3,2,1,0:T(8,128)} %param.17) | copy-start | bytes 3145732
  123.4 9.7 %copy-start.15 = (f32[1,8,32,1024]{3,2,1,0:T(8,128)S(1)}, f32[1,8,32,1024]{3,2,1,0:T(8,128)}, u32[]{:S(2)}) copy-start(f32[1,8,32,1024]{3,2,1,0:T(8,128)} %param.16) | copy-start | bytes 3145732
  125.2 12.6 %copy-start.31 = (s32[16]{0:T(128)S(1)}, s32[16]{0:T(128)}, u32[]{:S(2)}) copy-start(s32[16]{0:T(128)} %copy-done.28) | copy-start | bytes 196
  125.2 7.9 %collective-permute-start.8 = (f32[8,32,1024]{2,1,0:T(8,128)S(1)}, f32[8,32,1024]{2,1,0:T(8,128)S(1)}, u32[]{:S(2)}, u32[]{:S(2)}) collective-permute-start(f32[8,32,1024]{2,1,0:T(8,128)S(1)} %bitcast_multiply_fusion.5), channel_id=1, source_target_pairs={{64,0},{65,1},{66,2},{67,3},{68,4},{69,5},{70,6},{71,7},{72,8},{73... | collective-permute-start | bytes 3145736 | tf_op jit(solution)/shard_map/ppermute | solution.py:29
  136.5 6.0 %collective-permute-start.9 = (f32[8,32,1024]{2,1,0:T(8,128)}, f32[8,32,1024]{2,1,0:T(8,128)S(1)}, u32[]{:S(2)}, u32[]{:S(2)}) collective-permute-start(f32[8,32,1024]{2,1,0:T(8,128)} %get-tuple-element.6), channel_id=1, source_target_pairs={{0,64},{1,65},{2,66},{3,67},{4,68},{5,69},{6,70},{7,71},{8,72},{9,... | collective-permute-start | bytes 3145736 | tf_op jit(solution)/shard_map/ppermute | solution.py:29
  138.4 3.4 %copy-start.23 = (bf16[1,16,128]{2,1,0:T(8,128)(2,1)S(1)}, bf16[1,16,128]{2,1,0:T(8,128)(2,1)}, u32[]{:S(2)}) copy-start(bf16[1,16,128]{2,1,0:T(8,128)(2,1)} %param.25) | copy-start | bytes 12292
  138.4 3.4 %copy-start.25 = (bf16[1,16,128]{2,1,0:T(8,128)(2,1)S(1)}, bf16[1,16,128]{2,1,0:T(8,128)(2,1)}, u32[]{:S(2)}) copy-start(bf16[1,16,128]{2,1,0:T(8,128)(2,1)} %param.24) | copy-start | bytes 12292
  142.5 2.7 %copy-start.1 = (s32[1,16,128]{2,1,0:T(8,128)S(1)}, s32[1,16,128]{2,1,0:T(8,128)}, u32[]{:S(2)}) copy-start(s32[1,16,128]{2,1,0:T(8,128)} %param.22) | copy-start | bytes 24580
  (14 other events, 19.4 us)

commit v3 on v0

--- a/solution.py
+++ b/solution.py
@@ -13,13 +13,11 @@
     ends = count - 1
     head = lax.slice_in_dim(cells, 0, width, axis=dim)
     tail = lax.slice_in_dim(cells, cells.shape[dim] - width, cells.shape[dim], axis=dim)
+    flat = (-1, cells.shape[-1])
+    from_prev = lax.ppermute(tail.reshape(flat), axis, [(i, i + 1) for i in range(ends)])
+    from_next = lax.ppermute(head.reshape(flat), axis, [(i + 1, i) for i in range(ends)])
     return jnp.concatenate(
-        [
-            lax.ppermute(tail, axis, [(i, i + 1) for i in range(ends)]),
-            cells,
-            lax.ppermute(head, axis, [(i + 1, i) for i in range(ends)]),
-        ],
-        axis=dim,
+        [from_prev.reshape(tail.shape), cells, from_next.reshape(head.shape)], axis=dim
     )
 
 

time: 145 us -> 146 us (level)
  local copies, waits for them, and re-layouts: 16.3 us -> 21.4 us
  waiting for transfers between devices: 11.5 us -> 9.03 us
  other arithmetic: 32.3 us -> 30.6 us
    reshape x0 -> x8, local copies, waits for them, and re-layouts: none -> 5.06 us  [the longest x2 1.86 us: with_halo(): from_next.reshape(head.shape)]
    all_to_all x2, waiting for transfers between devices: 4.26 us -> 2.44 us  [on_device(): got = lax.all_to_all(both, 'space', split_axis=0, concat_axis=0, tiled=True)]
    unnamed x68 -> x74, local copies, waits for them, and re-layouts: 3.32 us -> 3.33 us
  transfers between devices with their start and end apart: 13 -> 13, of which waited for: 5 -> 5; matrix products, arithmetic and copies ran while one was open for 32% -> 35% of each run, Pallas kernels for 0% -> 0%
where the time goes in v3:
time: 146 us; the launch traced here: 145 us
  starting transfers between devices  55.6 us (38%)
  other arithmetic  30.6 us (21%)
  matrix products  27 us (18%)
  local copies, waits for them, and re-layouts  21.4 us (15%)
  waiting for transfers between devices  9.03 us (6%)
    all_to_all x2, starting transfers between devices, on_device(): got = lax.all_to_all(both, 'space', split_axis=0, concat_axis=0, tiled=True)  15.1 us
    ppermute x4, starting transfers between devices, shifted(): return lax.ppermute(value, axis, pairs)  14.4 us
    all_to_all x1, starting transfers between devices, on_device(): lax.all_to_all(packed_cells.reshape(owners_count, capacity, touched), 'sp...  11.6 us
    sub x2, other arithmetic, on_device(): source = r_model - err_field * upward  7.76 us
    ppermute x2, starting transfers between devices, with_halo(): lax.ppermute(tail.reshape(flat), axis, [(i, i + 1) for i in range(ends)])  6.79 us
    dot_general x2, matrix products, spread_cols(): jnp.einsum('slaj,sbj->slab', placed, col_oh, preferred_element_type=jnp.f...  6.72 us
    select_n x2, other arithmetic, on_device(): chosen = jnp.where(tm_here == 0, increment, dual_model)  6.02 us
    dot_general x2, matrix products, gather_cols(): jnp.einsum('slab,sbj->slaj', lines, col_oh, preferred_element_type=jnp.fl...  6.02 us
  transfers between devices with their start and end apart: 13, of which 5 were waited for; matrix products, arithmetic and copies ran while one was open for 35% of the time, Pallas kernels for 0%

profile of v3, /device:TPU:1, one launch (start us, length us, event | category | flops | bytes accessed | tf_op | source)
XLA Modules:
  0.0 145.0 jit_solution(14963961355433533616)
XLA Ops:
  0.7 1.5 %broadcast_select_fusion.1 = f32[1,8,32,1024]{3,2,1,0:T(8,128)S(1)} fusion(f32[1,8,32,1024]{3,2,1,0:T(8,128)} %param.13, f32[1,8,32,1024]{3,2,1,0:T(8,128)} %param.14, pred[]{:T(512)S(6)} %eq.87), kind=kLoop, calls=%fused_computation.115 | loop fusion | flops 262144 | bytes 3145729 | tf_op jit(solution)/shard_map/jit(_where)/select_n | solution.py:176
  3.0 4.6 %collective-permute-start = (f32[32,1024]{1,0:T(8,128)}, f32[32,1024]{1,0:T(8,128)}, u32[]{:S(2)}, u32[]{:S(2)}) collective-permute-start(f32[32,1024]{1,0:T(8,128)} %reshape.184), channel_id=1, source_target_pairs={{0,1},{1,2},{2,3},{3,4},{4,5},{5,6},{6,7},{7,8},{8,9},{9,10},{10,1... | collective-permute-start | bytes 393224 | tf_op jit(solution)/shard_map/ppermute | solution.py:17
  11.2 11.6 %all-to-all-start = ((s32[64,2,128]{2,1,0:T(2,128)}), s32[64,2,128]{2,1,0:T(2,128)S(1)}, u32[]{:S(2)}, u32[]{:S(2)}) async-start(s32[64,2,128]{2,1,0:T(2,128)} %bitcast.9), calls=%async_computation | async-start | bytes 131072 | tf_op jit(solution)/shard_map/all_to_all | solution.py:120
  22.8 2.8 %fusion.15 = bf16[16,1,1024]{2,1,0:T(2,128)(2,1)S(1)} fusion(bf16[1,16,128,1024]{3,2,1,0:T(8,128)(2,1)} %param.23, bf16[16,128,1]{1,0,2:T(8,128)(2,1)S(1)} %bitcast.269), kind=kOutput, calls=%fused_computation.13 | convolution fusion | flops 4194304 | bytes 4231168 | tf_op jit(solution)/shard_map/toj,to->tj/dot_general | solution.py:143
  27.1 4.1 %all-to-all-done = s32[64,2,128]{2,1,0:T(2,128)S(1)} async-done(((s32[64,2,128]{2,1,0:T(2,128)}), s32[64,2,128]{2,1,0:T(2,128)S(1)}, u32[]{:S(2)}, u32[]{:S(2)}) %all-to-all-start) | async-done | bytes 65568 | tf_op jit(solution)/shard_map/all_to_all | solution.py:120
  33.6 3.0 %multiply_reduce_fusion.1 = bf16[128,8,128]{2,1,0:T(8,128)(2,1)S(1)} fusion(f32[128,8,128]{2,1,0:T(8,128)S(1)} %get-tuple-element.32, s32[128,128]{1,0:T(8,128)S(1)} %get-tuple-element.35, bf16[128,8,8,128]{3,2,0,1:T(8,128)(2,1)S(1)} %bitcast.253), kind=kOutput, calls=%fused_computation.16 | convolution fusion | flops 272498688 | bytes 2949120 | tf_op jit(solution)/shard_map/slab,sbj->slaj/dot_general | solution.py:54
  37.6 5.9 %all-to-all-start.1 = ((bf16[64,2,16,128]{3,2,1,0:T(8,128)(2,1)}), bf16[64,2,16,128]{3,2,1,0:T(8,128)(2,1)}, u32[]{:S(2)}, u32[]{:S(2)}) async-start(bf16[64,2,16,128]{3,2,1,0:T(8,128)(2,1)} %copy.49), calls=%async_computation.1 | async-start | bytes 1048576 | tf_op jit(solution)/shard_map/all_to_all | solution.py:159
  49.6 1.7 %fusion.79 = f32[8,32,1024]{2,1,0:T(8,128)} fusion(f32[8,34,1024]{2,1,0:T(8,128)S(1)} %multiply_multiply_fusion.1, f32[8,32,1023]{2,1,0:T(8,128)S(1)} %get-tuple-element.19, f32[8,32,1]{2,1,0:T(8,128)S(1)} %get-tuple-element.21, f32[8,32,1]{2,1,0:T(8,128)S(1)} %get-tuple-element.20, f32[8,32,1023]{2,1,0:T(8,128)S(1)} %get-tuple-element.18, ...), kind=kLoop, calls=%fused_computation.77 | loop fusion | flops 2621440 | bytes 7340064 | tf_op jit(solution)/shard_map/mul | solution.py:42
  51.3 2.2 %collective-permute-start.2 = (f32[8,32,1024]{2,1,0:T(8,128)}, f32[8,32,1024]{2,1,0:T(8,128)}, u32[]{:S(2)}, u32[]{:S(2)}) collective-permute-start(f32[8,32,1024]{2,1,0:T(8,128)} %fusion.79), channel_id=1, source_target_pairs={{0,64},{64,0},{1,65},{65,1},{2,66},{66,2},{3,67},{67,3},{4,68},{68... | collective-permute-start | bytes 3145736 | tf_op jit(solution)/shard_map/ppermute | solution.py:183
  54.4 1.8 %fusion.153 = (bf16[64,1,16,128]{3,2,1,0:T(8,128)(2,1)}, bf16[64,1,16,128]{3,2,1,0:T(8,128)(2,1)S(1)}) fusion(bf16[64,2,16,128]{3,2,1,0:T(8,128)(2,1)} %all-to-all-done.1), kind=kLoop, calls=%fused_computation.192 | loop fusion | bytes 1048576 | tf_op jit(solution)/shard_map/slice | solution.py:160
  56.2 2.9 %fusion.29 = bf16[128,8,8,128]{3,2,1,0:T(8,128)(2,1)S(1)} fusion(s32[128,128]{1,0:T(8,128)S(1)} %get-tuple-element.35, bf16[128,8,128]{2,1,0:T(8,128)(2,1)S(1)} %copy-done.20, bf16[128,8,128]{2,1,0:T(8,128)(2,1)S(1)} %bitcast.265), kind=kOutput, calls=%fused_computation.32 | convolution fusion | flops 272629760 | bytes 2686976 | tf_op jit(solution)/shard_map/slaj,sbj->slab/dot_general | solution.py:65
  59.2 1.3 fusion.47
  60.7 2.7 %bitcast_multiply_fusion.7 = f32[8,32,1024]{2,1,0:T(8,128)} fusion(f32[1,8,32,1024]{3,2,1,0:T(8,128)S(1)} %copy-done.8, f32[8,8,4,8,128]{4,3,2,1,0:T(8,128)S(1)} %fusion.47, f32[8,32,1024]{2,1,0:T(8,128)} %collective-permute-done.2, f32[]{:T(128)S(6)} %sub.85, f32[1,8,32,1024]{3,2,1,0:T(8,128)S(1)} %copy-done.5), kind=kLoop, calls=%fused_computation.91 | loop fusion | flops 1310720 | bytes 5242884 | tf_op jit(solution)/shard_map/mul | solution.py:187
  63.4 6.1 %collective-permute-start.3 = (f32[8,32,1024]{2,1,0:T(8,128)}, f32[8,32,1024]{2,1,0:T(8,128)}, u32[]{:S(2)}, u32[]{:S(2)}) collective-permute-start(f32[8,32,1024]{2,1,0:T(8,128)} %bitcast_multiply_fusion.7), channel_id=1, source_target_pairs={{64,0},{65,1},{66,2},{67,3},{68,4},{69,5},{70,6},{71,7},{72,8},{73... | collective-permute-start | bytes 3145736 | tf_op jit(solution)/shard_map/ppermute | solution.py:27
  72.7 4.4 %fusion.82 = f32[8,32,1024]{2,1,0:T(8,128)} fusion(f32[1,8,32,1024]{3,2,1,0:T(8,128)} %param.17, f32[1,8,32,1024]{3,2,1,0:T(8,128)} %param.16, f32[1,8,32,1024]{3,2,1,0:T(8,128)S(1)} %copy-done.4, f32[1,8,32,1024]{3,2,1,0:T(8,128)S(1)} %copy-done.5, f32[8,32,1024]{2,1,0:T(8,128)} %collective-permute-done.2, f32[]{:T(128)S(6)} %sub.92, ...), kind=kLoop, calls=%fused_computation.84 | loop fusion | flops 3145728 | bytes 8388616 | tf_op jit(solution)/shard_map/sub | solution.py:204
  77.2 1.4 collective-permute-start.4
  82.2 4.6 %broadcast_select_fusion = (f32[8,32,1024]{2,1,0:T(8,128)S(1)}, f32[8,32,1024]{2,1,0:T(8,128)S(1)}, f32[8,32,1024]{2,1,0:T(8,128)}) fusion(pred[]{:T(512)S(6)} %eq.87, f32[8,32,1024]{2,1,0:T(8,128)} %fusion.82, f32[8,32,1024]{2,1,0:T(8,128)} %collective-permute-done.4, f32[1,8,32,1024]{3,2,1,0:T(8,128)} %param.18, f32[1,8,32,1024]{3,2,1,0:T(8,128)S(1)} %copy-done.4, ...), kind=kLoop, calls=%fused_computation.114 | loop fusion | flops 2621440 | bytes 11534341 | tf_op jit(solution)/shard_map/jit(_where)/select_n | solution.py:176
  88.5 3.0 %multiply_reduce_fusion = bf16[128,8,128]{2,1,0:T(8,128)(2,1)S(1)} fusion(f32[128,8,128]{2,1,0:T(8,128)S(1)} %copy-done.19, s32[128,128]{1,0:T(8,128)S(1)} %get-tuple-element.35, bf16[128,8,8,128]{3,2,0,1:T(8,128)(2,1)S(1)} %bitcast.254), kind=kOutput, calls=%fused_computation.15 | convolution fusion | flops 272498688 | bytes 2949120 | tf_op jit(solution)/shard_map/slab,sbj->slaj/dot_general | solution.py:54
  91.7 2.2 %collective-permute-start.5 = (f32[16,1024]{1,0:T(8,128)S(1)}, f32[16,1024]{1,0:T(8,128)S(1)}, u32[]{:S(2)}, u32[]{:S(2)}) collective-permute-start(f32[16,1024]{1,0:T(8,128)S(1)} %reshape.193), channel_id=1, source_target_pairs={{0,1},{1,2},{2,3},{3,4},{4,5},{5,6},{6,7},{7,8},{8,9},{9,10},{10,1... | collective-permute-start | bytes 196616 | tf_op jit(solution)/shard_map/ppermute | solution.py:17
  94.5 1.5 %collective-permute-start.6 = (f32[16,1024]{1,0:T(8,128)}, f32[16,1024]{1,0:T(8,128)}, u32[]{:S(2)}, u32[]{:S(2)}) collective-permute-start(f32[16,1024]{1,0:T(8,128)} %reshape.195), channel_id=1, source_target_pairs={{1,0},{2,1},{3,2},{4,3},{5,4},{6,5},{7,6},{8,7},{9,8},{10,9},{11,1... | collective-permute-start | bytes 196616 | tf_op jit(solution)/shard_map/ppermute | solution.py:18
  97.0 9.2 %all-to-all-start.2 = ((bf16[64,2,16,128]{3,2,1,0:T(8,128)(2,1)}), bf16[64,2,16,128]{3,2,1,0:T(8,128)(2,1)}, u32[]{:S(2)}, u32[]{:S(2)}) async-start(bf16[64,2,16,128]{3,2,1,0:T(8,128)(2,1)} %copy.58), calls=%async_computation.2 | async-start | bytes 1048576 | tf_op jit(solution)/shard_map/all_to_all | solution.py:159
  107.1 1.6 %maximum_multiply_fusion = f32[8,36,1024]{2,1,0:T(8,128)S(1)} fusion(f32[8,2,1024]{2,1,0:T(2,128)S(1)} %reshape.196, f32[8,32,1024]{2,1,0:T(8,128)S(1)} %copy-done.12, f32[8,2,1024]{2,1,0:T(2,128)S(1)} %reshape.194, f32[2,8,36,1024]{3,2,1,0:T(8,128)} %copy-done.3), kind=kLoop, calls=%fused_computation.53 | loop fusion | flops 884736 | bytes 3538944 | tf_op jit(solution)/shard_map/mul | solution.py:33
  111.1 1.7 %fusion.73 = f32[8,32,1024]{2,1,0:T(8,128)} fusion(f32[8,34,1024]{2,1,0:T(8,128)S(1)} %multiply_multiply_fusion, f32[8,32,1023]{2,1,0:T(8,128)S(1)} %get-tuple-element.11, f32[8,32,1]{2,1,0:T(8,128)S(1)} %get-tuple-element.13, f32[8,32,1]{2,1,0:T(8,128)S(1)} %get-tuple-element.12, f32[8,32,1023]{2,1,0:T(8,128)S(1)} %get-tuple-element.10, ...), kind=kLoop, calls=%fused_computation.70 | loop fusion | flops 2621440 | bytes 7340064 | tf_op jit(solution)/shard_map/mul | solution.py:42
  112.8 2.7 %collective-permute-start.7 = (f32[8,32,1024]{2,1,0:T(8,128)}, f32[8,32,1024]{2,1,0:T(8,128)}, u32[]{:S(2)}, u32[]{:S(2)}) collective-permute-start(f32[8,32,1024]{2,1,0:T(8,128)} %fusion.73), channel_id=1, source_target_pairs={{0,64},{64,0},{1,65},{65,1},{2,66},{66,2},{3,67},{67,3},{4,68},{68... | collective-permute-start | bytes 3145736 | tf_op jit(solution)/shard_map/ppermute | solution.py:183
  115.5 1.5 %all-to-all-done.2 = bf16[64,2,16,128]{3,2,1,0:T(8,128)(2,1)} async-done(((bf16[64,2,16,128]{3,2,1,0:T(8,128)(2,1)}), bf16[64,2,16,128]{3,2,1,0:T(8,128)(2,1)}, u32[]{:S(2)}, u32[]{:S(2)}) %all-to-all-start.2) | async-done | bytes 524320 | tf_op jit(solution)/shard_map/all_to_all | solution.py:159
  118.1 3.8 %fusion.34 = bf16[128,8,8,128]{3,2,1,0:T(8,128)(2,1)S(1)} fusion(s32[128,128]{1,0:T(8,128)S(1)} %copy-done.23, bf16[128,8,128]{2,1,0:T(8,128)(2,1)S(1)} %bitcast.264, bf16[128,8,128]{2,1,0:T(8,128)(2,1)} %get-tuple-element.33), kind=kOutput, calls=%fused_computation.33 | convolution fusion | flops 272629760 | bytes 2686976 | tf_op jit(solution)/shard_map/slaj,sbj->slab/dot_general | solution.py:65
  123.5 1.7 %bitcast_multiply_fusion.5 = f32[8,32,1024]{2,1,0:T(8,128)S(1)} fusion(f32[1,8,32,1024]{3,2,1,0:T(8,128)S(1)} %copy-done.9, f32[8,8,4,8,128]{4,3,2,1,0:T(8,128)S(1)} %fusion.50, f32[8,32,1024]{2,1,0:T(8,128)S(1)} %copy-done.10, f32[8,32,1024]{2,1,0:T(8,128)} %collective-permute-done.7, f32[]{:T(128)S(6)} %sub.85), kind=kLoop, calls=%fused_computation.89 | loop fusion | flops 1310720 | bytes 5242884 | tf_op jit(solution)/shard_map/mul | solution.py:187
  125.2 5.7 %collective-permute-start.8 = (f32[8,32,1024]{2,1,0:T(8,128)S(1)}, f32[8,32,1024]{2,1,0:T(8,128)S(1)}, u32[]{:S(2)}, u32[]{:S(2)}) collective-permute-start(f32[8,32,1024]{2,1,0:T(8,128)S(1)} %bitcast_multiply_fusion.5), channel_id=1, source_target_pairs={{64,0},{65,1},{66,2},{67,3},{68,4},{69,5},{70,6},{71,7},{72,8},{73... | collective-permute-start | bytes 3145736 | tf_op jit(solution)/shard_map/ppermute | solution.py:27
  130.9 2.2 %collective-permute-done.8 = f32[8,32,1024]{2,1,0:T(8,128)S(1)} collective-permute-done((f32[8,32,1024]{2,1,0:T(8,128)S(1)}, f32[8,32,1024]{2,1,0:T(8,128)S(1)}, u32[]{:S(2)}, u32[]{:S(2)}) %collective-permute-start.8) | collective-permute-done | bytes 1048608 | tf_op jit(solution)/shard_map/ppermute | solution.py:27
  133.1 3.3 %fusion.85 = (f32[8,32,1024]{2,1,0:T(8,128)}, f32[1,8,32,1024]{3,2,1,0:T(8,128)}) fusion(f32[8,32,1024]{2,1,0:T(8,128)S(1)} %copy-done.10, f32[1,8,32,1024]{3,2,1,0:T(8,128)S(1)} %copy-done.13, f32[1,8,32,1024]{3,2,1,0:T(8,128)S(1)} %copy-done.14, f32[8,32,1024]{2,1,0:T(8,128)S(1)} %get-tuple-element.4, f32[8,32,1024]{2,1,0:T(8,128)} %collective-permute-done.7, ...), kind=kLoop, calls=%fused_computation.87 | loop fusion | flops 3407872 | bytes 9437192 | tf_op jit(solution)/shard_map/sub | solution.py:204
  138.3 3.4 %fusion.9 = f32[16,1,128]{2,1,0:T(1,128)S(1)} fusion(bf16[16,1024,1]{1,2,0:T(2,128)(2,1)S(1)} %copy.72, bf16[1,16,128,1024]{3,2,1,0:T(8,128)(2,1)} %param.23), kind=kOutput, calls=%fused_computation.7 | convolution fusion | flops 4194304 | bytes 4235264 | tf_op jit(solution)/shard_map/toj,tj->to/dot_general | solution.py:168
  142.4 2.7 %fusion.90 = f32[1,8,32,1024]{3,2,1,0:T(8,128)} fusion(f32[8,32,1024]{2,1,0:T(8,128)S(1)} %get-tuple-element.4, f32[8,32,1024]{2,1,0:T(8,128)} %get-tuple-element.6, f32[8,32,1024]{2,1,0:T(8,128)S(1)} %collective-permute-done.9, f32[1,8,32,1024]{3,2,1,0:T(8,128)S(1)} %copy-done.9), kind=kLoop, calls=%fused_computation.96 | loop fusion | flops 786432 | bytes 5242880 | tf_op jit(solution)/shard_map/broadcast_in_dim | solution.py:209
  (144 shorter events, 34.8 us)
Async XLA Ops:
  0.6 9.3 %copy-start = (s32[1,16,128]{2,1,0:T(8,128)S(1)}, s32[1,16,128]{2,1,0:T(8,128)}, u32[]{:S(2)}) copy-start(s32[1,16,128]{2,1,0:T(8,128)} %param.22) | copy-start | bytes 24580
  2.2 7.5 %copy-start.35 = (s32[1,16]{1,0:T(1,128)S(1)}, s32[1,16]{1,0:T(1,128)}, u32[]{:S(2)}) copy-start(s32[1,16]{1,0:T(1,128)} %param.21) | copy-start | bytes 196
  2.2 20.6 %copy-start.21 = (bf16[1,16,128]{2,1,0:T(8,128)(2,1)S(1)}, bf16[1,16,128]{2,1,0:T(8,128)(2,1)}, u32[]{:S(2)}) copy-start(bf16[1,16,128]{2,1,0:T(8,128)(2,1)} %param.15) | copy-start | bytes 12292
  3.0 40.5 %collective-permute-start = (f32[32,1024]{1,0:T(8,128)}, f32[32,1024]{1,0:T(8,128)}, u32[]{:S(2)}, u32[]{:S(2)}) collective-permute-start(f32[32,1024]{1,0:T(8,128)} %reshape.184), channel_id=1, source_target_pairs={{0,1},{1,2},{2,3},{3,4},{4,5},{5,6},{6,7},{7,8},{8,9},{9,10},{10,1... | collective-permute-start | bytes 393224 | tf_op jit(solution)/shard_map/ppermute | solution.py:17
  8.4 36.1 %collective-permute-start.1 = (f32[32,1024]{1,0:T(8,128)}, f32[32,1024]{1,0:T(8,128)}, u32[]{:S(2)}, u32[]{:S(2)}) collective-permute-start(f32[32,1024]{1,0:T(8,128)} %reshape.186), channel_id=1, source_target_pairs={{1,0},{2,1},{3,2},{4,3},{5,4},{6,5},{7,6},{8,7},{9,8},{10,9},{11,1... | collective-permute-start | bytes 393224 | tf_op jit(solution)/shard_map/ppermute | solution.py:18
  11.2 20.0 %all-to-all-start = ((s32[64,2,128]{2,1,0:T(2,128)}), s32[64,2,128]{2,1,0:T(2,128)S(1)}, u32[]{:S(2)}, u32[]{:S(2)}) async-start(s32[64,2,128]{2,1,0:T(2,128)} %bitcast.9), calls=%async_computation | async-start | bytes 131072 | tf_op jit(solution)/shard_map/all_to_all | solution.py:120
  22.8 46.7 %copy-start.32 = (s32[16]{0:T(128)}, s32[16]{0:T(128)S(1)}, u32[]{:S(2)}) copy-start(s32[16]{0:T(128)S(1)} %multiply_add_fusion) | copy-start | bytes 196
  25.7 5.8 %copy-start.4 = (f32[1,8,32,1024]{3,2,1,0:T(8,128)S(1)}, f32[1,8,32,1024]{3,2,1,0:T(8,128)}, u32[]{:S(2)}) copy-start(f32[1,8,32,1024]{3,2,1,0:T(8,128)} %param.13) | copy-start | bytes 3145732
  31.3 56.8 %copy-start.22 = (s32[128,128]{1,0:T(8,128)}, s32[128,128]{1,0:T(8,128)S(1)}, u32[]{:S(2)}) copy-start(s32[128,128]{1,0:T(8,128)S(1)} %get-tuple-element.35) | copy-start | bytes 196612
  31.4 27.7 %copy-start.27 = (s32[128]{0:T(128)}, s32[128]{0:T(128)S(1)}, u32[]{:S(2)}) copy-start(s32[128]{0:T(128)S(1)} %fusion.106) | copy-start | bytes 1540
  37.6 16.9 %all-to-all-start.1 = ((bf16[64,2,16,128]{3,2,1,0:T(8,128)(2,1)}), bf16[64,2,16,128]{3,2,1,0:T(8,128)(2,1)}, u32[]{:S(2)}, u32[]{:S(2)}) async-start(bf16[64,2,16,128]{3,2,1,0:T(8,128)(2,1)} %copy.49), calls=%async_computation.1 | async-start | bytes 1048576 | tf_op jit(solution)/shard_map/all_to_all | solution.py:159
  49.6 6.6 %copy-start.20 = (bf16[128,8,128]{2,1,0:T(8,128)(2,1)S(1)}, bf16[128,8,128]{2,1,0:T(8,128)(2,1)}, u32[]{:S(2)}) copy-start(bf16[128,8,128]{2,1,0:T(8,128)(2,1)} %get-tuple-element.33) | copy-start | bytes 786436
  51.3 9.2 %collective-permute-start.2 = (f32[8,32,1024]{2,1,0:T(8,128)}, f32[8,32,1024]{2,1,0:T(8,128)}, u32[]{:S(2)}, u32[]{:S(2)}) collective-permute-start(f32[8,32,1024]{2,1,0:T(8,128)} %fusion.79), channel_id=1, source_target_pairs={{0,64},{64,0},{1,65},{65,1},{2,66},{66,2},{3,67},{67,3},{4,68},{68... | collective-permute-start | bytes 3145736 | tf_op jit(solution)/shard_map/ppermute | solution.py:183
  63.4 9.3 %collective-permute-start.3 = (f32[8,32,1024]{2,1,0:T(8,128)}, f32[8,32,1024]{2,1,0:T(8,128)}, u32[]{:S(2)}, u32[]{:S(2)}) collective-permute-start(f32[8,32,1024]{2,1,0:T(8,128)} %bitcast_multiply_fusion.7), channel_id=1, source_target_pairs={{64,0},{65,1},{66,2},{67,3},{68,4},{69,5},{70,6},{71,7},{72,8},{73... | collective-permute-start | bytes 3145736 | tf_op jit(solution)/shard_map/ppermute | solution.py:27
  72.7 5.9 %copy-start.2 = (bf16[1,16,128,1024]{3,2,1,0:T(8,128)(2,1)S(1)}, bf16[1,16,128,1024]{3,2,1,0:T(8,128)(2,1)}, u32[]{:S(2)}) copy-start(bf16[1,16,128,1024]{3,2,1,0:T(8,128)(2,1)} %param.23) | copy-start | bytes 12582916
  77.2 5.0 %collective-permute-start.4 = (f32[8,32,1024]{2,1,0:T(8,128)}, f32[8,32,1024]{2,1,0:T(8,128)}, u32[]{:S(2)}, u32[]{:S(2)}) collective-permute-start(f32[8,32,1024]{2,1,0:T(8,128)} %fusion.82), channel_id=1, source_target_pairs={{0,64},{1,65},{2,66},{3,67},{4,68},{5,69},{6,70},{7,71},{8,72},{9,... | collective-permute-start | bytes 3145736 | tf_op jit(solution)/shard_map/ppermute | solution.py:27
  81.9 4.8 %copy-start.28 = (s32[128]{0:T(128)S(1)}, s32[128]{0:T(128)}, u32[]{:S(2)}) copy-start(s32[128]{0:T(128)} %copy-done.27) | copy-start | bytes 1540
  86.7 4.8 %copy-start.11 = (f32[8,32,1024]{2,1,0:T(8,128)}, f32[8,32,1024]{2,1,0:T(8,128)S(1)}, u32[]{:S(2)}) copy-start(f32[8,32,1024]{2,1,0:T(8,128)S(1)} %get-tuple-element.3) | copy-start | bytes 3145732
  88.5 7.5 %copy-start.16 = (bf16[128,8,128]{2,1,0:T(8,128)(2,1)S(1)}, bf16[128,8,128]{2,1,0:T(8,128)(2,1)}, u32[]{:S(2)}) copy-start(bf16[128,8,128]{2,1,0:T(8,128)(2,1)} %copy.57) | copy-start | bytes 786436
  91.7 14.5 %collective-permute-start.5 = (f32[16,1024]{1,0:T(8,128)S(1)}, f32[16,1024]{1,0:T(8,128)S(1)}, u32[]{:S(2)}, u32[]{:S(2)}) collective-permute-start(f32[16,1024]{1,0:T(8,128)S(1)} %reshape.193), channel_id=1, source_target_pairs={{0,1},{1,2},{2,3},{3,4},{4,5},{5,6},{6,7},{7,8},{8,9},{9,10},{10,1... | collective-permute-start | bytes 196616 | tf_op jit(solution)/shard_map/ppermute | solution.py:17
  94.5 11.7 %collective-permute-start.6 = (f32[16,1024]{1,0:T(8,128)}, f32[16,1024]{1,0:T(8,128)}, u32[]{:S(2)}, u32[]{:S(2)}) collective-permute-start(f32[16,1024]{1,0:T(8,128)} %reshape.195), channel_id=1, source_target_pairs={{1,0},{2,1},{3,2},{4,3},{5,4},{6,5},{7,6},{8,7},{9,8},{10,9},{11,1... | collective-permute-start | bytes 196616 | tf_op jit(solution)/shard_map/ppermute | solution.py:18
  96.1 11.0 %copy-start.12 = (f32[8,32,1024]{2,1,0:T(8,128)S(1)}, f32[8,32,1024]{2,1,0:T(8,128)}, u32[]{:S(2)}) copy-start(f32[8,32,1024]{2,1,0:T(8,128)} %copy-done.11) | copy-start | bytes 3145732
  97.0 20.0 %all-to-all-start.2 = ((bf16[64,2,16,128]{3,2,1,0:T(8,128)(2,1)}), bf16[64,2,16,128]{3,2,1,0:T(8,128)(2,1)}, u32[]{:S(2)}, u32[]{:S(2)}) async-start(bf16[64,2,16,128]{3,2,1,0:T(8,128)(2,1)} %copy.58), calls=%async_computation.2 | async-start | bytes 1048576 | tf_op jit(solution)/shard_map/all_to_all | solution.py:159
  111.1 7.0 %copy-start.23 = (s32[128,128]{1,0:T(8,128)S(1)}, s32[128,128]{1,0:T(8,128)}, u32[]{:S(2)}) copy-start(s32[128,128]{1,0:T(8,128)} %copy-done.22) | copy-start | bytes 196612
  112.8 10.5 %collective-permute-start.7 = (f32[8,32,1024]{2,1,0:T(8,128)}, f32[8,32,1024]{2,1,0:T(8,128)}, u32[]{:S(2)}, u32[]{:S(2)}) collective-permute-start(f32[8,32,1024]{2,1,0:T(8,128)} %fusion.73), channel_id=1, source_target_pairs={{0,64},{64,0},{1,65},{65,1},{2,66},{66,2},{3,67},{67,3},{4,68},{68... | collective-permute-start | bytes 3145736 | tf_op jit(solution)/shard_map/ppermute | solution.py:183
  118.1 3.8 %copy-start.29 = (s32[128]{0:T(128)S(1)}, s32[128]{0:T(128)}, u32[]{:S(2)}) copy-start(s32[128]{0:T(128)} %copy-done.27) | copy-start | bytes 1540
  123.5 9.6 %copy-start.13 = (f32[1,8,32,1024]{3,2,1,0:T(8,128)S(1)}, f32[1,8,32,1024]{3,2,1,0:T(8,128)}, u32[]{:S(2)}) copy-start(f32[1,8,32,1024]{3,2,1,0:T(8,128)} %param.17) | copy-start | bytes 3145732
  123.5 9.6 %copy-start.14 = (f32[1,8,32,1024]{3,2,1,0:T(8,128)S(1)}, f32[1,8,32,1024]{3,2,1,0:T(8,128)}, u32[]{:S(2)}) copy-start(f32[1,8,32,1024]{3,2,1,0:T(8,128)} %param.16) | copy-start | bytes 3145732
  125.2 12.5 %copy-start.34 = (s32[16]{0:T(128)S(1)}, s32[16]{0:T(128)}, u32[]{:S(2)}) copy-start(s32[16]{0:T(128)} %copy-done.32) | copy-start | bytes 196
  125.2 7.9 %collective-permute-start.8 = (f32[8,32,1024]{2,1,0:T(8,128)S(1)}, f32[8,32,1024]{2,1,0:T(8,128)S(1)}, u32[]{:S(2)}, u32[]{:S(2)}) collective-permute-start(f32[8,32,1024]{2,1,0:T(8,128)S(1)} %bitcast_multiply_fusion.5), channel_id=1, source_target_pairs={{64,0},{65,1},{66,2},{67,3},{68,4},{69,5},{70,6},{71,7},{72,8},{73... | collective-permute-start | bytes 3145736 | tf_op jit(solution)/shard_map/ppermute | solution.py:27
  136.4 5.9 %collective-permute-start.9 = (f32[8,32,1024]{2,1,0:T(8,128)}, f32[8,32,1024]{2,1,0:T(8,128)S(1)}, u32[]{:S(2)}, u32[]{:S(2)}) collective-permute-start(f32[8,32,1024]{2,1,0:T(8,128)} %get-tuple-element.6), channel_id=1, source_target_pairs={{0,64},{1,65},{2,66},{3,67},{4,68},{5,69},{6,70},{7,71},{8,72},{9,... | collective-permute-start | bytes 3145736 | tf_op jit(solution)/shard_map/ppermute | solution.py:27
  138.3 3.4 %copy-start.26 = (bf16[1,16,128]{2,1,0:T(8,128)(2,1)S(1)}, bf16[1,16,128]{2,1,0:T(8,128)(2,1)}, u32[]{:S(2)}) copy-start(bf16[1,16,128]{2,1,0:T(8,128)(2,1)} %param.24) | copy-start | bytes 12292
  (17 other events, 30.5 us)

commit v4 on v0

--- a/solution.py
+++ b/solution.py
@@ -151,16 +151,16 @@
             tile_grad.reshape(tiles_here, touched, levels),
             preferred_element_type=jnp.float32,
         ).astype(jnp.bfloat16)
-        both = jnp.stack(
+        both = jnp.concatenate(
             [
                 wanted.reshape(owners_count, capacity * levels, touched),
                 sent_grad.reshape(owners_count, capacity * levels, touched),
             ],
-            axis=1,
+            axis=2,
         )
         got = lax.all_to_all(both, "space", split_axis=0, concat_axis=0, tiled=True)
-        got_cols = got[:, 0].reshape(slots_all, touch_levels)
-        got_grad = got[:, 1].reshape(slots_all, touch_levels)
+        got_cols = got[:, :, :touched].reshape(slots_all, touch_levels)
+        got_grad = got[:, :, touched:].reshape(slots_all, touch_levels)
         own_cols = jnp.einsum(
             "ts,slj->tjl",
             slot_oh,

time: 145 us -> 145 us (level)
  other arithmetic: 32.3 us -> 34 us
  local copies, waits for them, and re-layouts: 16.3 us -> 14.6 us
    concatenate x0 -> x2, other arithmetic: none -> 1.72 us  [on_device(): jnp.concatenate([wanted.reshape(owners_count, capacity * levels, touched)...]
    another operation x2 -> x0, local copies, waits for them, and re-layouts: 1.68 us -> none  [on_device(): jnp.stack([wanted.reshape(owners_count, capacity * levels, touched), sent...]
where the time goes in v4:
time: 145 us; the launch traced here: 144 us
  starting transfers between devices  55.7 us (38%)
  other arithmetic  34 us (23%)
  matrix products  27 us (19%)
  local copies, waits for them, and re-layouts  14.6 us (10%)
  waiting for transfers between devices  11.5 us (8%)
    all_to_all x2, starting transfers between devices, on_device(): got = lax.all_to_all(both, 'space', split_axis=0, concat_axis=0, tiled=True)  14.7 us
    ppermute x4, starting transfers between devices, shifted(): return lax.ppermute(value, axis, pairs)  14.4 us
    all_to_all x1, starting transfers between devices, on_device(): lax.all_to_all(packed_cells.reshape(owners_count, capacity, touched), 'sp...  11.5 us
    sub x2, other arithmetic, on_device(): source = r_model - err_field * upward  7.76 us
    ppermute x2, starting transfers between devices, with_halo(): lax.ppermute(tail, axis, [(i, i + 1) for i in range(ends)])  7.56 us
    dot_general x2, matrix products, spread_cols(): jnp.einsum('slaj,sbj->slab', placed, col_oh, preferred_element_type=jnp.f...  6.72 us
    select_n x2, other arithmetic, on_device(): chosen = jnp.where(tm_here == 0, increment, dual_model)  6.02 us
    dot_general x2, matrix products, gather_cols(): jnp.einsum('slab,sbj->slaj', lines, col_oh, preferred_element_type=jnp.fl...  6.02 us
  transfers between devices with their start and end apart: 13, of which 5 were waited for; matrix products, arithmetic and copies ran while one was open for 32% of the time, Pallas kernels for 0%

profile of v4, /device:TPU:1, one launch (start us, length us, event | category | flops | bytes accessed | tf_op | source)
XLA Modules:
  0.0 144.1 jit_solution(2904528657954048668)
XLA Ops:
  0.7 1.5 %broadcast_select_fusion.1 = f32[1,8,32,1024]{3,2,1,0:T(8,128)S(1)} fusion(f32[1,8,32,1024]{3,2,1,0:T(8,128)} %param.13, f32[1,8,32,1024]{3,2,1,0:T(8,128)} %param.14, pred[]{:T(512)S(6)} %eq.87), kind=kLoop, calls=%fused_computation.115 | loop fusion | flops 262144 | bytes 3145729 | tf_op jit(solution)/shard_map/jit(_where)/select_n | solution.py:178
  3.0 4.6 %collective-permute-start = (f32[2,8,2,1024]{3,2,1,0:T(2,128)}, f32[2,8,2,1024]{3,2,1,0:T(2,128)}, u32[]{:S(2)}, u32[]{:S(2)}) collective-permute-start(f32[2,8,2,1024]{3,2,1,0:T(2,128)} %get-tuple-element.8), channel_id=1, source_target_pairs={{0,1},{1,2},{2,3},{3,4},{4,5},{5,6},{6,7},{7,8},{8,9},{9,10},{10,1... | collective-permute-start | bytes 393224 | tf_op jit(solution)/shard_map/ppermute | solution.py:18
  10.5 11.5 %all-to-all-start = ((s32[64,2,128]{2,1,0:T(2,128)}), s32[64,2,128]{2,1,0:T(2,128)S(1)}, u32[]{:S(2)}, u32[]{:S(2)}) async-start(s32[64,2,128]{2,1,0:T(2,128)} %bitcast.9), calls=%async_computation | async-start | bytes 131072 | tf_op jit(solution)/shard_map/all_to_all | solution.py:122
  22.0 2.8 %fusion.15 = bf16[16,1,1024]{2,1,0:T(2,128)(2,1)S(1)} fusion(bf16[1,16,128,1024]{3,2,1,0:T(8,128)(2,1)} %param.23, bf16[16,128,1]{1,0,2:T(8,128)(2,1)S(1)} %bitcast.265), kind=kOutput, calls=%fused_computation.13 | convolution fusion | flops 4194304 | bytes 4231168 | tf_op jit(solution)/shard_map/toj,to->tj/dot_general | solution.py:145
  26.3 4.1 %all-to-all-done = s32[64,2,128]{2,1,0:T(2,128)S(1)} async-done(((s32[64,2,128]{2,1,0:T(2,128)}), s32[64,2,128]{2,1,0:T(2,128)S(1)}, u32[]{:S(2)}, u32[]{:S(2)}) %all-to-all-start) | async-done | bytes 65568 | tf_op jit(solution)/shard_map/all_to_all | solution.py:122
  32.8 3.0 %multiply_reduce_fusion.1 = bf16[128,8,128]{2,1,0:T(8,128)(2,1)S(1)} fusion(f32[128,8,128]{2,1,0:T(8,128)S(1)} %get-tuple-element.32, s32[128,128]{1,0:T(8,128)S(1)} %get-tuple-element.35, bf16[128,8,8,128]{3,2,0,1:T(8,128)(2,1)S(1)} %bitcast.249), kind=kOutput, calls=%fused_computation.16 | convolution fusion | flops 272498688 | bytes 2949120 | tf_op jit(solution)/shard_map/slab,sbj->slaj/dot_general | solution.py:56
  36.7 5.9 %all-to-all-start.1 = ((bf16[64,16,256]{2,1,0:T(8,128)(2,1)}), bf16[64,16,256]{2,1,0:T(8,128)(2,1)}, u32[]{:S(2)}, u32[]{:S(2)}) async-start(bf16[64,16,256]{2,1,0:T(8,128)(2,1)} %pad_maximum_fusion.1), calls=%async_computation.1 | async-start | bytes 1048576 | tf_op jit(solution)/shard_map/all_to_all | solution.py:161
  42.7 1.4 pad_maximum_fusion
  47.8 1.7 %fusion.79 = f32[8,32,1024]{2,1,0:T(8,128)} fusion(f32[8,34,1024]{2,1,0:T(8,128)S(1)} %multiply_multiply_fusion.1, f32[8,32,1023]{2,1,0:T(8,128)S(1)} %get-tuple-element.19, f32[8,32,1]{2,1,0:T(8,128)S(1)} %get-tuple-element.21, f32[8,32,1]{2,1,0:T(8,128)S(1)} %get-tuple-element.20, f32[8,32,1023]{2,1,0:T(8,128)S(1)} %get-tuple-element.18, ...), kind=kLoop, calls=%fused_computation.77 | loop fusion | flops 2621440 | bytes 7340064 | tf_op jit(solution)/shard_map/mul | solution.py:44
  49.5 2.2 %collective-permute-start.2 = (f32[8,32,1024]{2,1,0:T(8,128)}, f32[8,32,1024]{2,1,0:T(8,128)}, u32[]{:S(2)}, u32[]{:S(2)}) collective-permute-start(f32[8,32,1024]{2,1,0:T(8,128)} %fusion.79), channel_id=1, source_target_pairs={{0,64},{64,0},{1,65},{65,1},{2,66},{66,2},{3,67},{67,3},{4,68},{68... | collective-permute-start | bytes 3145736 | tf_op jit(solution)/shard_map/ppermute | solution.py:185
  51.7 1.9 %all-to-all-done.1 = bf16[64,16,256]{2,1,0:T(8,128)(2,1)} async-done(((bf16[64,16,256]{2,1,0:T(8,128)(2,1)}), bf16[64,16,256]{2,1,0:T(8,128)(2,1)}, u32[]{:S(2)}, u32[]{:S(2)}) %all-to-all-start.1) | async-done | bytes 524320 | tf_op jit(solution)/shard_map/all_to_all | solution.py:161
  53.6 1.8 %fusion.153 = (bf16[64,16,128]{2,1,0:T(8,128)(2,1)}, bf16[64,16,128]{2,1,0:T(8,128)(2,1)S(1)}) fusion(bf16[64,16,256]{2,1,0:T(8,128)(2,1)} %all-to-all-done.1), kind=kLoop, calls=%fused_computation.192 | loop fusion | bytes 1048576 | tf_op jit(solution)/shard_map/slice | solution.py:162
  55.4 2.9 %fusion.29 = bf16[128,8,8,128]{3,2,1,0:T(8,128)(2,1)S(1)} fusion(s32[128,128]{1,0:T(8,128)S(1)} %get-tuple-element.35, bf16[128,8,128]{2,1,0:T(8,128)(2,1)S(1)} %copy-done.19, bf16[128,8,128]{2,1,0:T(8,128)(2,1)S(1)} %bitcast.261), kind=kOutput, calls=%fused_computation.32 | convolution fusion | flops 272629760 | bytes 2686976 | tf_op jit(solution)/shard_map/slaj,sbj->slab/dot_general | solution.py:67
  59.9 2.7 %bitcast_multiply_fusion.7 = f32[8,32,1024]{2,1,0:T(8,128)} fusion(f32[1,8,32,1024]{3,2,1,0:T(8,128)S(1)} %copy-done.8, f32[8,8,4,8,128]{4,3,2,1,0:T(8,128)S(1)} %fusion.47, f32[8,32,1024]{2,1,0:T(8,128)} %collective-permute-done.2, f32[]{:T(128)S(6)} %sub.85, f32[1,8,32,1024]{3,2,1,0:T(8,128)S(1)} %copy-done.5), kind=kLoop, calls=%fused_computation.91 | loop fusion | flops 1310720 | bytes 5242884 | tf_op jit(solution)/shard_map/mul | solution.py:189
  62.6 6.1 %collective-permute-start.3 = (f32[8,32,1024]{2,1,0:T(8,128)}, f32[8,32,1024]{2,1,0:T(8,128)}, u32[]{:S(2)}, u32[]{:S(2)}) collective-permute-start(f32[8,32,1024]{2,1,0:T(8,128)} %bitcast_multiply_fusion.7), channel_id=1, source_target_pairs={{64,0},{65,1},{66,2},{67,3},{68,4},{69,5},{70,6},{71,7},{72,8},{73... | collective-permute-start | bytes 3145736 | tf_op jit(solution)/shard_map/ppermute | solution.py:29
  71.9 4.4 %fusion.82 = f32[8,32,1024]{2,1,0:T(8,128)} fusion(f32[1,8,32,1024]{3,2,1,0:T(8,128)} %param.17, f32[1,8,32,1024]{3,2,1,0:T(8,128)} %param.16, f32[1,8,32,1024]{3,2,1,0:T(8,128)S(1)} %copy-done.4, f32[1,8,32,1024]{3,2,1,0:T(8,128)S(1)} %copy-done.5, f32[8,32,1024]{2,1,0:T(8,128)} %collective-permute-done.2, f32[]{:T(128)S(6)} %sub.92, ...), kind=kLoop, calls=%fused_computation.84 | loop fusion | flops 3145728 | bytes 8388616 | tf_op jit(solution)/shard_map/sub | solution.py:206
  76.3 1.4 collective-permute-start.4
  81.3 4.6 %broadcast_select_fusion = (f32[8,32,1024]{2,1,0:T(8,128)S(1)}, f32[8,32,1024]{2,1,0:T(8,128)S(1)}, f32[8,32,1024]{2,1,0:T(8,128)}) fusion(pred[]{:T(512)S(6)} %eq.87, f32[8,32,1024]{2,1,0:T(8,128)} %fusion.82, f32[8,32,1024]{2,1,0:T(8,128)} %collective-permute-done.4, f32[1,8,32,1024]{3,2,1,0:T(8,128)} %param.18, f32[1,8,32,1024]{3,2,1,0:T(8,128)S(1)} %copy-done.4, ...), kind=kLoop, calls=%fused_computation.114 | loop fusion | flops 2621440 | bytes 11534341 | tf_op jit(solution)/shard_map/jit(_where)/select_n | solution.py:178
  87.7 3.0 %multiply_reduce_fusion = bf16[128,8,128]{2,1,0:T(8,128)(2,1)S(1)} fusion(f32[128,8,128]{2,1,0:T(8,128)S(1)} %copy-done.18, s32[128,128]{1,0:T(8,128)S(1)} %get-tuple-element.35, bf16[128,8,8,128]{3,2,0,1:T(8,128)(2,1)S(1)} %bitcast.250), kind=kOutput, calls=%fused_computation.15 | convolution fusion | flops 272498688 | bytes 2949120 | tf_op jit(solution)/shard_map/slab,sbj->slaj/dot_general | solution.py:56
  91.4 2.9 %collective-permute-start.5 = (f32[8,2,1024]{2,1,0:T(2,128)}, f32[8,2,1024]{2,1,0:T(2,128)}, u32[]{:S(2)}, u32[]{:S(2)}) collective-permute-start(f32[8,2,1024]{2,1,0:T(2,128)} %get-tuple-element.26), channel_id=1, source_target_pairs={{0,1},{1,2},{2,3},{3,4},{4,5},{5,6},{6,7},{7,8},{8,9},{9,10},{10,1... | collective-permute-start | bytes 196616 | tf_op jit(solution)/shard_map/ppermute | solution.py:18
  96.5 8.8 %all-to-all-start.2 = ((bf16[64,16,256]{2,1,0:T(8,128)(2,1)}), bf16[64,16,256]{2,1,0:T(8,128)(2,1)}, u32[]{:S(2)}, u32[]{:S(2)}) async-start(bf16[64,16,256]{2,1,0:T(8,128)(2,1)} %pad_maximum_fusion.2), calls=%async_computation.2 | async-start | bytes 1048576 | tf_op jit(solution)/shard_map/all_to_all | solution.py:161
  105.3 1.7 %maximum_multiply_fusion = f32[8,36,1024]{2,1,0:T(8,128)S(1)} fusion(f32[8,2,1024]{2,1,0:T(2,128)} %collective-permute-done.6, f32[8,32,1024]{2,1,0:T(8,128)S(1)} %copy-done.12, f32[8,2,1024]{2,1,0:T(2,128)} %collective-permute-done.5, f32[2,8,36,1024]{3,2,1,0:T(8,128)} %copy-done.3), kind=kLoop, calls=%fused_computation.53 | loop fusion | flops 884736 | bytes 3538944 | tf_op jit(solution)/shard_map/mul | solution.py:35
  109.4 1.7 %fusion.73 = f32[8,32,1024]{2,1,0:T(8,128)} fusion(f32[8,34,1024]{2,1,0:T(8,128)S(1)} %multiply_multiply_fusion, f32[8,32,1023]{2,1,0:T(8,128)S(1)} %get-tuple-element.11, f32[8,32,1]{2,1,0:T(8,128)S(1)} %get-tuple-element.13, f32[8,32,1]{2,1,0:T(8,128)S(1)} %get-tuple-element.12, f32[8,32,1023]{2,1,0:T(8,128)S(1)} %get-tuple-element.10, ...), kind=kLoop, calls=%fused_computation.70 | loop fusion | flops 2621440 | bytes 7340064 | tf_op jit(solution)/shard_map/mul | solution.py:44
  111.0 2.7 %collective-permute-start.7 = (f32[8,32,1024]{2,1,0:T(8,128)}, f32[8,32,1024]{2,1,0:T(8,128)}, u32[]{:S(2)}, u32[]{:S(2)}) collective-permute-start(f32[8,32,1024]{2,1,0:T(8,128)} %fusion.73), channel_id=1, source_target_pairs={{0,64},{64,0},{1,65},{65,1},{2,66},{66,2},{3,67},{67,3},{4,68},{68... | collective-permute-start | bytes 3145736 | tf_op jit(solution)/shard_map/ppermute | solution.py:185
  113.7 2.4 %all-to-all-done.2 = bf16[64,16,256]{2,1,0:T(8,128)(2,1)} async-done(((bf16[64,16,256]{2,1,0:T(8,128)(2,1)}), bf16[64,16,256]{2,1,0:T(8,128)(2,1)}, u32[]{:S(2)}, u32[]{:S(2)}) %all-to-all-start.2) | async-done | bytes 524320 | tf_op jit(solution)/shard_map/all_to_all | solution.py:161
  117.2 3.8 %fusion.34 = bf16[128,8,8,128]{3,2,1,0:T(8,128)(2,1)S(1)} fusion(s32[128,128]{1,0:T(8,128)S(1)} %get-tuple-element.35, bf16[128,8,128]{2,1,0:T(8,128)(2,1)S(1)} %bitcast.260, bf16[128,8,128]{2,1,0:T(8,128)(2,1)} %get-tuple-element.33), kind=kOutput, calls=%fused_computation.33 | convolution fusion | flops 272629760 | bytes 2686976 | tf_op jit(solution)/shard_map/slaj,sbj->slab/dot_general | solution.py:67
  122.6 1.7 %bitcast_multiply_fusion.5 = f32[8,32,1024]{2,1,0:T(8,128)S(1)} fusion(f32[1,8,32,1024]{3,2,1,0:T(8,128)S(1)} %copy-done.9, f32[8,8,4,8,128]{4,3,2,1,0:T(8,128)S(1)} %fusion.50, f32[8,32,1024]{2,1,0:T(8,128)S(1)} %copy-done.10, f32[8,32,1024]{2,1,0:T(8,128)} %collective-permute-done.7, f32[]{:T(128)S(6)} %sub.85), kind=kLoop, calls=%fused_computation.89 | loop fusion | flops 1310720 | bytes 5242884 | tf_op jit(solution)/shard_map/mul | solution.py:189
  124.3 5.7 %collective-permute-start.8 = (f32[8,32,1024]{2,1,0:T(8,128)S(1)}, f32[8,32,1024]{2,1,0:T(8,128)S(1)}, u32[]{:S(2)}, u32[]{:S(2)}) collective-permute-start(f32[8,32,1024]{2,1,0:T(8,128)S(1)} %bitcast_multiply_fusion.5), channel_id=1, source_target_pairs={{64,0},{65,1},{66,2},{67,3},{68,4},{69,5},{70,6},{71,7},{72,8},{73... | collective-permute-start | bytes 3145736 | tf_op jit(solution)/shard_map/ppermute | solution.py:29
  130.0 2.2 %collective-permute-done.8 = f32[8,32,1024]{2,1,0:T(8,128)S(1)} collective-permute-done((f32[8,32,1024]{2,1,0:T(8,128)S(1)}, f32[8,32,1024]{2,1,0:T(8,128)S(1)}, u32[]{:S(2)}, u32[]{:S(2)}) %collective-permute-start.8) | collective-permute-done | bytes 1048608 | tf_op jit(solution)/shard_map/ppermute | solution.py:29
  132.2 3.3 %fusion.85 = (f32[8,32,1024]{2,1,0:T(8,128)}, f32[1,8,32,1024]{3,2,1,0:T(8,128)}) fusion(f32[8,32,1024]{2,1,0:T(8,128)S(1)} %copy-done.10, f32[1,8,32,1024]{3,2,1,0:T(8,128)S(1)} %copy-done.13, f32[1,8,32,1024]{3,2,1,0:T(8,128)S(1)} %copy-done.14, f32[8,32,1024]{2,1,0:T(8,128)S(1)} %get-tuple-element.4, f32[8,32,1024]{2,1,0:T(8,128)} %collective-permute-done.7, ...), kind=kLoop, calls=%fused_computation.87 | loop fusion | flops 3407872 | bytes 9437192 | tf_op jit(solution)/shard_map/sub | solution.py:206
  137.4 3.4 %fusion.9 = f32[16,1,128]{2,1,0:T(1,128)S(1)} fusion(bf16[16,1024,1]{1,2,0:T(2,128)(2,1)S(1)} %copy.54, bf16[1,16,128,1024]{3,2,1,0:T(8,128)(2,1)} %param.23), kind=kOutput, calls=%fused_computation.7 | convolution fusion | flops 4194304 | bytes 4235264 | tf_op jit(solution)/shard_map/toj,tj->to/dot_general | solution.py:170
  141.5 2.7 %fusion.90 = f32[1,8,32,1024]{3,2,1,0:T(8,128)} fusion(f32[8,32,1024]{2,1,0:T(8,128)S(1)} %get-tuple-element.4, f32[8,32,1024]{2,1,0:T(8,128)} %get-tuple-element.6, f32[8,32,1024]{2,1,0:T(8,128)S(1)} %collective-permute-done.9, f32[1,8,32,1024]{3,2,1,0:T(8,128)S(1)} %copy-done.9), kind=kLoop, calls=%fused_computation.96 | loop fusion | flops 786432 | bytes 5242880 | tf_op jit(solution)/shard_map/broadcast_in_dim | solution.py:211
  (128 shorter events, 32.3 us)
Async XLA Ops:
  0.6 8.6 %copy-start = (s32[1,16,128]{2,1,0:T(8,128)S(1)}, s32[1,16,128]{2,1,0:T(8,128)}, u32[]{:S(2)}) copy-start(s32[1,16,128]{2,1,0:T(8,128)} %param.22) | copy-start | bytes 24580
  2.1 6.8 %copy-start.32 = (s32[1,16]{1,0:T(1,128)S(1)}, s32[1,16]{1,0:T(1,128)}, u32[]{:S(2)}) copy-start(s32[1,16]{1,0:T(1,128)} %param.21) | copy-start | bytes 196
  2.1 19.9 %copy-start.20 = (bf16[1,16,128]{2,1,0:T(8,128)(2,1)S(1)}, bf16[1,16,128]{2,1,0:T(8,128)(2,1)}, u32[]{:S(2)}) copy-start(bf16[1,16,128]{2,1,0:T(8,128)(2,1)} %param.15) | copy-start | bytes 12292
  3.0 39.6 %collective-permute-start = (f32[2,8,2,1024]{3,2,1,0:T(2,128)}, f32[2,8,2,1024]{3,2,1,0:T(2,128)}, u32[]{:S(2)}, u32[]{:S(2)}) collective-permute-start(f32[2,8,2,1024]{3,2,1,0:T(2,128)} %get-tuple-element.8), channel_id=1, source_target_pairs={{0,1},{1,2},{2,3},{3,4},{4,5},{5,6},{6,7},{7,8},{8,9},{9,10},{10,1... | collective-permute-start | bytes 393224 | tf_op jit(solution)/shard_map/ppermute | solution.py:18
  7.6 35.0 %collective-permute-start.1 = (f32[2,8,2,1024]{3,2,1,0:T(2,128)}, f32[2,8,2,1024]{3,2,1,0:T(2,128)}, u32[]{:S(2)}, u32[]{:S(2)}) collective-permute-start(f32[2,8,2,1024]{3,2,1,0:T(2,128)} %get-tuple-element.9), channel_id=1, source_target_pairs={{1,0},{2,1},{3,2},{4,3},{5,4},{6,5},{7,6},{8,7},{9,8},{10,9},{11,1... | collective-permute-start | bytes 393224 | tf_op jit(solution)/shard_map/ppermute | solution.py:20
  10.5 20.0 %all-to-all-start = ((s32[64,2,128]{2,1,0:T(2,128)}), s32[64,2,128]{2,1,0:T(2,128)S(1)}, u32[]{:S(2)}, u32[]{:S(2)}) async-start(s32[64,2,128]{2,1,0:T(2,128)} %bitcast.9), calls=%async_computation | async-start | bytes 131072 | tf_op jit(solution)/shard_map/all_to_all | solution.py:122
  22.0 46.6 %copy-start.29 = (s32[16]{0:T(128)}, s32[16]{0:T(128)S(1)}, u32[]{:S(2)}) copy-start(s32[16]{0:T(128)S(1)} %multiply_add_fusion) | copy-start | bytes 196
  24.9 5.8 %copy-start.4 = (f32[1,8,32,1024]{3,2,1,0:T(8,128)S(1)}, f32[1,8,32,1024]{3,2,1,0:T(8,128)}, u32[]{:S(2)}) copy-start(f32[1,8,32,1024]{3,2,1,0:T(8,128)} %param.13) | copy-start | bytes 3145732
  30.7 27.6 %copy-start.24 = (s32[128]{0:T(128)}, s32[128]{0:T(128)S(1)}, u32[]{:S(2)}) copy-start(s32[128]{0:T(128)S(1)} %fusion.106) | copy-start | bytes 1540
  32.8 3.0 %copy-start.17 = (f32[128,8,128]{2,1,0:T(8,128)}, f32[128,8,128]{2,1,0:T(8,128)S(1)}, u32[]{:S(2)}) copy-start(f32[128,8,128]{2,1,0:T(8,128)S(1)} %get-tuple-element.32) | copy-start | bytes 1572868
  32.8 3.0 %copy-start.16 = (bf16[128,8,128]{2,1,0:T(8,128)(2,1)S(1)}, bf16[128,8,128]{2,1,0:T(8,128)(2,1)}, u32[]{:S(2)}) copy-start(bf16[128,8,128]{2,1,0:T(8,128)(2,1)} %copy.34) | copy-start | bytes 786436
  36.7 16.9 %all-to-all-start.1 = ((bf16[64,16,256]{2,1,0:T(8,128)(2,1)}), bf16[64,16,256]{2,1,0:T(8,128)(2,1)}, u32[]{:S(2)}, u32[]{:S(2)}) async-start(bf16[64,16,256]{2,1,0:T(8,128)(2,1)} %pad_maximum_fusion.1), calls=%async_computation.1 | async-start | bytes 1048576 | tf_op jit(solution)/shard_map/all_to_all | solution.py:161
  47.8 7.6 %copy-start.19 = (bf16[128,8,128]{2,1,0:T(8,128)(2,1)S(1)}, bf16[128,8,128]{2,1,0:T(8,128)(2,1)}, u32[]{:S(2)}) copy-start(bf16[128,8,128]{2,1,0:T(8,128)(2,1)} %get-tuple-element.33) | copy-start | bytes 786436
  49.5 10.2 %collective-permute-start.2 = (f32[8,32,1024]{2,1,0:T(8,128)}, f32[8,32,1024]{2,1,0:T(8,128)}, u32[]{:S(2)}, u32[]{:S(2)}) collective-permute-start(f32[8,32,1024]{2,1,0:T(8,128)} %fusion.79), channel_id=1, source_target_pairs={{0,64},{64,0},{1,65},{65,1},{2,66},{66,2},{3,67},{67,3},{4,68},{68... | collective-permute-start | bytes 3145736 | tf_op jit(solution)/shard_map/ppermute | solution.py:185
  59.7 2.9 %copy-start.7 = (f32[8,8,4,8,128]{4,3,2,1,0:T(8,128)}, f32[8,8,4,8,128]{4,3,2,1,0:T(8,128)S(1)}, u32[]{:S(2)}) copy-start(f32[8,8,4,8,128]{4,3,2,1,0:T(8,128)S(1)} %fusion.47) | copy-start | bytes 3145732
  62.6 9.3 %collective-permute-start.3 = (f32[8,32,1024]{2,1,0:T(8,128)}, f32[8,32,1024]{2,1,0:T(8,128)}, u32[]{:S(2)}, u32[]{:S(2)}) collective-permute-start(f32[8,32,1024]{2,1,0:T(8,128)} %bitcast_multiply_fusion.7), channel_id=1, source_target_pairs={{64,0},{65,1},{66,2},{67,3},{68,4},{69,5},{70,6},{71,7},{72,8},{73... | collective-permute-start | bytes 3145736 | tf_op jit(solution)/shard_map/ppermute | solution.py:29
  71.9 5.9 %copy-start.2 = (bf16[1,16,128,1024]{3,2,1,0:T(8,128)(2,1)S(1)}, bf16[1,16,128,1024]{3,2,1,0:T(8,128)(2,1)}, u32[]{:S(2)}) copy-start(bf16[1,16,128,1024]{3,2,1,0:T(8,128)(2,1)} %param.23) | copy-start | bytes 12582916
  76.3 5.0 %collective-permute-start.4 = (f32[8,32,1024]{2,1,0:T(8,128)}, f32[8,32,1024]{2,1,0:T(8,128)}, u32[]{:S(2)}, u32[]{:S(2)}) collective-permute-start(f32[8,32,1024]{2,1,0:T(8,128)} %fusion.82), channel_id=1, source_target_pairs={{0,64},{1,65},{2,66},{3,67},{4,68},{5,69},{6,70},{7,71},{8,72},{9,... | collective-permute-start | bytes 3145736 | tf_op jit(solution)/shard_map/ppermute | solution.py:29
  80.4 5.5 %copy-start.25 = (s32[128]{0:T(128)S(1)}, s32[128]{0:T(128)}, u32[]{:S(2)}) copy-start(s32[128]{0:T(128)} %copy-done.24) | copy-start | bytes 1540
  85.9 4.8 %copy-start.11 = (f32[8,32,1024]{2,1,0:T(8,128)}, f32[8,32,1024]{2,1,0:T(8,128)S(1)}, u32[]{:S(2)}) copy-start(f32[8,32,1024]{2,1,0:T(8,128)S(1)} %get-tuple-element.3) | copy-start | bytes 3145732
  91.4 13.9 %copy-start.12 = (f32[8,32,1024]{2,1,0:T(8,128)S(1)}, f32[8,32,1024]{2,1,0:T(8,128)}, u32[]{:S(2)}) copy-start(f32[8,32,1024]{2,1,0:T(8,128)} %copy-done.11) | copy-start | bytes 3145732
  91.4 13.9 %collective-permute-start.5 = (f32[8,2,1024]{2,1,0:T(2,128)}, f32[8,2,1024]{2,1,0:T(2,128)}, u32[]{:S(2)}, u32[]{:S(2)}) collective-permute-start(f32[8,2,1024]{2,1,0:T(2,128)} %get-tuple-element.26), channel_id=1, source_target_pairs={{0,1},{1,2},{2,3},{3,4},{4,5},{5,6},{6,7},{7,8},{8,9},{9,10},{10,1... | collective-permute-start | bytes 196616 | tf_op jit(solution)/shard_map/ppermute | solution.py:18
  94.3 11.0 %collective-permute-start.6 = (f32[8,2,1024]{2,1,0:T(2,128)S(1)}, f32[8,2,1024]{2,1,0:T(2,128)}, u32[]{:S(2)}, u32[]{:S(2)}) collective-permute-start(f32[8,2,1024]{2,1,0:T(2,128)S(1)} %get-tuple-element.27), channel_id=1, source_target_pairs={{1,0},{2,1},{3,2},{4,3},{5,4},{6,5},{7,6},{8,7},{9,8},{10,9},{11,1... | collective-permute-start | bytes 196616 | tf_op jit(solution)/shard_map/ppermute | solution.py:20
  96.5 19.6 %all-to-all-start.2 = ((bf16[64,16,256]{2,1,0:T(8,128)(2,1)}), bf16[64,16,256]{2,1,0:T(8,128)(2,1)}, u32[]{:S(2)}, u32[]{:S(2)}) async-start(bf16[64,16,256]{2,1,0:T(8,128)(2,1)} %pad_maximum_fusion.2), calls=%async_computation.2 | async-start | bytes 1048576 | tf_op jit(solution)/shard_map/all_to_all | solution.py:161
  111.0 11.3 %collective-permute-start.7 = (f32[8,32,1024]{2,1,0:T(8,128)}, f32[8,32,1024]{2,1,0:T(8,128)}, u32[]{:S(2)}, u32[]{:S(2)}) collective-permute-start(f32[8,32,1024]{2,1,0:T(8,128)} %fusion.73), channel_id=1, source_target_pairs={{0,64},{64,0},{1,65},{65,1},{2,66},{66,2},{3,67},{67,3},{4,68},{68... | collective-permute-start | bytes 3145736 | tf_op jit(solution)/shard_map/ppermute | solution.py:185
  117.2 3.8 %copy-start.26 = (s32[128]{0:T(128)S(1)}, s32[128]{0:T(128)}, u32[]{:S(2)}) copy-start(s32[128]{0:T(128)} %copy-done.24) | copy-start | bytes 1540
  122.6 9.6 %copy-start.13 = (f32[1,8,32,1024]{3,2,1,0:T(8,128)S(1)}, f32[1,8,32,1024]{3,2,1,0:T(8,128)}, u32[]{:S(2)}) copy-start(f32[1,8,32,1024]{3,2,1,0:T(8,128)} %param.17) | copy-start | bytes 3145732
  122.6 9.6 %copy-start.14 = (f32[1,8,32,1024]{3,2,1,0:T(8,128)S(1)}, f32[1,8,32,1024]{3,2,1,0:T(8,128)}, u32[]{:S(2)}) copy-start(f32[1,8,32,1024]{3,2,1,0:T(8,128)} %param.16) | copy-start | bytes 3145732
  124.3 12.5 %copy-start.31 = (s32[16]{0:T(128)S(1)}, s32[16]{0:T(128)}, u32[]{:S(2)}) copy-start(s32[16]{0:T(128)} %copy-done.29) | copy-start | bytes 196
  124.3 7.9 %collective-permute-start.8 = (f32[8,32,1024]{2,1,0:T(8,128)S(1)}, f32[8,32,1024]{2,1,0:T(8,128)S(1)}, u32[]{:S(2)}, u32[]{:S(2)}) collective-permute-start(f32[8,32,1024]{2,1,0:T(8,128)S(1)} %bitcast_multiply_fusion.5), channel_id=1, source_target_pairs={{64,0},{65,1},{66,2},{67,3},{68,4},{69,5},{70,6},{71,7},{72,8},{73... | collective-permute-start | bytes 3145736 | tf_op jit(solution)/shard_map/ppermute | solution.py:29
  135.5 5.9 %collective-permute-start.9 = (f32[8,32,1024]{2,1,0:T(8,128)}, f32[8,32,1024]{2,1,0:T(8,128)S(1)}, u32[]{:S(2)}, u32[]{:S(2)}) collective-permute-start(f32[8,32,1024]{2,1,0:T(8,128)} %get-tuple-element.6), channel_id=1, source_target_pairs={{0,64},{1,65},{2,66},{3,67},{4,68},{5,69},{6,70},{7,71},{8,72},{9,... | collective-permute-start | bytes 3145736 | tf_op jit(solution)/shard_map/ppermute | solution.py:29
  137.4 3.4 %copy-start.23 = (bf16[1,16,128]{2,1,0:T(8,128)(2,1)S(1)}, bf16[1,16,128]{2,1,0:T(8,128)(2,1)}, u32[]{:S(2)}) copy-start(bf16[1,16,128]{2,1,0:T(8,128)(2,1)} %param.24) | copy-start | bytes 12292
  (14 other events, 21.6 us)

commit v5 on v4

--- a/solution.py
+++ b/solution.py
@@ -186,7 +186,13 @@
             forward = other * (1.0 - is_first)
             backward = other * (1.0 - is_last)
             r_dual = -(dual_model - backward) - adjoint_field
-            upward = r_dual + shifted(decay_field * r_dual, "tm", -1)
+            decayed = decay_field * r_dual
+            if repeat == ITERS - 1:
+                own_cols, decayed = lax.optimization_barrier((own_cols, decayed))
+                obs_image = jnp.einsum(
+                    "toj,tj->to", jac_tiles, own_cols, preferred_element_type=jnp.float32
+                )
+            upward = r_dual + shifted(decayed, "tm", -1)
         else:
             if scaling_ext is None:
                 scaling_ext = with_halo(scaling, "space", 1, SUBSTEPS)

time: 145 us -> 144 us (level)
    unnamed x68 -> x70, local copies, waits for them, and re-layouts: 3.32 us -> 3.32 us
where the time goes in v5:
time: 144 us; the launch traced here: 143 us
  starting transfers between devices  55.7 us (39%)
  other arithmetic  34 us (24%)
  matrix products  26.1 us (18%)
  local copies, waits for them, and re-layouts  14.6 us (10%)
  waiting for transfers between devices  11.5 us (8%)
    all_to_all x2, starting transfers between devices, on_device(): got = lax.all_to_all(both, 'space', split_axis=0, concat_axis=0, tiled=True)  14.7 us
    ppermute x4, starting transfers between devices, shifted(): return lax.ppermute(value, axis, pairs)  14.4 us
    all_to_all x1, starting transfers between devices, on_device(): lax.all_to_all(packed_cells.reshape(owners_count, capacity, touched), 'sp...  11.6 us
    sub x2, other arithmetic, on_device(): source = r_model - err_field * upward  7.76 us
    ppermute x2, starting transfers between devices, with_halo(): lax.ppermute(tail, axis, [(i, i + 1) for i in range(ends)])  7.53 us
    dot_general x2, matrix products, gather_cols(): jnp.einsum('slab,sbj->slaj', lines, col_oh, preferred_element_type=jnp.fl...  6.02 us
    select_n x2, other arithmetic, on_device(): chosen = jnp.where(tm_here == 0, increment, dual_model)  6.02 us
    dot_general x2, matrix products, spread_cols(): jnp.einsum('slaj,sbj->slab', placed, col_oh, preferred_element_type=jnp.f...  5.79 us
  transfers between devices with their start and end apart: 13, of which 5 were waited for; matrix products, arithmetic and copies ran while one was open for 32% of the time, Pallas kernels for 0%

profile of v5, /device:TPU:1, one launch (start us, length us, event | category | flops | bytes accessed | tf_op | source)
XLA Modules:
  0.0 143.2 jit_solution(10974580917130784393)
XLA Ops:
  0.7 1.5 %broadcast_select_fusion.1 = f32[1,8,32,1024]{3,2,1,0:T(8,128)S(1)} fusion(f32[1,8,32,1024]{3,2,1,0:T(8,128)} %param.13, f32[1,8,32,1024]{3,2,1,0:T(8,128)} %param.14, pred[]{:T(512)S(6)} %eq.87), kind=kLoop, calls=%fused_computation.115 | loop fusion | flops 262144 | bytes 3145729 | tf_op jit(solution)/shard_map/jit(_where)/select_n | solution.py:178
  3.0 4.6 %collective-permute-start = (f32[2,8,2,1024]{3,2,1,0:T(2,128)}, f32[2,8,2,1024]{3,2,1,0:T(2,128)}, u32[]{:S(2)}, u32[]{:S(2)}) collective-permute-start(f32[2,8,2,1024]{3,2,1,0:T(2,128)} %get-tuple-element.12), channel_id=1, source_target_pairs={{0,1},{1,2},{2,3},{3,4},{4,5},{5,6},{6,7},{7,8},{8,9},{9,10},{10,1... | collective-permute-start | bytes 393224 | tf_op jit(solution)/shard_map/ppermute | solution.py:18
  10.4 11.6 %all-to-all-start = ((s32[64,2,128]{2,1,0:T(2,128)}), s32[64,2,128]{2,1,0:T(2,128)S(1)}, u32[]{:S(2)}, u32[]{:S(2)}) async-start(s32[64,2,128]{2,1,0:T(2,128)} %bitcast.9), calls=%async_computation | async-start | bytes 131072 | tf_op jit(solution)/shard_map/all_to_all | solution.py:122
  22.0 2.8 %fusion.15 = bf16[16,1,1024]{2,1,0:T(2,128)(2,1)S(1)} fusion(bf16[1,16,128,1024]{3,2,1,0:T(8,128)(2,1)} %param.23, bf16[16,128,1]{1,0,2:T(8,128)(2,1)S(1)} %bitcast.264), kind=kOutput, calls=%fused_computation.13 | convolution fusion | flops 4194304 | bytes 4231168 | tf_op jit(solution)/shard_map/toj,to->tj/dot_general | solution.py:145
  26.3 4.1 %all-to-all-done = s32[64,2,128]{2,1,0:T(2,128)S(1)} async-done(((s32[64,2,128]{2,1,0:T(2,128)}), s32[64,2,128]{2,1,0:T(2,128)S(1)}, u32[]{:S(2)}, u32[]{:S(2)}) %all-to-all-start) | async-done | bytes 65568 | tf_op jit(solution)/shard_map/all_to_all | solution.py:122
  32.8 3.0 %multiply_reduce_fusion.1 = bf16[128,8,128]{2,1,0:T(8,128)(2,1)S(1)} fusion(f32[128,8,128]{2,1,0:T(8,128)S(1)} %get-tuple-element.36, s32[128,128]{1,0:T(8,128)S(1)} %get-tuple-element.39, bf16[128,8,8,128]{3,2,0,1:T(8,128)(2,1)S(1)} %bitcast.248), kind=kOutput, calls=%fused_computation.16 | convolution fusion | flops 272498688 | bytes 2949120 | tf_op jit(solution)/shard_map/slab,sbj->slaj/dot_general | solution.py:56
  36.7 5.9 %all-to-all-start.1 = ((bf16[64,16,256]{2,1,0:T(8,128)(2,1)}), bf16[64,16,256]{2,1,0:T(8,128)(2,1)}, u32[]{:S(2)}, u32[]{:S(2)}) async-start(bf16[64,16,256]{2,1,0:T(8,128)(2,1)} %pad_maximum_fusion.1), calls=%async_computation.1 | async-start | bytes 1048576 | tf_op jit(solution)/shard_map/all_to_all | solution.py:161
  42.7 1.4 pad_maximum_fusion
  47.8 1.7 %fusion.79 = f32[8,32,1024]{2,1,0:T(8,128)} fusion(f32[8,34,1024]{2,1,0:T(8,128)S(1)} %multiply_multiply_fusion.1, f32[8,32,1023]{2,1,0:T(8,128)S(1)} %get-tuple-element.23, f32[8,32,1]{2,1,0:T(8,128)S(1)} %get-tuple-element.25, f32[8,32,1]{2,1,0:T(8,128)S(1)} %get-tuple-element.24, f32[8,32,1023]{2,1,0:T(8,128)S(1)} %get-tuple-element.22, ...), kind=kLoop, calls=%fused_computation.77 | loop fusion | flops 2621440 | bytes 7340064 | tf_op jit(solution)/shard_map/mul | solution.py:44
  49.5 2.2 %collective-permute-start.2 = (f32[8,32,1024]{2,1,0:T(8,128)}, f32[8,32,1024]{2,1,0:T(8,128)}, u32[]{:S(2)}, u32[]{:S(2)}) collective-permute-start(f32[8,32,1024]{2,1,0:T(8,128)} %fusion.79), channel_id=1, source_target_pairs={{0,64},{64,0},{1,65},{65,1},{2,66},{66,2},{3,67},{67,3},{4,68},{68... | collective-permute-start | bytes 3145736 | tf_op jit(solution)/shard_map/ppermute | solution.py:185
  51.7 1.9 %all-to-all-done.1 = bf16[64,16,256]{2,1,0:T(8,128)(2,1)} async-done(((bf16[64,16,256]{2,1,0:T(8,128)(2,1)}), bf16[64,16,256]{2,1,0:T(8,128)(2,1)}, u32[]{:S(2)}, u32[]{:S(2)}) %all-to-all-start.1) | async-done | bytes 524320 | tf_op jit(solution)/shard_map/all_to_all | solution.py:161
  53.6 1.8 %fusion.153 = (bf16[64,16,128]{2,1,0:T(8,128)(2,1)}, bf16[64,16,128]{2,1,0:T(8,128)(2,1)S(1)}) fusion(bf16[64,16,256]{2,1,0:T(8,128)(2,1)} %all-to-all-done.1), kind=kLoop, calls=%fused_computation.192 | loop fusion | bytes 1048576 | tf_op jit(solution)/shard_map/slice | solution.py:162
  55.4 2.9 %fusion.29 = bf16[128,8,8,128]{3,2,1,0:T(8,128)(2,1)S(1)} fusion(s32[128,128]{1,0:T(8,128)S(1)} %get-tuple-element.39, bf16[128,8,128]{2,1,0:T(8,128)(2,1)S(1)} %copy-done.19, bf16[128,8,128]{2,1,0:T(8,128)(2,1)S(1)} %bitcast.259), kind=kOutput, calls=%fused_computation.32 | convolution fusion | flops 272629760 | bytes 2686976 | tf_op jit(solution)/shard_map/slaj,sbj->slab/dot_general | solution.py:67
  59.9 2.7 %bitcast_multiply_fusion.7 = f32[8,32,1024]{2,1,0:T(8,128)} fusion(f32[1,8,32,1024]{3,2,1,0:T(8,128)S(1)} %copy-done.8, f32[8,8,4,8,128]{4,3,2,1,0:T(8,128)S(1)} %fusion.47, f32[8,32,1024]{2,1,0:T(8,128)} %collective-permute-done.2, f32[]{:T(128)S(6)} %sub.85, f32[1,8,32,1024]{3,2,1,0:T(8,128)S(1)} %copy-done.5), kind=kLoop, calls=%fused_computation.91 | loop fusion | flops 1310720 | bytes 5242884 | tf_op jit(solution)/shard_map/mul | solution.py:189
  62.6 6.1 %collective-permute-start.3 = (f32[8,32,1024]{2,1,0:T(8,128)}, f32[8,32,1024]{2,1,0:T(8,128)}, u32[]{:S(2)}, u32[]{:S(2)}) collective-permute-start(f32[8,32,1024]{2,1,0:T(8,128)} %bitcast_multiply_fusion.7), channel_id=1, source_target_pairs={{64,0},{65,1},{66,2},{67,3},{68,4},{69,5},{70,6},{71,7},{72,8},{73... | collective-permute-start | bytes 3145736 | tf_op jit(solution)/shard_map/ppermute | solution.py:29
  71.9 4.4 %fusion.82 = f32[8,32,1024]{2,1,0:T(8,128)} fusion(f32[1,8,32,1024]{3,2,1,0:T(8,128)} %param.17, f32[1,8,32,1024]{3,2,1,0:T(8,128)} %param.16, f32[1,8,32,1024]{3,2,1,0:T(8,128)S(1)} %copy-done.4, f32[1,8,32,1024]{3,2,1,0:T(8,128)S(1)} %copy-done.5, f32[8,32,1024]{2,1,0:T(8,128)} %collective-permute-done.2, f32[]{:T(128)S(6)} %sub.92, ...), kind=kLoop, calls=%fused_computation.84 | loop fusion | flops 3145728 | bytes 8388616 | tf_op jit(solution)/shard_map/sub | solution.py:212
  76.3 1.4 collective-permute-start.4
  81.3 4.6 %broadcast_select_fusion = (f32[8,32,1024]{2,1,0:T(8,128)S(1)}, f32[8,32,1024]{2,1,0:T(8,128)S(1)}, f32[8,32,1024]{2,1,0:T(8,128)}) fusion(pred[]{:T(512)S(6)} %eq.87, f32[8,32,1024]{2,1,0:T(8,128)} %fusion.82, f32[8,32,1024]{2,1,0:T(8,128)} %collective-permute-done.4, f32[1,8,32,1024]{3,2,1,0:T(8,128)} %param.18, f32[1,8,32,1024]{3,2,1,0:T(8,128)S(1)} %copy-done.4, ...), kind=kLoop, calls=%fused_computation.114 | loop fusion | flops 2621440 | bytes 11534341 | tf_op jit(solution)/shard_map/jit(_where)/select_n | solution.py:178
  87.7 3.0 %multiply_reduce_fusion = bf16[128,8,128]{2,1,0:T(8,128)(2,1)S(1)} fusion(f32[128,8,128]{2,1,0:T(8,128)S(1)} %copy-done.18, s32[128,128]{1,0:T(8,128)S(1)} %get-tuple-element.39, bf16[128,8,8,128]{3,2,0,1:T(8,128)(2,1)S(1)} %bitcast.249), kind=kOutput, calls=%fused_computation.15 | convolution fusion | flops 272498688 | bytes 2949120 | tf_op jit(solution)/shard_map/slab,sbj->slaj/dot_general | solution.py:56
  91.4 2.9 %collective-permute-start.5 = (f32[8,2,1024]{2,1,0:T(2,128)}, f32[8,2,1024]{2,1,0:T(2,128)}, u32[]{:S(2)}, u32[]{:S(2)}) collective-permute-start(f32[8,2,1024]{2,1,0:T(2,128)} %get-tuple-element.30), channel_id=1, source_target_pairs={{0,1},{1,2},{2,3},{3,4},{4,5},{5,6},{6,7},{7,8},{8,9},{9,10},{10,1... | collective-permute-start | bytes 196616 | tf_op jit(solution)/shard_map/ppermute | solution.py:18
  96.5 8.8 %all-to-all-start.2 = ((bf16[64,16,256]{2,1,0:T(8,128)(2,1)}), bf16[64,16,256]{2,1,0:T(8,128)(2,1)}, u32[]{:S(2)}, u32[]{:S(2)}) async-start(bf16[64,16,256]{2,1,0:T(8,128)(2,1)} %pad_maximum_fusion.2), calls=%async_computation.2 | async-start | bytes 1048576 | tf_op jit(solution)/shard_map/all_to_all | solution.py:161
  105.3 1.7 %maximum_multiply_fusion = f32[8,36,1024]{2,1,0:T(8,128)S(1)} fusion(f32[8,2,1024]{2,1,0:T(2,128)} %collective-permute-done.6, f32[8,32,1024]{2,1,0:T(8,128)S(1)} %copy-done.12, f32[8,2,1024]{2,1,0:T(2,128)} %collective-permute-done.5, f32[2,8,36,1024]{3,2,1,0:T(8,128)} %copy-done.3), kind=kLoop, calls=%fused_computation.53 | loop fusion | flops 884736 | bytes 3538944 | tf_op jit(solution)/shard_map/mul | solution.py:35
  109.4 1.7 %fusion.73 = f32[8,32,1024]{2,1,0:T(8,128)} fusion(f32[8,34,1024]{2,1,0:T(8,128)S(1)} %multiply_multiply_fusion, f32[8,32,1023]{2,1,0:T(8,128)S(1)} %get-tuple-element.15, f32[8,32,1]{2,1,0:T(8,128)S(1)} %get-tuple-element.17, f32[8,32,1]{2,1,0:T(8,128)S(1)} %get-tuple-element.16, f32[8,32,1023]{2,1,0:T(8,128)S(1)} %get-tuple-element.14, ...), kind=kLoop, calls=%fused_computation.70 | loop fusion | flops 2621440 | bytes 7340064 | tf_op jit(solution)/shard_map/mul | solution.py:44
  111.0 2.7 %collective-permute-start.7 = (f32[8,32,1024]{2,1,0:T(8,128)}, f32[8,32,1024]{2,1,0:T(8,128)}, u32[]{:S(2)}, u32[]{:S(2)}) collective-permute-start(f32[8,32,1024]{2,1,0:T(8,128)} %fusion.73), channel_id=1, source_target_pairs={{0,64},{64,0},{1,65},{65,1},{2,66},{66,2},{3,67},{67,3},{4,68},{68... | collective-permute-start | bytes 3145736 | tf_op jit(solution)/shard_map/ppermute | solution.py:185
  113.7 2.4 %all-to-all-done.2 = bf16[64,16,256]{2,1,0:T(8,128)(2,1)} async-done(((bf16[64,16,256]{2,1,0:T(8,128)(2,1)}), bf16[64,16,256]{2,1,0:T(8,128)(2,1)}, u32[]{:S(2)}, u32[]{:S(2)}) %all-to-all-start.2) | async-done | bytes 524320 | tf_op jit(solution)/shard_map/all_to_all | solution.py:161
  117.6 2.9 %fusion.34 = bf16[128,8,8,128]{3,2,1,0:T(8,128)(2,1)S(1)} fusion(s32[128,128]{1,0:T(8,128)S(1)} %get-tuple-element.39, bf16[128,8,128]{2,1,0:T(8,128)(2,1)S(1)} %bitcast.258, bf16[128,8,128]{2,1,0:T(8,128)(2,1)S(1)} %copy-done.20), kind=kOutput, calls=%fused_computation.33 | convolution fusion | flops 272629760 | bytes 2686976 | tf_op jit(solution)/shard_map/slaj,sbj->slab/dot_general | solution.py:67
  122.0 1.7 %bitcast_multiply_fusion.5 = f32[8,32,1024]{2,1,0:T(8,128)S(1)} fusion(f32[1,8,32,1024]{3,2,1,0:T(8,128)S(1)} %copy-done.9, f32[8,8,4,8,128]{4,3,2,1,0:T(8,128)S(1)} %fusion.50, f32[8,32,1024]{2,1,0:T(8,128)S(1)} %copy-done.10, f32[8,32,1024]{2,1,0:T(8,128)} %collective-permute-done.7, f32[]{:T(128)S(6)} %sub.85), kind=kLoop, calls=%fused_computation.89 | loop fusion | flops 1310720 | bytes 5242884 | tf_op jit(solution)/shard_map/mul | solution.py:189
  123.8 5.7 %collective-permute-start.8 = (f32[8,32,1024]{2,1,0:T(8,128)S(1)}, f32[8,32,1024]{2,1,0:T(8,128)S(1)}, u32[]{:S(2)}, u32[]{:S(2)}) collective-permute-start(f32[8,32,1024]{2,1,0:T(8,128)S(1)} %bitcast_multiply_fusion.5), channel_id=1, source_target_pairs={{64,0},{65,1},{66,2},{67,3},{68,4},{69,5},{70,6},{71,7},{72,8},{73... | collective-permute-start | bytes 3145736 | tf_op jit(solution)/shard_map/ppermute | solution.py:29
  129.5 2.2 %collective-permute-done.8 = f32[8,32,1024]{2,1,0:T(8,128)S(1)} collective-permute-done((f32[8,32,1024]{2,1,0:T(8,128)S(1)}, f32[8,32,1024]{2,1,0:T(8,128)S(1)}, u32[]{:S(2)}, u32[]{:S(2)}) %collective-permute-start.8) | collective-permute-done | bytes 1048608 | tf_op jit(solution)/shard_map/ppermute | solution.py:29
  131.7 3.3 %fusion.85 = (f32[8,32,1024]{2,1,0:T(8,128)}, f32[1,8,32,1024]{3,2,1,0:T(8,128)}) fusion(f32[8,32,1024]{2,1,0:T(8,128)S(1)} %copy-done.10, f32[1,8,32,1024]{3,2,1,0:T(8,128)S(1)} %copy-done.13, f32[1,8,32,1024]{3,2,1,0:T(8,128)S(1)} %copy-done.14, f32[8,32,1024]{2,1,0:T(8,128)S(1)} %get-tuple-element.8, f32[8,32,1024]{2,1,0:T(8,128)} %collective-permute-done.7, ...), kind=kLoop, calls=%fused_computation.87 | loop fusion | flops 3407872 | bytes 9437192 | tf_op jit(solution)/shard_map/sub | solution.py:212
  136.5 3.4 %fusion.9 = f32[16,1,128]{2,1,0:T(1,128)S(1)} fusion(bf16[16,1024,1]{1,2,0:T(2,128)(2,1)S(1)} %copy.54, bf16[1,16,128,1024]{3,2,1,0:T(8,128)(2,1)} %param.23), kind=kOutput, calls=%fused_computation.7 | convolution fusion | flops 4194304 | bytes 4235264 | tf_op jit(solution)/shard_map/toj,tj->to/dot_general | solution.py:192
  140.5 2.7 %fusion.90 = f32[1,8,32,1024]{3,2,1,0:T(8,128)} fusion(f32[8,32,1024]{2,1,0:T(8,128)S(1)} %get-tuple-element.8, f32[8,32,1024]{2,1,0:T(8,128)} %get-tuple-element.10, f32[8,32,1024]{2,1,0:T(8,128)S(1)} %collective-permute-done.9, f32[1,8,32,1024]{3,2,1,0:T(8,128)S(1)} %copy-done.9), kind=kLoop, calls=%fused_computation.96 | loop fusion | flops 786432 | bytes 5242880 | tf_op jit(solution)/shard_map/broadcast_in_dim | solution.py:217
  (130 shorter events, 32.3 us)
Async XLA Ops:
  0.6 8.6 %copy-start = (s32[1,16,128]{2,1,0:T(8,128)S(1)}, s32[1,16,128]{2,1,0:T(8,128)}, u32[]{:S(2)}) copy-start(s32[1,16,128]{2,1,0:T(8,128)} %param.22) | copy-start | bytes 24580
  2.1 6.8 %copy-start.33 = (s32[1,16]{1,0:T(1,128)S(1)}, s32[1,16]{1,0:T(1,128)}, u32[]{:S(2)}) copy-start(s32[1,16]{1,0:T(1,128)} %param.21) | copy-start | bytes 196
  2.1 19.9 %copy-start.21 = (bf16[1,16,128]{2,1,0:T(8,128)(2,1)S(1)}, bf16[1,16,128]{2,1,0:T(8,128)(2,1)}, u32[]{:S(2)}) copy-start(bf16[1,16,128]{2,1,0:T(8,128)(2,1)} %param.15) | copy-start | bytes 12292
  3.0 39.7 %collective-permute-start = (f32[2,8,2,1024]{3,2,1,0:T(2,128)}, f32[2,8,2,1024]{3,2,1,0:T(2,128)}, u32[]{:S(2)}, u32[]{:S(2)}) collective-permute-start(f32[2,8,2,1024]{3,2,1,0:T(2,128)} %get-tuple-element.12), channel_id=1, source_target_pairs={{0,1},{1,2},{2,3},{3,4},{4,5},{5,6},{6,7},{7,8},{8,9},{9,10},{10,1... | collective-permute-start | bytes 393224 | tf_op jit(solution)/shard_map/ppermute | solution.py:18
  7.6 35.1 %collective-permute-start.1 = (f32[2,8,2,1024]{3,2,1,0:T(2,128)}, f32[2,8,2,1024]{3,2,1,0:T(2,128)}, u32[]{:S(2)}, u32[]{:S(2)}) collective-permute-start(f32[2,8,2,1024]{3,2,1,0:T(2,128)} %get-tuple-element.13), channel_id=1, source_target_pairs={{1,0},{2,1},{3,2},{4,3},{5,4},{6,5},{7,6},{8,7},{9,8},{10,9},{11,1... | collective-permute-start | bytes 393224 | tf_op jit(solution)/shard_map/ppermute | solution.py:20
  10.4 20.0 %all-to-all-start = ((s32[64,2,128]{2,1,0:T(2,128)}), s32[64,2,128]{2,1,0:T(2,128)S(1)}, u32[]{:S(2)}, u32[]{:S(2)}) async-start(s32[64,2,128]{2,1,0:T(2,128)} %bitcast.9), calls=%async_computation | async-start | bytes 131072 | tf_op jit(solution)/shard_map/all_to_all | solution.py:122
  22.0 46.7 %copy-start.30 = (s32[16]{0:T(128)}, s32[16]{0:T(128)S(1)}, u32[]{:S(2)}) copy-start(s32[16]{0:T(128)S(1)} %multiply_add_fusion) | copy-start | bytes 196
  24.9 5.8 %copy-start.4 = (f32[1,8,32,1024]{3,2,1,0:T(8,128)S(1)}, f32[1,8,32,1024]{3,2,1,0:T(8,128)}, u32[]{:S(2)}) copy-start(f32[1,8,32,1024]{3,2,1,0:T(8,128)} %param.13) | copy-start | bytes 3145732
  30.6 27.7 %copy-start.25 = (s32[128]{0:T(128)}, s32[128]{0:T(128)S(1)}, u32[]{:S(2)}) copy-start(s32[128]{0:T(128)S(1)} %fusion.106) | copy-start | bytes 1540
  32.8 3.0 %copy-start.17 = (f32[128,8,128]{2,1,0:T(8,128)}, f32[128,8,128]{2,1,0:T(8,128)S(1)}, u32[]{:S(2)}) copy-start(f32[128,8,128]{2,1,0:T(8,128)S(1)} %get-tuple-element.36) | copy-start | bytes 1572868
  32.8 3.0 %copy-start.16 = (bf16[128,8,128]{2,1,0:T(8,128)(2,1)S(1)}, bf16[128,8,128]{2,1,0:T(8,128)(2,1)}, u32[]{:S(2)}) copy-start(bf16[128,8,128]{2,1,0:T(8,128)(2,1)} %copy.34) | copy-start | bytes 786436
  36.7 16.9 %all-to-all-start.1 = ((bf16[64,16,256]{2,1,0:T(8,128)(2,1)}), bf16[64,16,256]{2,1,0:T(8,128)(2,1)}, u32[]{:S(2)}, u32[]{:S(2)}) async-start(bf16[64,16,256]{2,1,0:T(8,128)(2,1)} %pad_maximum_fusion.1), calls=%async_computation.1 | async-start | bytes 1048576 | tf_op jit(solution)/shard_map/all_to_all | solution.py:161
  47.8 7.6 %copy-start.19 = (bf16[128,8,128]{2,1,0:T(8,128)(2,1)S(1)}, bf16[128,8,128]{2,1,0:T(8,128)(2,1)}, u32[]{:S(2)}) copy-start(bf16[128,8,128]{2,1,0:T(8,128)(2,1)} %get-tuple-element.37) | copy-start | bytes 786436
  49.5 10.2 %collective-permute-start.2 = (f32[8,32,1024]{2,1,0:T(8,128)}, f32[8,32,1024]{2,1,0:T(8,128)}, u32[]{:S(2)}, u32[]{:S(2)}) collective-permute-start(f32[8,32,1024]{2,1,0:T(8,128)} %fusion.79), channel_id=1, source_target_pairs={{0,64},{64,0},{1,65},{65,1},{2,66},{66,2},{3,67},{67,3},{4,68},{68... | collective-permute-start | bytes 3145736 | tf_op jit(solution)/shard_map/ppermute | solution.py:185
  62.6 9.3 %collective-permute-start.3 = (f32[8,32,1024]{2,1,0:T(8,128)}, f32[8,32,1024]{2,1,0:T(8,128)}, u32[]{:S(2)}, u32[]{:S(2)}) collective-permute-start(f32[8,32,1024]{2,1,0:T(8,128)} %bitcast_multiply_fusion.7), channel_id=1, source_target_pairs={{64,0},{65,1},{66,2},{67,3},{68,4},{69,5},{70,6},{71,7},{72,8},{73... | collective-permute-start | bytes 3145736 | tf_op jit(solution)/shard_map/ppermute | solution.py:29
  71.9 5.9 %copy-start.2 = (bf16[1,16,128,1024]{3,2,1,0:T(8,128)(2,1)S(1)}, bf16[1,16,128,1024]{3,2,1,0:T(8,128)(2,1)}, u32[]{:S(2)}) copy-start(bf16[1,16,128,1024]{3,2,1,0:T(8,128)(2,1)} %param.23) | copy-start | bytes 12582916
  76.3 5.0 %collective-permute-start.4 = (f32[8,32,1024]{2,1,0:T(8,128)}, f32[8,32,1024]{2,1,0:T(8,128)}, u32[]{:S(2)}, u32[]{:S(2)}) collective-permute-start(f32[8,32,1024]{2,1,0:T(8,128)} %fusion.82), channel_id=1, source_target_pairs={{0,64},{1,65},{2,66},{3,67},{4,68},{5,69},{6,70},{7,71},{8,72},{9,... | collective-permute-start | bytes 3145736 | tf_op jit(solution)/shard_map/ppermute | solution.py:29
  80.4 5.5 %copy-start.26 = (s32[128]{0:T(128)S(1)}, s32[128]{0:T(128)}, u32[]{:S(2)}) copy-start(s32[128]{0:T(128)} %copy-done.25) | copy-start | bytes 1540
  85.9 4.8 %copy-start.11 = (f32[8,32,1024]{2,1,0:T(8,128)}, f32[8,32,1024]{2,1,0:T(8,128)S(1)}, u32[]{:S(2)}) copy-start(f32[8,32,1024]{2,1,0:T(8,128)S(1)} %get-tuple-element.7) | copy-start | bytes 3145732
  91.4 13.9 %copy-start.12 = (f32[8,32,1024]{2,1,0:T(8,128)S(1)}, f32[8,32,1024]{2,1,0:T(8,128)}, u32[]{:S(2)}) copy-start(f32[8,32,1024]{2,1,0:T(8,128)} %copy-done.11) | copy-start | bytes 3145732
  91.4 13.9 %collective-permute-start.5 = (f32[8,2,1024]{2,1,0:T(2,128)}, f32[8,2,1024]{2,1,0:T(2,128)}, u32[]{:S(2)}, u32[]{:S(2)}) collective-permute-start(f32[8,2,1024]{2,1,0:T(2,128)} %get-tuple-element.30), channel_id=1, source_target_pairs={{0,1},{1,2},{2,3},{3,4},{4,5},{5,6},{6,7},{7,8},{8,9},{9,10},{10,1... | collective-permute-start | bytes 196616 | tf_op jit(solution)/shard_map/ppermute | solution.py:18
  94.3 11.0 %collective-permute-start.6 = (f32[8,2,1024]{2,1,0:T(2,128)S(1)}, f32[8,2,1024]{2,1,0:T(2,128)}, u32[]{:S(2)}, u32[]{:S(2)}) collective-permute-start(f32[8,2,1024]{2,1,0:T(2,128)S(1)} %get-tuple-element.31), channel_id=1, source_target_pairs={{1,0},{2,1},{3,2},{4,3},{5,4},{6,5},{7,6},{8,7},{9,8},{10,9},{11,1... | collective-permute-start | bytes 196616 | tf_op jit(solution)/shard_map/ppermute | solution.py:20
  96.5 19.6 %all-to-all-start.2 = ((bf16[64,16,256]{2,1,0:T(8,128)(2,1)}), bf16[64,16,256]{2,1,0:T(8,128)(2,1)}, u32[]{:S(2)}, u32[]{:S(2)}) async-start(bf16[64,16,256]{2,1,0:T(8,128)(2,1)} %pad_maximum_fusion.2), calls=%async_computation.2 | async-start | bytes 1048576 | tf_op jit(solution)/shard_map/all_to_all | solution.py:161
  109.4 7.8 %copy-start.32 = (s32[16]{0:T(128)S(1)}, s32[16]{0:T(128)}, u32[]{:S(2)}) copy-start(s32[16]{0:T(128)} %copy-done.30) | copy-start | bytes 196
  111.0 6.5 %copy-start.20 = (bf16[128,8,128]{2,1,0:T(8,128)(2,1)S(1)}, bf16[128,8,128]{2,1,0:T(8,128)(2,1)}, u32[]{:S(2)}) copy-start(bf16[128,8,128]{2,1,0:T(8,128)(2,1)} %get-tuple-element.37) | copy-start | bytes 786436
  111.0 10.8 %collective-permute-start.7 = (f32[8,32,1024]{2,1,0:T(8,128)}, f32[8,32,1024]{2,1,0:T(8,128)}, u32[]{:S(2)}, u32[]{:S(2)}) collective-permute-start(f32[8,32,1024]{2,1,0:T(8,128)} %fusion.73), channel_id=1, source_target_pairs={{0,64},{64,0},{1,65},{65,1},{2,66},{66,2},{3,67},{67,3},{4,68},{68... | collective-permute-start | bytes 3145736 | tf_op jit(solution)/shard_map/ppermute | solution.py:185
  117.6 2.9 %copy-start.27 = (s32[128]{0:T(128)S(1)}, s32[128]{0:T(128)}, u32[]{:S(2)}) copy-start(s32[128]{0:T(128)} %copy-done.25) | copy-start | bytes 1540
  122.0 9.6 %copy-start.13 = (f32[1,8,32,1024]{3,2,1,0:T(8,128)S(1)}, f32[1,8,32,1024]{3,2,1,0:T(8,128)}, u32[]{:S(2)}) copy-start(f32[1,8,32,1024]{3,2,1,0:T(8,128)} %param.17) | copy-start | bytes 3145732
  122.0 9.6 %copy-start.14 = (f32[1,8,32,1024]{3,2,1,0:T(8,128)S(1)}, f32[1,8,32,1024]{3,2,1,0:T(8,128)}, u32[]{:S(2)}) copy-start(f32[1,8,32,1024]{3,2,1,0:T(8,128)} %param.16) | copy-start | bytes 3145732
  123.8 7.9 %collective-permute-start.8 = (f32[8,32,1024]{2,1,0:T(8,128)S(1)}, f32[8,32,1024]{2,1,0:T(8,128)S(1)}, u32[]{:S(2)}, u32[]{:S(2)}) collective-permute-start(f32[8,32,1024]{2,1,0:T(8,128)S(1)} %bitcast_multiply_fusion.5), channel_id=1, source_target_pairs={{64,0},{65,1},{66,2},{67,3},{68,4},{69,5},{70,6},{71,7},{72,8},{73... | collective-permute-start | bytes 3145736 | tf_op jit(solution)/shard_map/ppermute | solution.py:29
  135.0 5.5 %collective-permute-start.9 = (f32[8,32,1024]{2,1,0:T(8,128)}, f32[8,32,1024]{2,1,0:T(8,128)S(1)}, u32[]{:S(2)}, u32[]{:S(2)}) collective-permute-start(f32[8,32,1024]{2,1,0:T(8,128)} %get-tuple-element.10), channel_id=1, source_target_pairs={{0,64},{1,65},{2,66},{3,67},{4,68},{5,69},{6,70},{7,71},{8,72},{9,... | collective-permute-start | bytes 3145736 | tf_op jit(solution)/shard_map/ppermute | solution.py:29
  136.5 3.4 %copy-start.24 = (bf16[1,16,128]{2,1,0:T(8,128)(2,1)S(1)}, bf16[1,16,128]{2,1,0:T(8,128)(2,1)}, u32[]{:S(2)}) copy-start(bf16[1,16,128]{2,1,0:T(8,128)(2,1)} %param.24) | copy-start | bytes 12292
  (15 other events, 24.5 us)

commit v6 on v5

--- a/solution.py
+++ b/solution.py
@@ -53,9 +53,8 @@
         "sr,lrc->slc", row_oh, fields.astype(jnp.bfloat16), preferred_element_type=jnp.float32
     ).astype(jnp.bfloat16)
     lines = lines.reshape(slots, levels, groups, lanes)
-    picked = jnp.einsum("slab,sbj->slaj", lines, col_oh, preferred_element_type=jnp.float32)
-    picked = jnp.sum(picked * group_mask[:, None, :, :], axis=2)
-    return picked.astype(jnp.bfloat16)
+    picked = jnp.einsum("slab,sbj->slaj", lines, col_oh, preferred_element_type=jnp.bfloat16)
+    return jnp.sum(picked * group_mask[:, None, :, :].astype(jnp.bfloat16), axis=2)
 
 
 def spread_cols(values, row_oh, col_oh, group_mask, levels, col_count):

time: 144 us -> 143 us (level)
  no operation moved by 1% of the time
where the time goes in v6:
time: 143 us; the launch traced here: 142 us
  starting transfers between devices  55.7 us (39%)
  other arithmetic  33.2 us (23%)
  matrix products  26.1 us (18%)
  local copies, waits for them, and re-layouts  14.5 us (10%)
  waiting for transfers between devices  11.5 us (8%)
    all_to_all x2, starting transfers between devices, on_device(): got = lax.all_to_all(both, 'space', split_axis=0, concat_axis=0, tiled=True)  14.7 us
    ppermute x4, starting transfers between devices, shifted(): return lax.ppermute(value, axis, pairs)  14.4 us
    all_to_all x1, starting transfers between devices, on_device(): lax.all_to_all(packed_cells.reshape(owners_count, capacity, touched), 'sp...  11.5 us
    sub x2, other arithmetic, on_device(): source = r_model - err_field * upward  7.76 us
    ppermute x2, starting transfers between devices, with_halo(): lax.ppermute(tail, axis, [(i, i + 1) for i in range(ends)])  7.56 us
    dot_general x2, matrix products, gather_cols(): jnp.einsum('slab,sbj->slaj', lines, col_oh, preferred_element_type=jnp.bf...  6.06 us
    select_n x2, other arithmetic, on_device(): chosen = jnp.where(tm_here == 0, increment, dual_model)  6.02 us
    dot_general x2, matrix products, spread_cols(): jnp.einsum('slaj,sbj->slab', placed, col_oh, preferred_element_type=jnp.f...  5.79 us
  transfers between devices with their start and end apart: 13, of which 5 were waited for; matrix products, arithmetic and copies ran while one was open for 32% of the time, Pallas kernels for 0%

profile of v6, /device:TPU:1, one launch (start us, length us, event | category | flops | bytes accessed | tf_op | source)
XLA Modules:
  0.0 142.4 jit_solution(11231457942130401011)
XLA Ops:
  0.7 1.5 %broadcast_select_fusion.1 = f32[1,8,32,1024]{3,2,1,0:T(8,128)S(1)} fusion(f32[1,8,32,1024]{3,2,1,0:T(8,128)} %param.13, f32[1,8,32,1024]{3,2,1,0:T(8,128)} %param.14, pred[]{:T(512)S(6)} %eq.84), kind=kLoop, calls=%fused_computation.115 | loop fusion | flops 262144 | bytes 3145729 | tf_op jit(solution)/shard_map/jit(_where)/select_n | solution.py:177
  3.0 4.6 %collective-permute-start = (f32[2,8,2,1024]{3,2,1,0:T(2,128)}, f32[2,8,2,1024]{3,2,1,0:T(2,128)}, u32[]{:S(2)}, u32[]{:S(2)}) collective-permute-start(f32[2,8,2,1024]{3,2,1,0:T(2,128)} %get-tuple-element.12), channel_id=1, source_target_pairs={{0,1},{1,2},{2,3},{3,4},{4,5},{5,6},{6,7},{7,8},{8,9},{9,10},{10,1... | collective-permute-start | bytes 393224 | tf_op jit(solution)/shard_map/ppermute | solution.py:18
  10.5 11.5 %all-to-all-start = ((s32[64,2,128]{2,1,0:T(2,128)}), s32[64,2,128]{2,1,0:T(2,128)S(1)}, u32[]{:S(2)}, u32[]{:S(2)}) async-start(s32[64,2,128]{2,1,0:T(2,128)} %bitcast.9), calls=%async_computation | async-start | bytes 131072 | tf_op jit(solution)/shard_map/all_to_all | solution.py:121
  22.0 2.8 %fusion.15 = bf16[16,1,1024]{2,1,0:T(2,128)(2,1)S(1)} fusion(bf16[1,16,128,1024]{3,2,1,0:T(8,128)(2,1)} %param.23, bf16[16,128,1]{1,0,2:T(8,128)(2,1)S(1)} %bitcast.264), kind=kOutput, calls=%fused_computation.13 | convolution fusion | flops 4194304 | bytes 4231168 | tf_op jit(solution)/shard_map/toj,to->tj/dot_general | solution.py:144
  26.3 4.1 %all-to-all-done = s32[64,2,128]{2,1,0:T(2,128)S(1)} async-done(((s32[64,2,128]{2,1,0:T(2,128)}), s32[64,2,128]{2,1,0:T(2,128)S(1)}, u32[]{:S(2)}, u32[]{:S(2)}) %all-to-all-start) | async-done | bytes 65568 | tf_op jit(solution)/shard_map/all_to_all | solution.py:121
  32.1 3.0 %multiply_reduce_fusion.1 = bf16[128,8,128]{2,1,0:T(8,128)(2,1)S(1)} fusion(s32[128,128]{1,0:T(8,128)S(1)} %get-tuple-element.37, bf16[128,8,8,128]{3,2,0,1:T(8,128)(2,1)S(1)} %bitcast.248, bf16[128,8,128]{2,1,0:T(8,128)(2,1)S(1)} %convert_convert_fusion), kind=kOutput, calls=%fused_computation.29 | convolution fusion | flops 272498688 | bytes 2686976 | tf_op jit(solution)/shard_map/slab,sbj->slaj/dot_general | solution.py:56
  36.0 5.9 %all-to-all-start.1 = ((bf16[64,16,256]{2,1,0:T(8,128)(2,1)}), bf16[64,16,256]{2,1,0:T(8,128)(2,1)}, u32[]{:S(2)}, u32[]{:S(2)}) async-start(bf16[64,16,256]{2,1,0:T(8,128)(2,1)} %pad_maximum_fusion.1), calls=%async_computation.1 | async-start | bytes 1048576 | tf_op jit(solution)/shard_map/all_to_all | solution.py:160
  42.0 1.4 pad_maximum_fusion
  47.1 1.7 %fusion.79 = f32[8,32,1024]{2,1,0:T(8,128)} fusion(f32[8,34,1024]{2,1,0:T(8,128)S(1)} %multiply_multiply_fusion.1, f32[8,32,1023]{2,1,0:T(8,128)S(1)} %get-tuple-element.23, f32[8,32,1]{2,1,0:T(8,128)S(1)} %get-tuple-element.25, f32[8,32,1]{2,1,0:T(8,128)S(1)} %get-tuple-element.24, f32[8,32,1023]{2,1,0:T(8,128)S(1)} %get-tuple-element.22, ...), kind=kLoop, calls=%fused_computation.77 | loop fusion | flops 2621440 | bytes 7340064 | tf_op jit(solution)/shard_map/mul | solution.py:44
  48.8 2.2 %collective-permute-start.2 = (f32[8,32,1024]{2,1,0:T(8,128)}, f32[8,32,1024]{2,1,0:T(8,128)}, u32[]{:S(2)}, u32[]{:S(2)}) collective-permute-start(f32[8,32,1024]{2,1,0:T(8,128)} %fusion.79), channel_id=1, source_target_pairs={{0,64},{64,0},{1,65},{65,1},{2,66},{66,2},{3,67},{67,3},{4,68},{68... | collective-permute-start | bytes 3145736 | tf_op jit(solution)/shard_map/ppermute | solution.py:184
  51.0 1.9 %all-to-all-done.1 = bf16[64,16,256]{2,1,0:T(8,128)(2,1)} async-done(((bf16[64,16,256]{2,1,0:T(8,128)(2,1)}), bf16[64,16,256]{2,1,0:T(8,128)(2,1)}, u32[]{:S(2)}, u32[]{:S(2)}) %all-to-all-start.1) | async-done | bytes 524320 | tf_op jit(solution)/shard_map/all_to_all | solution.py:160
  52.9 1.8 %fusion.151 = (bf16[64,16,128]{2,1,0:T(8,128)(2,1)}, bf16[64,16,128]{2,1,0:T(8,128)(2,1)S(1)}) fusion(bf16[64,16,256]{2,1,0:T(8,128)(2,1)} %all-to-all-done.1), kind=kLoop, calls=%fused_computation.191 | loop fusion | bytes 1048576 | tf_op jit(solution)/shard_map/slice | solution.py:161
  54.7 2.9 %fusion.29 = bf16[128,8,8,128]{3,2,1,0:T(8,128)(2,1)S(1)} fusion(s32[128,128]{1,0:T(8,128)S(1)} %get-tuple-element.37, bf16[128,8,128]{2,1,0:T(8,128)(2,1)S(1)} %bitcast.260, bf16[128,8,128]{2,1,0:T(8,128)(2,1)S(1)} %copy-done.18), kind=kOutput, calls=%fused_computation.32 | convolution fusion | flops 272629760 | bytes 2686976 | tf_op jit(solution)/shard_map/slaj,sbj->slab/dot_general | solution.py:66
  59.2 2.7 %bitcast_multiply_fusion.7 = f32[8,32,1024]{2,1,0:T(8,128)} fusion(f32[1,8,32,1024]{3,2,1,0:T(8,128)S(1)} %copy-done.8, f32[8,8,4,8,128]{4,3,2,1,0:T(8,128)S(1)} %fusion.47, f32[8,32,1024]{2,1,0:T(8,128)} %collective-permute-done.2, f32[]{:T(128)S(6)} %sub.85, f32[1,8,32,1024]{3,2,1,0:T(8,128)S(1)} %copy-done.5), kind=kLoop, calls=%fused_computation.91 | loop fusion | flops 1310720 | bytes 5242884 | tf_op jit(solution)/shard_map/mul | solution.py:188
  61.9 6.1 %collective-permute-start.3 = (f32[8,32,1024]{2,1,0:T(8,128)}, f32[8,32,1024]{2,1,0:T(8,128)}, u32[]{:S(2)}, u32[]{:S(2)}) collective-permute-start(f32[8,32,1024]{2,1,0:T(8,128)} %bitcast_multiply_fusion.7), channel_id=1, source_target_pairs={{64,0},{65,1},{66,2},{67,3},{68,4},{69,5},{70,6},{71,7},{72,8},{73... | collective-permute-start | bytes 3145736 | tf_op jit(solution)/shard_map/ppermute | solution.py:29
  71.2 4.4 %fusion.82 = f32[8,32,1024]{2,1,0:T(8,128)} fusion(f32[1,8,32,1024]{3,2,1,0:T(8,128)} %param.17, f32[1,8,32,1024]{3,2,1,0:T(8,128)} %param.16, f32[1,8,32,1024]{3,2,1,0:T(8,128)S(1)} %copy-done.4, f32[1,8,32,1024]{3,2,1,0:T(8,128)S(1)} %copy-done.5, f32[8,32,1024]{2,1,0:T(8,128)} %collective-permute-done.2, f32[]{:T(128)S(6)} %sub.92, ...), kind=kLoop, calls=%fused_computation.84 | loop fusion | flops 3145728 | bytes 8388616 | tf_op jit(solution)/shard_map/sub | solution.py:211
  75.6 1.4 collective-permute-start.4
  80.7 4.6 %broadcast_select_fusion = (f32[8,32,1024]{2,1,0:T(8,128)S(1)}, f32[8,32,1024]{2,1,0:T(8,128)S(1)}, f32[8,32,1024]{2,1,0:T(8,128)}) fusion(pred[]{:T(512)S(6)} %eq.84, f32[8,32,1024]{2,1,0:T(8,128)} %fusion.82, f32[8,32,1024]{2,1,0:T(8,128)} %collective-permute-done.4, f32[1,8,32,1024]{3,2,1,0:T(8,128)} %param.18, f32[1,8,32,1024]{3,2,1,0:T(8,128)S(1)} %copy-done.4, ...), kind=kLoop, calls=%fused_computation.114 | loop fusion | flops 2621440 | bytes 11534341 | tf_op jit(solution)/shard_map/jit(_where)/select_n | solution.py:177
  86.9 3.0 %multiply_reduce_fusion = bf16[128,8,128]{2,1,0:T(8,128)(2,1)S(1)} fusion(s32[128,128]{1,0:T(8,128)S(1)} %get-tuple-element.37, bf16[128,8,8,128]{3,2,0,1:T(8,128)(2,1)S(1)} %bitcast.249, bf16[128,8,128]{2,1,0:T(8,128)(2,1)S(1)} %copy-done.19), kind=kOutput, calls=%fused_computation.27 | convolution fusion | flops 272498688 | bytes 2686976 | tf_op jit(solution)/shard_map/slab,sbj->slaj/dot_general | solution.py:56
  90.6 2.9 %collective-permute-start.5 = (f32[8,2,1024]{2,1,0:T(2,128)}, f32[8,2,1024]{2,1,0:T(2,128)}, u32[]{:S(2)}, u32[]{:S(2)}) collective-permute-start(f32[8,2,1024]{2,1,0:T(2,128)} %get-tuple-element.30), channel_id=1, source_target_pairs={{0,1},{1,2},{2,3},{3,4},{4,5},{5,6},{6,7},{7,8},{8,9},{9,10},{10,1... | collective-permute-start | bytes 196616 | tf_op jit(solution)/shard_map/ppermute | solution.py:18
  95.8 8.8 %all-to-all-start.2 = ((bf16[64,16,256]{2,1,0:T(8,128)(2,1)}), bf16[64,16,256]{2,1,0:T(8,128)(2,1)}, u32[]{:S(2)}, u32[]{:S(2)}) async-start(bf16[64,16,256]{2,1,0:T(8,128)(2,1)} %pad_maximum_fusion.2), calls=%async_computation.2 | async-start | bytes 1048576 | tf_op jit(solution)/shard_map/all_to_all | solution.py:160
  104.6 1.7 %maximum_multiply_fusion = f32[8,36,1024]{2,1,0:T(8,128)S(1)} fusion(f32[8,2,1024]{2,1,0:T(2,128)} %collective-permute-done.6, f32[8,32,1024]{2,1,0:T(8,128)S(1)} %copy-done.12, f32[8,2,1024]{2,1,0:T(2,128)} %collective-permute-done.5, f32[2,8,36,1024]{3,2,1,0:T(8,128)} %copy-done.3), kind=kLoop, calls=%fused_computation.53 | loop fusion | flops 884736 | bytes 3538944 | tf_op jit(solution)/shard_map/mul | solution.py:35
  108.6 1.7 %fusion.73 = f32[8,32,1024]{2,1,0:T(8,128)} fusion(f32[8,34,1024]{2,1,0:T(8,128)S(1)} %multiply_multiply_fusion, f32[8,32,1023]{2,1,0:T(8,128)S(1)} %get-tuple-element.15, f32[8,32,1]{2,1,0:T(8,128)S(1)} %get-tuple-element.17, f32[8,32,1]{2,1,0:T(8,128)S(1)} %get-tuple-element.16, f32[8,32,1023]{2,1,0:T(8,128)S(1)} %get-tuple-element.14, ...), kind=kLoop, calls=%fused_computation.70 | loop fusion | flops 2621440 | bytes 7340064 | tf_op jit(solution)/shard_map/mul | solution.py:44
  110.3 2.7 %collective-permute-start.7 = (f32[8,32,1024]{2,1,0:T(8,128)}, f32[8,32,1024]{2,1,0:T(8,128)}, u32[]{:S(2)}, u32[]{:S(2)}) collective-permute-start(f32[8,32,1024]{2,1,0:T(8,128)} %fusion.73), channel_id=1, source_target_pairs={{0,64},{64,0},{1,65},{65,1},{2,66},{66,2},{3,67},{67,3},{4,68},{68... | collective-permute-start | bytes 3145736 | tf_op jit(solution)/shard_map/ppermute | solution.py:184
  113.0 2.4 %all-to-all-done.2 = bf16[64,16,256]{2,1,0:T(8,128)(2,1)} async-done(((bf16[64,16,256]{2,1,0:T(8,128)(2,1)}), bf16[64,16,256]{2,1,0:T(8,128)(2,1)}, u32[]{:S(2)}, u32[]{:S(2)}) %all-to-all-start.2) | async-done | bytes 524320 | tf_op jit(solution)/shard_map/all_to_all | solution.py:160
  116.8 2.9 %fusion.34 = bf16[128,8,8,128]{3,2,1,0:T(8,128)(2,1)S(1)} fusion(s32[128,128]{1,0:T(8,128)S(1)} %get-tuple-element.37, bf16[128,8,128]{2,1,0:T(8,128)(2,1)S(1)} %bitcast.258, bf16[128,8,128]{2,1,0:T(8,128)(2,1)S(1)} %copy-done.20), kind=kOutput, calls=%fused_computation.33 | convolution fusion | flops 272629760 | bytes 2686976 | tf_op jit(solution)/shard_map/slaj,sbj->slab/dot_general | solution.py:66
  121.3 1.7 %bitcast_multiply_fusion.5 = f32[8,32,1024]{2,1,0:T(8,128)S(1)} fusion(f32[1,8,32,1024]{3,2,1,0:T(8,128)S(1)} %copy-done.9, f32[8,8,4,8,128]{4,3,2,1,0:T(8,128)S(1)} %fusion.50, f32[8,32,1024]{2,1,0:T(8,128)S(1)} %copy-done.10, f32[8,32,1024]{2,1,0:T(8,128)} %collective-permute-done.7, f32[]{:T(128)S(6)} %sub.85), kind=kLoop, calls=%fused_computation.89 | loop fusion | flops 1310720 | bytes 5242884 | tf_op jit(solution)/shard_map/mul | solution.py:188
  123.0 5.7 %collective-permute-start.8 = (f32[8,32,1024]{2,1,0:T(8,128)S(1)}, f32[8,32,1024]{2,1,0:T(8,128)S(1)}, u32[]{:S(2)}, u32[]{:S(2)}) collective-permute-start(f32[8,32,1024]{2,1,0:T(8,128)S(1)} %bitcast_multiply_fusion.5), channel_id=1, source_target_pairs={{64,0},{65,1},{66,2},{67,3},{68,4},{69,5},{70,6},{71,7},{72,8},{73... | collective-permute-start | bytes 3145736 | tf_op jit(solution)/shard_map/ppermute | solution.py:29
  128.7 2.2 %collective-permute-done.8 = f32[8,32,1024]{2,1,0:T(8,128)S(1)} collective-permute-done((f32[8,32,1024]{2,1,0:T(8,128)S(1)}, f32[8,32,1024]{2,1,0:T(8,128)S(1)}, u32[]{:S(2)}, u32[]{:S(2)}) %collective-permute-start.8) | collective-permute-done | bytes 1048608 | tf_op jit(solution)/shard_map/ppermute | solution.py:29
  130.9 3.3 %fusion.85 = (f32[8,32,1024]{2,1,0:T(8,128)}, f32[1,8,32,1024]{3,2,1,0:T(8,128)}) fusion(f32[8,32,1024]{2,1,0:T(8,128)S(1)} %copy-done.10, f32[1,8,32,1024]{3,2,1,0:T(8,128)S(1)} %copy-done.13, f32[1,8,32,1024]{3,2,1,0:T(8,128)S(1)} %copy-done.14, f32[8,32,1024]{2,1,0:T(8,128)S(1)} %get-tuple-element.8, f32[8,32,1024]{2,1,0:T(8,128)} %collective-permute-done.7, ...), kind=kLoop, calls=%fused_computation.87 | loop fusion | flops 3407872 | bytes 9437192 | tf_op jit(solution)/shard_map/sub | solution.py:211
  135.8 3.4 %fusion.9 = f32[16,1,128]{2,1,0:T(1,128)S(1)} fusion(bf16[16,1024,1]{1,2,0:T(2,128)(2,1)S(1)} %copy.54, bf16[1,16,128,1024]{3,2,1,0:T(8,128)(2,1)} %param.23), kind=kOutput, calls=%fused_computation.7 | convolution fusion | flops 4194304 | bytes 4235264 | tf_op jit(solution)/shard_map/toj,tj->to/dot_general | solution.py:191
  139.8 2.7 %fusion.90 = f32[1,8,32,1024]{3,2,1,0:T(8,128)} fusion(f32[8,32,1024]{2,1,0:T(8,128)S(1)} %get-tuple-element.8, f32[8,32,1024]{2,1,0:T(8,128)} %get-tuple-element.10, f32[8,32,1024]{2,1,0:T(8,128)S(1)} %collective-permute-done.9, f32[1,8,32,1024]{3,2,1,0:T(8,128)S(1)} %copy-done.9), kind=kLoop, calls=%fused_computation.96 | loop fusion | flops 786432 | bytes 5242880 | tf_op jit(solution)/shard_map/broadcast_in_dim | solution.py:216
  (130 shorter events, 31.5 us)
Async XLA Ops:
  0.6 8.6 %copy-start = (s32[1,16,128]{2,1,0:T(8,128)S(1)}, s32[1,16,128]{2,1,0:T(8,128)}, u32[]{:S(2)}) copy-start(s32[1,16,128]{2,1,0:T(8,128)} %param.22) | copy-start | bytes 24580
  2.1 6.8 %copy-start.33 = (s32[1,16]{1,0:T(1,128)S(1)}, s32[1,16]{1,0:T(1,128)}, u32[]{:S(2)}) copy-start(s32[1,16]{1,0:T(1,128)} %param.21) | copy-start | bytes 196
  2.1 19.9 %copy-start.21 = (bf16[1,16,128]{2,1,0:T(8,128)(2,1)S(1)}, bf16[1,16,128]{2,1,0:T(8,128)(2,1)}, u32[]{:S(2)}) copy-start(bf16[1,16,128]{2,1,0:T(8,128)(2,1)} %param.15) | copy-start | bytes 12292
  3.0 39.0 %collective-permute-start = (f32[2,8,2,1024]{3,2,1,0:T(2,128)}, f32[2,8,2,1024]{3,2,1,0:T(2,128)}, u32[]{:S(2)}, u32[]{:S(2)}) collective-permute-start(f32[2,8,2,1024]{3,2,1,0:T(2,128)} %get-tuple-element.12), channel_id=1, source_target_pairs={{0,1},{1,2},{2,3},{3,4},{4,5},{5,6},{6,7},{7,8},{8,9},{9,10},{10,1... | collective-permute-start | bytes 393224 | tf_op jit(solution)/shard_map/ppermute | solution.py:18
  7.6 34.4 %collective-permute-start.1 = (f32[2,8,2,1024]{3,2,1,0:T(2,128)}, f32[2,8,2,1024]{3,2,1,0:T(2,128)}, u32[]{:S(2)}, u32[]{:S(2)}) collective-permute-start(f32[2,8,2,1024]{3,2,1,0:T(2,128)} %get-tuple-element.13), channel_id=1, source_target_pairs={{1,0},{2,1},{3,2},{4,3},{5,4},{6,5},{7,6},{8,7},{9,8},{10,9},{11,1... | collective-permute-start | bytes 393224 | tf_op jit(solution)/shard_map/ppermute | solution.py:20
  10.5 20.0 %all-to-all-start = ((s32[64,2,128]{2,1,0:T(2,128)}), s32[64,2,128]{2,1,0:T(2,128)S(1)}, u32[]{:S(2)}, u32[]{:S(2)}) async-start(s32[64,2,128]{2,1,0:T(2,128)} %bitcast.9), calls=%async_computation | async-start | bytes 131072 | tf_op jit(solution)/shard_map/all_to_all | solution.py:121
  22.0 46.0 %copy-start.30 = (s32[16]{0:T(128)}, s32[16]{0:T(128)S(1)}, u32[]{:S(2)}) copy-start(s32[16]{0:T(128)S(1)} %multiply_add_fusion) | copy-start | bytes 196
  24.9 5.8 %copy-start.4 = (f32[1,8,32,1024]{3,2,1,0:T(8,128)S(1)}, f32[1,8,32,1024]{3,2,1,0:T(8,128)}, u32[]{:S(2)}) copy-start(f32[1,8,32,1024]{3,2,1,0:T(8,128)} %param.13) | copy-start | bytes 3145732
  30.6 27.0 %copy-start.25 = (s32[128]{0:T(128)}, s32[128]{0:T(128)S(1)}, u32[]{:S(2)}) copy-start(s32[128]{0:T(128)S(1)} %fusion.104) | copy-start | bytes 1540
  32.1 3.0 %copy-start.16 = (bf16[128,8,128]{2,1,0:T(8,128)(2,1)S(1)}, bf16[128,8,128]{2,1,0:T(8,128)(2,1)}, u32[]{:S(2)}) copy-start(bf16[128,8,128]{2,1,0:T(8,128)(2,1)} %copy.34) | copy-start | bytes 786436
  36.0 16.9 %all-to-all-start.1 = ((bf16[64,16,256]{2,1,0:T(8,128)(2,1)}), bf16[64,16,256]{2,1,0:T(8,128)(2,1)}, u32[]{:S(2)}, u32[]{:S(2)}) async-start(bf16[64,16,256]{2,1,0:T(8,128)(2,1)} %pad_maximum_fusion.1), calls=%async_computation.1 | async-start | bytes 1048576 | tf_op jit(solution)/shard_map/all_to_all | solution.py:160
  47.1 7.6 %copy-start.18 = (bf16[128,8,128]{2,1,0:T(8,128)(2,1)S(1)}, bf16[128,8,128]{2,1,0:T(8,128)(2,1)}, u32[]{:S(2)}) copy-start(bf16[128,8,128]{2,1,0:T(8,128)(2,1)} %copy-done.17) | copy-start | bytes 786436
  48.8 10.2 %collective-permute-start.2 = (f32[8,32,1024]{2,1,0:T(8,128)}, f32[8,32,1024]{2,1,0:T(8,128)}, u32[]{:S(2)}, u32[]{:S(2)}) collective-permute-start(f32[8,32,1024]{2,1,0:T(8,128)} %fusion.79), channel_id=1, source_target_pairs={{0,64},{64,0},{1,65},{65,1},{2,66},{66,2},{3,67},{67,3},{4,68},{68... | collective-permute-start | bytes 3145736 | tf_op jit(solution)/shard_map/ppermute | solution.py:184
  59.0 2.9 %copy-start.7 = (f32[8,8,4,8,128]{4,3,2,1,0:T(8,128)}, f32[8,8,4,8,128]{4,3,2,1,0:T(8,128)S(1)}, u32[]{:S(2)}) copy-start(f32[8,8,4,8,128]{4,3,2,1,0:T(8,128)S(1)} %fusion.47) | copy-start | bytes 3145732
  61.9 9.3 %collective-permute-start.3 = (f32[8,32,1024]{2,1,0:T(8,128)}, f32[8,32,1024]{2,1,0:T(8,128)}, u32[]{:S(2)}, u32[]{:S(2)}) collective-permute-start(f32[8,32,1024]{2,1,0:T(8,128)} %bitcast_multiply_fusion.7), channel_id=1, source_target_pairs={{64,0},{65,1},{66,2},{67,3},{68,4},{69,5},{70,6},{71,7},{72,8},{73... | collective-permute-start | bytes 3145736 | tf_op jit(solution)/shard_map/ppermute | solution.py:29
  71.2 5.9 %copy-start.2 = (bf16[1,16,128,1024]{3,2,1,0:T(8,128)(2,1)S(1)}, bf16[1,16,128,1024]{3,2,1,0:T(8,128)(2,1)}, u32[]{:S(2)}) copy-start(bf16[1,16,128,1024]{3,2,1,0:T(8,128)(2,1)} %param.23) | copy-start | bytes 12582916
  75.6 5.0 %collective-permute-start.4 = (f32[8,32,1024]{2,1,0:T(8,128)}, f32[8,32,1024]{2,1,0:T(8,128)}, u32[]{:S(2)}, u32[]{:S(2)}) collective-permute-start(f32[8,32,1024]{2,1,0:T(8,128)} %fusion.82), channel_id=1, source_target_pairs={{0,64},{1,65},{2,66},{3,67},{4,68},{5,69},{6,70},{7,71},{8,72},{9,... | collective-permute-start | bytes 3145736 | tf_op jit(solution)/shard_map/ppermute | solution.py:29
  79.7 5.5 %copy-start.26 = (s32[128]{0:T(128)S(1)}, s32[128]{0:T(128)}, u32[]{:S(2)}) copy-start(s32[128]{0:T(128)} %copy-done.25) | copy-start | bytes 1540
  85.2 4.7 %copy-start.11 = (f32[8,32,1024]{2,1,0:T(8,128)}, f32[8,32,1024]{2,1,0:T(8,128)S(1)}, u32[]{:S(2)}) copy-start(f32[8,32,1024]{2,1,0:T(8,128)S(1)} %get-tuple-element.7) | copy-start | bytes 3145732
  90.6 13.9 %copy-start.12 = (f32[8,32,1024]{2,1,0:T(8,128)S(1)}, f32[8,32,1024]{2,1,0:T(8,128)}, u32[]{:S(2)}) copy-start(f32[8,32,1024]{2,1,0:T(8,128)} %copy-done.11) | copy-start | bytes 3145732
  90.6 13.9 %collective-permute-start.5 = (f32[8,2,1024]{2,1,0:T(2,128)}, f32[8,2,1024]{2,1,0:T(2,128)}, u32[]{:S(2)}, u32[]{:S(2)}) collective-permute-start(f32[8,2,1024]{2,1,0:T(2,128)} %get-tuple-element.30), channel_id=1, source_target_pairs={{0,1},{1,2},{2,3},{3,4},{4,5},{5,6},{6,7},{7,8},{8,9},{9,10},{10,1... | collective-permute-start | bytes 196616 | tf_op jit(solution)/shard_map/ppermute | solution.py:18
  93.6 11.0 %collective-permute-start.6 = (f32[8,2,1024]{2,1,0:T(2,128)S(1)}, f32[8,2,1024]{2,1,0:T(2,128)}, u32[]{:S(2)}, u32[]{:S(2)}) collective-permute-start(f32[8,2,1024]{2,1,0:T(2,128)S(1)} %get-tuple-element.31), channel_id=1, source_target_pairs={{1,0},{2,1},{3,2},{4,3},{5,4},{6,5},{7,6},{8,7},{9,8},{10,9},{11,1... | collective-permute-start | bytes 196616 | tf_op jit(solution)/shard_map/ppermute | solution.py:20
  95.8 19.6 %all-to-all-start.2 = ((bf16[64,16,256]{2,1,0:T(8,128)(2,1)}), bf16[64,16,256]{2,1,0:T(8,128)(2,1)}, u32[]{:S(2)}, u32[]{:S(2)}) async-start(bf16[64,16,256]{2,1,0:T(8,128)(2,1)} %pad_maximum_fusion.2), calls=%async_computation.2 | async-start | bytes 1048576 | tf_op jit(solution)/shard_map/all_to_all | solution.py:160
  108.6 7.8 %copy-start.32 = (s32[16]{0:T(128)S(1)}, s32[16]{0:T(128)}, u32[]{:S(2)}) copy-start(s32[16]{0:T(128)} %copy-done.30) | copy-start | bytes 196
  110.3 6.5 %copy-start.20 = (bf16[128,8,128]{2,1,0:T(8,128)(2,1)S(1)}, bf16[128,8,128]{2,1,0:T(8,128)(2,1)}, u32[]{:S(2)}) copy-start(bf16[128,8,128]{2,1,0:T(8,128)(2,1)} %copy-done.17) | copy-start | bytes 786436
  110.3 10.8 %collective-permute-start.7 = (f32[8,32,1024]{2,1,0:T(8,128)}, f32[8,32,1024]{2,1,0:T(8,128)}, u32[]{:S(2)}, u32[]{:S(2)}) collective-permute-start(f32[8,32,1024]{2,1,0:T(8,128)} %fusion.73), channel_id=1, source_target_pairs={{0,64},{64,0},{1,65},{65,1},{2,66},{66,2},{3,67},{67,3},{4,68},{68... | collective-permute-start | bytes 3145736 | tf_op jit(solution)/shard_map/ppermute | solution.py:184
  116.8 2.9 %copy-start.27 = (s32[128]{0:T(128)S(1)}, s32[128]{0:T(128)}, u32[]{:S(2)}) copy-start(s32[128]{0:T(128)} %copy-done.25) | copy-start | bytes 1540
  121.3 9.6 %copy-start.13 = (f32[1,8,32,1024]{3,2,1,0:T(8,128)S(1)}, f32[1,8,32,1024]{3,2,1,0:T(8,128)}, u32[]{:S(2)}) copy-start(f32[1,8,32,1024]{3,2,1,0:T(8,128)} %param.17) | copy-start | bytes 3145732
  121.3 9.6 %copy-start.14 = (f32[1,8,32,1024]{3,2,1,0:T(8,128)S(1)}, f32[1,8,32,1024]{3,2,1,0:T(8,128)}, u32[]{:S(2)}) copy-start(f32[1,8,32,1024]{3,2,1,0:T(8,128)} %param.16) | copy-start | bytes 3145732
  123.0 7.9 %collective-permute-start.8 = (f32[8,32,1024]{2,1,0:T(8,128)S(1)}, f32[8,32,1024]{2,1,0:T(8,128)S(1)}, u32[]{:S(2)}, u32[]{:S(2)}) collective-permute-start(f32[8,32,1024]{2,1,0:T(8,128)S(1)} %bitcast_multiply_fusion.5), channel_id=1, source_target_pairs={{64,0},{65,1},{66,2},{67,3},{68,4},{69,5},{70,6},{71,7},{72,8},{73... | collective-permute-start | bytes 3145736 | tf_op jit(solution)/shard_map/ppermute | solution.py:29
  134.2 5.5 %collective-permute-start.9 = (f32[8,32,1024]{2,1,0:T(8,128)}, f32[8,32,1024]{2,1,0:T(8,128)S(1)}, u32[]{:S(2)}, u32[]{:S(2)}) collective-permute-start(f32[8,32,1024]{2,1,0:T(8,128)} %get-tuple-element.10), channel_id=1, source_target_pairs={{0,64},{1,65},{2,66},{3,67},{4,68},{5,69},{6,70},{7,71},{8,72},{9,... | collective-permute-start | bytes 3145736 | tf_op jit(solution)/shard_map/ppermute | solution.py:29
  135.7 3.4 %copy-start.24 = (bf16[1,16,128]{2,1,0:T(8,128)(2,1)S(1)}, bf16[1,16,128]{2,1,0:T(8,128)(2,1)}, u32[]{:S(2)}) copy-start(bf16[1,16,128]{2,1,0:T(8,128)(2,1)} %param.24) | copy-start | bytes 12292
  (15 other events, 22.9 us)

commit v7 on v6

--- a/solution.py
+++ b/solution.py
@@ -63,10 +63,8 @@
     row_count = row_oh.shape[1]
     grads = values.reshape(slots, levels, 1, touched)
     placed = grads * group_mask[:, None, :, :].astype(jnp.bfloat16)
-    lines = jnp.einsum("slaj,sbj->slab", placed, col_oh, preferred_element_type=jnp.float32)
-    total = jnp.einsum(
-        "sr,slab->lrab", row_oh, lines.astype(jnp.bfloat16), preferred_element_type=jnp.float32
-    )
+    lines = jnp.einsum("slaj,sbj->slab", placed, col_oh, preferred_element_type=jnp.bfloat16)
+    total = jnp.einsum("sr,slab->lrab", row_oh, lines, preferred_element_type=jnp.float32)
     return total.reshape(levels, row_count, groups * lanes)
 
 

time: 143 us -> 143 us (level)
  no operation moved by 1% of the time
where the time goes in v7:
time: 143 us; the launch traced here: 142 us
  starting transfers between devices  55.7 us (39%)
  other arithmetic  33.2 us (23%)
  matrix products  26.1 us (18%)
  local copies, waits for them, and re-layouts  14.5 us (10%)
  waiting for transfers between devices  11.5 us (8%)
    all_to_all x2, starting transfers between devices, on_device(): got = lax.all_to_all(both, 'space', split_axis=0, concat_axis=0, tiled=True)  14.7 us
    ppermute x4, starting transfers between devices, shifted(): return lax.ppermute(value, axis, pairs)  14.4 us
    all_to_all x1, starting transfers between devices, on_device(): lax.all_to_all(packed_cells.reshape(owners_count, capacity, touched), 'sp...  11.5 us
    sub x2, other arithmetic, on_device(): source = r_model - err_field * upward  7.76 us
    ppermute x2, starting transfers between devices, with_halo(): lax.ppermute(tail, axis, [(i, i + 1) for i in range(ends)])  7.56 us
    dot_general x2, matrix products, gather_cols(): jnp.einsum('slab,sbj->slaj', lines, col_oh, preferred_element_type=jnp.bf...  6.06 us
    select_n x2, other arithmetic, on_device(): chosen = jnp.where(tm_here == 0, increment, dual_model)  6.02 us
    dot_general x2, matrix products, spread_cols(): jnp.einsum('slaj,sbj->slab', placed, col_oh, preferred_element_type=jnp.b...  5.79 us
  transfers between devices with their start and end apart: 13, of which 5 were waited for; matrix products, arithmetic and copies ran while one was open for 32% of the time, Pallas kernels for 0%

profile of v7, /device:TPU:1, one launch (start us, length us, event | category | flops | bytes accessed | tf_op | source)
XLA Modules:
  0.0 142.4 jit_solution(11231457942130401011)
XLA Ops:
  0.7 1.5 %broadcast_select_fusion.1 = f32[1,8,32,1024]{3,2,1,0:T(8,128)S(1)} fusion(f32[1,8,32,1024]{3,2,1,0:T(8,128)} %param.13, f32[1,8,32,1024]{3,2,1,0:T(8,128)} %param.14, pred[]{:T(512)S(6)} %eq.84), kind=kLoop, calls=%fused_computation.113 | loop fusion | flops 262144 | bytes 3145729 | tf_op jit(solution)/shard_map/jit(_where)/select_n | solution.py:175
  3.0 4.6 %collective-permute-start = (f32[2,8,2,1024]{3,2,1,0:T(2,128)}, f32[2,8,2,1024]{3,2,1,0:T(2,128)}, u32[]{:S(2)}, u32[]{:S(2)}) collective-permute-start(f32[2,8,2,1024]{3,2,1,0:T(2,128)} %get-tuple-element.12), channel_id=1, source_target_pairs={{0,1},{1,2},{2,3},{3,4},{4,5},{5,6},{6,7},{7,8},{8,9},{9,10},{10,1... | collective-permute-start | bytes 393224 | tf_op jit(solution)/shard_map/ppermute | solution.py:18
  10.5 11.5 %all-to-all-start = ((s32[64,2,128]{2,1,0:T(2,128)}), s32[64,2,128]{2,1,0:T(2,128)S(1)}, u32[]{:S(2)}, u32[]{:S(2)}) async-start(s32[64,2,128]{2,1,0:T(2,128)} %bitcast.9), calls=%async_computation | async-start | bytes 131072 | tf_op jit(solution)/shard_map/all_to_all | solution.py:119
  22.0 2.8 %fusion.15 = bf16[16,1,1024]{2,1,0:T(2,128)(2,1)S(1)} fusion(bf16[1,16,128,1024]{3,2,1,0:T(8,128)(2,1)} %param.23, bf16[16,128,1]{1,0,2:T(8,128)(2,1)S(1)} %bitcast.260), kind=kOutput, calls=%fused_computation.13 | convolution fusion | flops 4194304 | bytes 4231168 | tf_op jit(solution)/shard_map/toj,to->tj/dot_general | solution.py:142
  26.3 4.1 %all-to-all-done = s32[64,2,128]{2,1,0:T(2,128)S(1)} async-done(((s32[64,2,128]{2,1,0:T(2,128)}), s32[64,2,128]{2,1,0:T(2,128)S(1)}, u32[]{:S(2)}, u32[]{:S(2)}) %all-to-all-start) | async-done | bytes 65568 | tf_op jit(solution)/shard_map/all_to_all | solution.py:119
  32.1 3.0 %multiply_reduce_fusion.1 = bf16[128,8,128]{2,1,0:T(8,128)(2,1)S(1)} fusion(s32[128,128]{1,0:T(8,128)S(1)} %get-tuple-element.37, bf16[128,8,8,128]{3,2,0,1:T(8,128)(2,1)S(1)} %bitcast.244, bf16[128,8,128]{2,1,0:T(8,128)(2,1)S(1)} %convert_convert_fusion), kind=kOutput, calls=%fused_computation.29 | convolution fusion | flops 272498688 | bytes 2686976 | tf_op jit(solution)/shard_map/slab,sbj->slaj/dot_general | solution.py:56
  36.0 5.9 %all-to-all-start.1 = ((bf16[64,16,256]{2,1,0:T(8,128)(2,1)}), bf16[64,16,256]{2,1,0:T(8,128)(2,1)}, u32[]{:S(2)}, u32[]{:S(2)}) async-start(bf16[64,16,256]{2,1,0:T(8,128)(2,1)} %pad_maximum_fusion.1), calls=%async_computation.1 | async-start | bytes 1048576 | tf_op jit(solution)/shard_map/all_to_all | solution.py:158
  42.0 1.4 pad_maximum_fusion
  47.1 1.7 %fusion.69 = f32[8,32,1024]{2,1,0:T(8,128)} fusion(f32[8,34,1024]{2,1,0:T(8,128)S(1)} %multiply_multiply_fusion.1, f32[8,32,1023]{2,1,0:T(8,128)S(1)} %get-tuple-element.23, f32[8,32,1]{2,1,0:T(8,128)S(1)} %get-tuple-element.25, f32[8,32,1]{2,1,0:T(8,128)S(1)} %get-tuple-element.24, f32[8,32,1023]{2,1,0:T(8,128)S(1)} %get-tuple-element.22, ...), kind=kLoop, calls=%fused_computation.75 | loop fusion | flops 2621440 | bytes 7340064 | tf_op jit(solution)/shard_map/mul | solution.py:44
  48.8 2.2 %collective-permute-start.2 = (f32[8,32,1024]{2,1,0:T(8,128)}, f32[8,32,1024]{2,1,0:T(8,128)}, u32[]{:S(2)}, u32[]{:S(2)}) collective-permute-start(f32[8,32,1024]{2,1,0:T(8,128)} %fusion.69), channel_id=1, source_target_pairs={{0,64},{64,0},{1,65},{65,1},{2,66},{66,2},{3,67},{67,3},{4,68},{68... | collective-permute-start | bytes 3145736 | tf_op jit(solution)/shard_map/ppermute | solution.py:182
  51.0 1.9 %all-to-all-done.1 = bf16[64,16,256]{2,1,0:T(8,128)(2,1)} async-done(((bf16[64,16,256]{2,1,0:T(8,128)(2,1)}), bf16[64,16,256]{2,1,0:T(8,128)(2,1)}, u32[]{:S(2)}, u32[]{:S(2)}) %all-to-all-start.1) | async-done | bytes 524320 | tf_op jit(solution)/shard_map/all_to_all | solution.py:158
  52.9 1.8 %fusion.141 = (bf16[64,16,128]{2,1,0:T(8,128)(2,1)}, bf16[64,16,128]{2,1,0:T(8,128)(2,1)S(1)}) fusion(bf16[64,16,256]{2,1,0:T(8,128)(2,1)} %all-to-all-done.1), kind=kLoop, calls=%fused_computation.189 | loop fusion | bytes 1048576 | tf_op jit(solution)/shard_map/slice | solution.py:159
  54.7 2.9 %fusion.5 = bf16[128,8,8,128]{3,2,1,0:T(8,128)(2,1)S(1)} fusion(s32[128,128]{1,0:T(8,128)S(1)} %get-tuple-element.37, bf16[128,8,128]{2,1,0:T(8,128)(2,1)S(1)} %bitcast.256, bf16[128,8,128]{2,1,0:T(8,128)(2,1)S(1)} %copy-done.18), kind=kOutput, calls=%fused_computation.5 | convolution fusion | flops 271581184 | bytes 2686976 | tf_op jit(solution)/shard_map/slaj,sbj->slab/dot_general | solution.py:66
  59.2 2.7 %bitcast_multiply_fusion.7 = f32[8,32,1024]{2,1,0:T(8,128)} fusion(f32[1,8,32,1024]{3,2,1,0:T(8,128)S(1)} %copy-done.8, f32[8,8,4,8,128]{4,3,2,1,0:T(8,128)S(1)} %fusion.37, f32[8,32,1024]{2,1,0:T(8,128)} %collective-permute-done.2, f32[]{:T(128)S(6)} %sub.85, f32[1,8,32,1024]{3,2,1,0:T(8,128)S(1)} %copy-done.5), kind=kLoop, calls=%fused_computation.89 | loop fusion | flops 1310720 | bytes 5242884 | tf_op jit(solution)/shard_map/mul | solution.py:186
  61.9 6.1 %collective-permute-start.3 = (f32[8,32,1024]{2,1,0:T(8,128)}, f32[8,32,1024]{2,1,0:T(8,128)}, u32[]{:S(2)}, u32[]{:S(2)}) collective-permute-start(f32[8,32,1024]{2,1,0:T(8,128)} %bitcast_multiply_fusion.7), channel_id=1, source_target_pairs={{64,0},{65,1},{66,2},{67,3},{68,4},{69,5},{70,6},{71,7},{72,8},{73... | collective-permute-start | bytes 3145736 | tf_op jit(solution)/shard_map/ppermute | solution.py:29
  71.2 4.4 %fusion.72 = f32[8,32,1024]{2,1,0:T(8,128)} fusion(f32[1,8,32,1024]{3,2,1,0:T(8,128)} %param.17, f32[1,8,32,1024]{3,2,1,0:T(8,128)} %param.16, f32[1,8,32,1024]{3,2,1,0:T(8,128)S(1)} %copy-done.4, f32[1,8,32,1024]{3,2,1,0:T(8,128)S(1)} %copy-done.5, f32[8,32,1024]{2,1,0:T(8,128)} %collective-permute-done.2, f32[]{:T(128)S(6)} %sub.92, ...), kind=kLoop, calls=%fused_computation.82 | loop fusion | flops 3145728 | bytes 8388616 | tf_op jit(solution)/shard_map/sub | solution.py:209
  75.6 1.4 collective-permute-start.4
  80.7 4.6 %broadcast_select_fusion = (f32[8,32,1024]{2,1,0:T(8,128)S(1)}, f32[8,32,1024]{2,1,0:T(8,128)S(1)}, f32[8,32,1024]{2,1,0:T(8,128)}) fusion(pred[]{:T(512)S(6)} %eq.84, f32[8,32,1024]{2,1,0:T(8,128)} %fusion.72, f32[8,32,1024]{2,1,0:T(8,128)} %collective-permute-done.4, f32[1,8,32,1024]{3,2,1,0:T(8,128)} %param.18, f32[1,8,32,1024]{3,2,1,0:T(8,128)S(1)} %copy-done.4, ...), kind=kLoop, calls=%fused_computation.112 | loop fusion | flops 2621440 | bytes 11534341 | tf_op jit(solution)/shard_map/jit(_where)/select_n | solution.py:175
  86.9 3.0 %multiply_reduce_fusion = bf16[128,8,128]{2,1,0:T(8,128)(2,1)S(1)} fusion(s32[128,128]{1,0:T(8,128)S(1)} %get-tuple-element.37, bf16[128,8,8,128]{3,2,0,1:T(8,128)(2,1)S(1)} %bitcast.245, bf16[128,8,128]{2,1,0:T(8,128)(2,1)S(1)} %copy-done.19), kind=kOutput, calls=%fused_computation.27 | convolution fusion | flops 272498688 | bytes 2686976 | tf_op jit(solution)/shard_map/slab,sbj->slaj/dot_general | solution.py:56
  90.6 2.9 %collective-permute-start.5 = (f32[8,2,1024]{2,1,0:T(2,128)}, f32[8,2,1024]{2,1,0:T(2,128)}, u32[]{:S(2)}, u32[]{:S(2)}) collective-permute-start(f32[8,2,1024]{2,1,0:T(2,128)} %get-tuple-element.30), channel_id=1, source_target_pairs={{0,1},{1,2},{2,3},{3,4},{4,5},{5,6},{6,7},{7,8},{8,9},{9,10},{10,1... | collective-permute-start | bytes 196616 | tf_op jit(solution)/shard_map/ppermute | solution.py:18
  95.8 8.8 %all-to-all-start.2 = ((bf16[64,16,256]{2,1,0:T(8,128)(2,1)}), bf16[64,16,256]{2,1,0:T(8,128)(2,1)}, u32[]{:S(2)}, u32[]{:S(2)}) async-start(bf16[64,16,256]{2,1,0:T(8,128)(2,1)} %pad_maximum_fusion.2), calls=%async_computation.2 | async-start | bytes 1048576 | tf_op jit(solution)/shard_map/all_to_all | solution.py:158
  104.6 1.7 %maximum_multiply_fusion = f32[8,36,1024]{2,1,0:T(8,128)S(1)} fusion(f32[8,2,1024]{2,1,0:T(2,128)} %collective-permute-done.6, f32[8,32,1024]{2,1,0:T(8,128)S(1)} %copy-done.12, f32[8,2,1024]{2,1,0:T(2,128)} %collective-permute-done.5, f32[2,8,36,1024]{3,2,1,0:T(8,128)} %copy-done.3), kind=kLoop, calls=%fused_computation.51 | loop fusion | flops 884736 | bytes 3538944 | tf_op jit(solution)/shard_map/mul | solution.py:35
  108.6 1.7 %fusion.63 = f32[8,32,1024]{2,1,0:T(8,128)} fusion(f32[8,34,1024]{2,1,0:T(8,128)S(1)} %multiply_multiply_fusion, f32[8,32,1023]{2,1,0:T(8,128)S(1)} %get-tuple-element.15, f32[8,32,1]{2,1,0:T(8,128)S(1)} %get-tuple-element.17, f32[8,32,1]{2,1,0:T(8,128)S(1)} %get-tuple-element.16, f32[8,32,1023]{2,1,0:T(8,128)S(1)} %get-tuple-element.14, ...), kind=kLoop, calls=%fused_computation.68 | loop fusion | flops 2621440 | bytes 7340064 | tf_op jit(solution)/shard_map/mul | solution.py:44
  110.3 2.7 %collective-permute-start.7 = (f32[8,32,1024]{2,1,0:T(8,128)}, f32[8,32,1024]{2,1,0:T(8,128)}, u32[]{:S(2)}, u32[]{:S(2)}) collective-permute-start(f32[8,32,1024]{2,1,0:T(8,128)} %fusion.63), channel_id=1, source_target_pairs={{0,64},{64,0},{1,65},{65,1},{2,66},{66,2},{3,67},{67,3},{4,68},{68... | collective-permute-start | bytes 3145736 | tf_op jit(solution)/shard_map/ppermute | solution.py:182
  113.0 2.4 %all-to-all-done.2 = bf16[64,16,256]{2,1,0:T(8,128)(2,1)} async-done(((bf16[64,16,256]{2,1,0:T(8,128)(2,1)}), bf16[64,16,256]{2,1,0:T(8,128)(2,1)}, u32[]{:S(2)}, u32[]{:S(2)}) %all-to-all-start.2) | async-done | bytes 524320 | tf_op jit(solution)/shard_map/all_to_all | solution.py:158
  116.8 2.9 %fusion.1 = bf16[128,8,8,128]{3,2,1,0:T(8,128)(2,1)S(1)} fusion(s32[128,128]{1,0:T(8,128)S(1)} %get-tuple-element.37, bf16[128,8,128]{2,1,0:T(8,128)(2,1)S(1)} %bitcast.254, bf16[128,8,128]{2,1,0:T(8,128)(2,1)S(1)} %copy-done.20), kind=kOutput, calls=%fused_computation.3 | convolution fusion | flops 271581184 | bytes 2686976 | tf_op jit(solution)/shard_map/slaj,sbj->slab/dot_general | solution.py:66
  121.3 1.7 %bitcast_multiply_fusion.5 = f32[8,32,1024]{2,1,0:T(8,128)S(1)} fusion(f32[1,8,32,1024]{3,2,1,0:T(8,128)S(1)} %copy-done.9, f32[8,8,4,8,128]{4,3,2,1,0:T(8,128)S(1)} %fusion.40, f32[8,32,1024]{2,1,0:T(8,128)S(1)} %copy-done.10, f32[8,32,1024]{2,1,0:T(8,128)} %collective-permute-done.7, f32[]{:T(128)S(6)} %sub.85), kind=kLoop, calls=%fused_computation.87 | loop fusion | flops 1310720 | bytes 5242884 | tf_op jit(solution)/shard_map/mul | solution.py:186
  123.0 5.7 %collective-permute-start.8 = (f32[8,32,1024]{2,1,0:T(8,128)S(1)}, f32[8,32,1024]{2,1,0:T(8,128)S(1)}, u32[]{:S(2)}, u32[]{:S(2)}) collective-permute-start(f32[8,32,1024]{2,1,0:T(8,128)S(1)} %bitcast_multiply_fusion.5), channel_id=1, source_target_pairs={{64,0},{65,1},{66,2},{67,3},{68,4},{69,5},{70,6},{71,7},{72,8},{73... | collective-permute-start | bytes 3145736 | tf_op jit(solution)/shard_map/ppermute | solution.py:29
  128.7 2.2 %collective-permute-done.8 = f32[8,32,1024]{2,1,0:T(8,128)S(1)} collective-permute-done((f32[8,32,1024]{2,1,0:T(8,128)S(1)}, f32[8,32,1024]{2,1,0:T(8,128)S(1)}, u32[]{:S(2)}, u32[]{:S(2)}) %collective-permute-start.8) | collective-permute-done | bytes 1048608 | tf_op jit(solution)/shard_map/ppermute | solution.py:29
  130.9 3.3 %fusion.75 = (f32[8,32,1024]{2,1,0:T(8,128)}, f32[1,8,32,1024]{3,2,1,0:T(8,128)}) fusion(f32[8,32,1024]{2,1,0:T(8,128)S(1)} %copy-done.10, f32[1,8,32,1024]{3,2,1,0:T(8,128)S(1)} %copy-done.13, f32[1,8,32,1024]{3,2,1,0:T(8,128)S(1)} %copy-done.14, f32[8,32,1024]{2,1,0:T(8,128)S(1)} %get-tuple-element.8, f32[8,32,1024]{2,1,0:T(8,128)} %collective-permute-done.7, ...), kind=kLoop, calls=%fused_computation.85 | loop fusion | flops 3407872 | bytes 9437192 | tf_op jit(solution)/shard_map/sub | solution.py:209
  135.8 3.4 %fusion.9 = f32[16,1,128]{2,1,0:T(1,128)S(1)} fusion(bf16[16,1024,1]{1,2,0:T(2,128)(2,1)S(1)} %copy.54, bf16[1,16,128,1024]{3,2,1,0:T(8,128)(2,1)} %param.23), kind=kOutput, calls=%fused_computation.7 | convolution fusion | flops 4194304 | bytes 4235264 | tf_op jit(solution)/shard_map/toj,tj->to/dot_general | solution.py:189
  139.8 2.7 %fusion.80 = f32[1,8,32,1024]{3,2,1,0:T(8,128)} fusion(f32[8,32,1024]{2,1,0:T(8,128)S(1)} %get-tuple-element.8, f32[8,32,1024]{2,1,0:T(8,128)} %get-tuple-element.10, f32[8,32,1024]{2,1,0:T(8,128)S(1)} %collective-permute-done.9, f32[1,8,32,1024]{3,2,1,0:T(8,128)S(1)} %copy-done.9), kind=kLoop, calls=%fused_computation.94 | loop fusion | flops 786432 | bytes 5242880 | tf_op jit(solution)/shard_map/broadcast_in_dim | solution.py:214
  (130 shorter events, 31.5 us)
Async XLA Ops:
  0.6 8.6 %copy-start = (s32[1,16,128]{2,1,0:T(8,128)S(1)}, s32[1,16,128]{2,1,0:T(8,128)}, u32[]{:S(2)}) copy-start(s32[1,16,128]{2,1,0:T(8,128)} %param.22) | copy-start | bytes 24580
  2.1 6.8 %copy-start.33 = (s32[1,16]{1,0:T(1,128)S(1)}, s32[1,16]{1,0:T(1,128)}, u32[]{:S(2)}) copy-start(s32[1,16]{1,0:T(1,128)} %param.21) | copy-start | bytes 196
  2.1 19.9 %copy-start.21 = (bf16[1,16,128]{2,1,0:T(8,128)(2,1)S(1)}, bf16[1,16,128]{2,1,0:T(8,128)(2,1)}, u32[]{:S(2)}) copy-start(bf16[1,16,128]{2,1,0:T(8,128)(2,1)} %param.15) | copy-start | bytes 12292
  3.0 39.0 %collective-permute-start = (f32[2,8,2,1024]{3,2,1,0:T(2,128)}, f32[2,8,2,1024]{3,2,1,0:T(2,128)}, u32[]{:S(2)}, u32[]{:S(2)}) collective-permute-start(f32[2,8,2,1024]{3,2,1,0:T(2,128)} %get-tuple-element.12), channel_id=1, source_target_pairs={{0,1},{1,2},{2,3},{3,4},{4,5},{5,6},{6,7},{7,8},{8,9},{9,10},{10,1... | collective-permute-start | bytes 393224 | tf_op jit(solution)/shard_map/ppermute | solution.py:18
  7.6 34.4 %collective-permute-start.1 = (f32[2,8,2,1024]{3,2,1,0:T(2,128)}, f32[2,8,2,1024]{3,2,1,0:T(2,128)}, u32[]{:S(2)}, u32[]{:S(2)}) collective-permute-start(f32[2,8,2,1024]{3,2,1,0:T(2,128)} %get-tuple-element.13), channel_id=1, source_target_pairs={{1,0},{2,1},{3,2},{4,3},{5,4},{6,5},{7,6},{8,7},{9,8},{10,9},{11,1... | collective-permute-start | bytes 393224 | tf_op jit(solution)/shard_map/ppermute | solution.py:20
  10.5 20.0 %all-to-all-start = ((s32[64,2,128]{2,1,0:T(2,128)}), s32[64,2,128]{2,1,0:T(2,128)S(1)}, u32[]{:S(2)}, u32[]{:S(2)}) async-start(s32[64,2,128]{2,1,0:T(2,128)} %bitcast.9), calls=%async_computation | async-start | bytes 131072 | tf_op jit(solution)/shard_map/all_to_all | solution.py:119
  22.0 46.0 %copy-start.30 = (s32[16]{0:T(128)}, s32[16]{0:T(128)S(1)}, u32[]{:S(2)}) copy-start(s32[16]{0:T(128)S(1)} %multiply_add_fusion) | copy-start | bytes 196
  24.9 5.8 %copy-start.4 = (f32[1,8,32,1024]{3,2,1,0:T(8,128)S(1)}, f32[1,8,32,1024]{3,2,1,0:T(8,128)}, u32[]{:S(2)}) copy-start(f32[1,8,32,1024]{3,2,1,0:T(8,128)} %param.13) | copy-start | bytes 3145732
  30.6 27.0 %copy-start.25 = (s32[128]{0:T(128)}, s32[128]{0:T(128)S(1)}, u32[]{:S(2)}) copy-start(s32[128]{0:T(128)S(1)} %fusion.94) | copy-start | bytes 1540
  32.1 3.0 %copy-start.16 = (bf16[128,8,128]{2,1,0:T(8,128)(2,1)S(1)}, bf16[128,8,128]{2,1,0:T(8,128)(2,1)}, u32[]{:S(2)}) copy-start(bf16[128,8,128]{2,1,0:T(8,128)(2,1)} %copy.34) | copy-start | bytes 786436
  36.0 16.9 %all-to-all-start.1 = ((bf16[64,16,256]{2,1,0:T(8,128)(2,1)}), bf16[64,16,256]{2,1,0:T(8,128)(2,1)}, u32[]{:S(2)}, u32[]{:S(2)}) async-start(bf16[64,16,256]{2,1,0:T(8,128)(2,1)} %pad_maximum_fusion.1), calls=%async_computation.1 | async-start | bytes 1048576 | tf_op jit(solution)/shard_map/all_to_all | solution.py:158
  47.1 7.6 %copy-start.18 = (bf16[128,8,128]{2,1,0:T(8,128)(2,1)S(1)}, bf16[128,8,128]{2,1,0:T(8,128)(2,1)}, u32[]{:S(2)}) copy-start(bf16[128,8,128]{2,1,0:T(8,128)(2,1)} %copy-done.17) | copy-start | bytes 786436
  48.8 10.2 %collective-permute-start.2 = (f32[8,32,1024]{2,1,0:T(8,128)}, f32[8,32,1024]{2,1,0:T(8,128)}, u32[]{:S(2)}, u32[]{:S(2)}) collective-permute-start(f32[8,32,1024]{2,1,0:T(8,128)} %fusion.69), channel_id=1, source_target_pairs={{0,64},{64,0},{1,65},{65,1},{2,66},{66,2},{3,67},{67,3},{4,68},{68... | collective-permute-start | bytes 3145736 | tf_op jit(solution)/shard_map/ppermute | solution.py:182
  59.0 2.9 %copy-start.7 = (f32[8,8,4,8,128]{4,3,2,1,0:T(8,128)}, f32[8,8,4,8,128]{4,3,2,1,0:T(8,128)S(1)}, u32[]{:S(2)}) copy-start(f32[8,8,4,8,128]{4,3,2,1,0:T(8,128)S(1)} %fusion.37) | copy-start | bytes 3145732
  61.9 9.3 %collective-permute-start.3 = (f32[8,32,1024]{2,1,0:T(8,128)}, f32[8,32,1024]{2,1,0:T(8,128)}, u32[]{:S(2)}, u32[]{:S(2)}) collective-permute-start(f32[8,32,1024]{2,1,0:T(8,128)} %bitcast_multiply_fusion.7), channel_id=1, source_target_pairs={{64,0},{65,1},{66,2},{67,3},{68,4},{69,5},{70,6},{71,7},{72,8},{73... | collective-permute-start | bytes 3145736 | tf_op jit(solution)/shard_map/ppermute | solution.py:29
  71.2 5.9 %copy-start.2 = (bf16[1,16,128,1024]{3,2,1,0:T(8,128)(2,1)S(1)}, bf16[1,16,128,1024]{3,2,1,0:T(8,128)(2,1)}, u32[]{:S(2)}) copy-start(bf16[1,16,128,1024]{3,2,1,0:T(8,128)(2,1)} %param.23) | copy-start | bytes 12582916
  75.6 5.0 %collective-permute-start.4 = (f32[8,32,1024]{2,1,0:T(8,128)}, f32[8,32,1024]{2,1,0:T(8,128)}, u32[]{:S(2)}, u32[]{:S(2)}) collective-permute-start(f32[8,32,1024]{2,1,0:T(8,128)} %fusion.72), channel_id=1, source_target_pairs={{0,64},{1,65},{2,66},{3,67},{4,68},{5,69},{6,70},{7,71},{8,72},{9,... | collective-permute-start | bytes 3145736 | tf_op jit(solution)/shard_map/ppermute | solution.py:29
  79.7 5.5 %copy-start.26 = (s32[128]{0:T(128)S(1)}, s32[128]{0:T(128)}, u32[]{:S(2)}) copy-start(s32[128]{0:T(128)} %copy-done.25) | copy-start | bytes 1540
  85.2 4.7 %copy-start.11 = (f32[8,32,1024]{2,1,0:T(8,128)}, f32[8,32,1024]{2,1,0:T(8,128)S(1)}, u32[]{:S(2)}) copy-start(f32[8,32,1024]{2,1,0:T(8,128)S(1)} %get-tuple-element.7) | copy-start | bytes 3145732
  90.6 13.9 %copy-start.12 = (f32[8,32,1024]{2,1,0:T(8,128)S(1)}, f32[8,32,1024]{2,1,0:T(8,128)}, u32[]{:S(2)}) copy-start(f32[8,32,1024]{2,1,0:T(8,128)} %copy-done.11) | copy-start | bytes 3145732
  90.6 13.9 %collective-permute-start.5 = (f32[8,2,1024]{2,1,0:T(2,128)}, f32[8,2,1024]{2,1,0:T(2,128)}, u32[]{:S(2)}, u32[]{:S(2)}) collective-permute-start(f32[8,2,1024]{2,1,0:T(2,128)} %get-tuple-element.30), channel_id=1, source_target_pairs={{0,1},{1,2},{2,3},{3,4},{4,5},{5,6},{6,7},{7,8},{8,9},{9,10},{10,1... | collective-permute-start | bytes 196616 | tf_op jit(solution)/shard_map/ppermute | solution.py:18
  93.6 11.0 %collective-permute-start.6 = (f32[8,2,1024]{2,1,0:T(2,128)S(1)}, f32[8,2,1024]{2,1,0:T(2,128)}, u32[]{:S(2)}, u32[]{:S(2)}) collective-permute-start(f32[8,2,1024]{2,1,0:T(2,128)S(1)} %get-tuple-element.31), channel_id=1, source_target_pairs={{1,0},{2,1},{3,2},{4,3},{5,4},{6,5},{7,6},{8,7},{9,8},{10,9},{11,1... | collective-permute-start | bytes 196616 | tf_op jit(solution)/shard_map/ppermute | solution.py:20
  95.8 19.6 %all-to-all-start.2 = ((bf16[64,16,256]{2,1,0:T(8,128)(2,1)}), bf16[64,16,256]{2,1,0:T(8,128)(2,1)}, u32[]{:S(2)}, u32[]{:S(2)}) async-start(bf16[64,16,256]{2,1,0:T(8,128)(2,1)} %pad_maximum_fusion.2), calls=%async_computation.2 | async-start | bytes 1048576 | tf_op jit(solution)/shard_map/all_to_all | solution.py:158
  108.6 7.8 %copy-start.32 = (s32[16]{0:T(128)S(1)}, s32[16]{0:T(128)}, u32[]{:S(2)}) copy-start(s32[16]{0:T(128)} %copy-done.30) | copy-start | bytes 196
  110.3 6.5 %copy-start.20 = (bf16[128,8,128]{2,1,0:T(8,128)(2,1)S(1)}, bf16[128,8,128]{2,1,0:T(8,128)(2,1)}, u32[]{:S(2)}) copy-start(bf16[128,8,128]{2,1,0:T(8,128)(2,1)} %copy-done.17) | copy-start | bytes 786436
  110.3 10.8 %collective-permute-start.7 = (f32[8,32,1024]{2,1,0:T(8,128)}, f32[8,32,1024]{2,1,0:T(8,128)}, u32[]{:S(2)}, u32[]{:S(2)}) collective-permute-start(f32[8,32,1024]{2,1,0:T(8,128)} %fusion.63), channel_id=1, source_target_pairs={{0,64},{64,0},{1,65},{65,1},{2,66},{66,2},{3,67},{67,3},{4,68},{68... | collective-permute-start | bytes 3145736 | tf_op jit(solution)/shard_map/ppermute | solution.py:182
  116.8 2.9 %copy-start.27 = (s32[128]{0:T(128)S(1)}, s32[128]{0:T(128)}, u32[]{:S(2)}) copy-start(s32[128]{0:T(128)} %copy-done.25) | copy-start | bytes 1540
  121.3 9.6 %copy-start.13 = (f32[1,8,32,1024]{3,2,1,0:T(8,128)S(1)}, f32[1,8,32,1024]{3,2,1,0:T(8,128)}, u32[]{:S(2)}) copy-start(f32[1,8,32,1024]{3,2,1,0:T(8,128)} %param.17) | copy-start | bytes 3145732
  121.3 9.6 %copy-start.14 = (f32[1,8,32,1024]{3,2,1,0:T(8,128)S(1)}, f32[1,8,32,1024]{3,2,1,0:T(8,128)}, u32[]{:S(2)}) copy-start(f32[1,8,32,1024]{3,2,1,0:T(8,128)} %param.16) | copy-start | bytes 3145732
  123.0 7.9 %collective-permute-start.8 = (f32[8,32,1024]{2,1,0:T(8,128)S(1)}, f32[8,32,1024]{2,1,0:T(8,128)S(1)}, u32[]{:S(2)}, u32[]{:S(2)}) collective-permute-start(f32[8,32,1024]{2,1,0:T(8,128)S(1)} %bitcast_multiply_fusion.5), channel_id=1, source_target_pairs={{64,0},{65,1},{66,2},{67,3},{68,4},{69,5},{70,6},{71,7},{72,8},{73... | collective-permute-start | bytes 3145736 | tf_op jit(solution)/shard_map/ppermute | solution.py:29
  134.2 5.5 %collective-permute-start.9 = (f32[8,32,1024]{2,1,0:T(8,128)}, f32[8,32,1024]{2,1,0:T(8,128)S(1)}, u32[]{:S(2)}, u32[]{:S(2)}) collective-permute-start(f32[8,32,1024]{2,1,0:T(8,128)} %get-tuple-element.10), channel_id=1, source_target_pairs={{0,64},{1,65},{2,66},{3,67},{4,68},{5,69},{6,70},{7,71},{8,72},{9,... | collective-permute-start | bytes 3145736 | tf_op jit(solution)/shard_map/ppermute | solution.py:29
  135.7 3.4 %copy-start.24 = (bf16[1,16,128]{2,1,0:T(8,128)(2,1)S(1)}, bf16[1,16,128]{2,1,0:T(8,128)(2,1)}, u32[]{:S(2)}) copy-start(bf16[1,16,128]{2,1,0:T(8,128)(2,1)} %param.24) | copy-start | bytes 12292
  (15 other events, 22.9 us)

commit v8 on v7

--- a/solution.py
+++ b/solution.py
@@ -50,8 +50,8 @@
     slots, lanes, touched = col_oh.shape
     groups = col_count // lanes
     lines = jnp.einsum(
-        "sr,lrc->slc", row_oh, fields.astype(jnp.bfloat16), preferred_element_type=jnp.float32
-    ).astype(jnp.bfloat16)
+        "sr,lrc->slc", row_oh, fields.astype(jnp.bfloat16), preferred_element_type=jnp.bfloat16
+    )
     lines = lines.reshape(slots, levels, groups, lanes)
     picked = jnp.einsum("slab,sbj->slaj", lines, col_oh, preferred_element_type=jnp.bfloat16)
     return jnp.sum(picked * group_mask[:, None, :, :].astype(jnp.bfloat16), axis=2)

time: 143 us -> 141 us (0.986)
  other arithmetic: 33.2 us -> 30.7 us
  local copies, waits for them, and re-layouts: 14.5 us -> 12.6 us
  waiting for transfers between devices: 11.5 us -> 13 us
    unnamed x0 -> x1, other arithmetic: none -> 1.81 us
    mul x2, other arithmetic: 4.47 us -> 2.89 us  [on_device(): decayed = decay_field * r_dual]
    select_n x2 -> x1, other arithmetic: 6.02 us -> 4.64 us  [on_device(): chosen = jnp.where(tm_here == 0, increment, dual_model)]
    unnamed x70 -> x67, local copies, waits for them, and re-layouts: 3.24 us -> 3 us
  transfers between devices with their start and end apart: 13 -> 13, of which waited for: 5 -> 5; matrix products, arithmetic and copies ran while one was open for 32% -> 30% of each run, Pallas kernels for 0% -> 0%
where the time goes in v8:
time: 141 us; the launch traced here: 139 us
  starting transfers between devices  54.8 us (39%)
  other arithmetic  30.7 us (22%)
  matrix products  26.6 us (19%)
  waiting for transfers between devices  13 us (9%)
  local copies, waits for them, and re-layouts  12.6 us (9%)
    ppermute x4, starting transfers between devices, shifted(): return lax.ppermute(value, axis, pairs)  14.8 us
    all_to_all x2, starting transfers between devices, on_device(): got = lax.all_to_all(both, 'space', split_axis=0, concat_axis=0, tiled=True)  13.6 us
    all_to_all x1, starting transfers between devices, on_device(): lax.all_to_all(packed_cells.reshape(owners_count, capacity, touched), 'sp...  12 us
    sub x2, other arithmetic, on_device(): source = r_model - err_field * upward  7.4 us
    ppermute x2, starting transfers between devices, with_halo(): lax.ppermute(tail, axis, [(i, i + 1) for i in range(ends)])  6.89 us
    dot_general x2, matrix products, gather_cols(): jnp.einsum('slab,sbj->slaj', lines, col_oh, preferred_element_type=jnp.bf...  6.6 us
    dot_general x2, matrix products, spread_cols(): jnp.einsum('slaj,sbj->slab', placed, col_oh, preferred_element_type=jnp.b...  5.79 us
    all_to_all x2, waiting for transfers between devices, on_device(): got = lax.all_to_all(both, 'space', split_axis=0, concat_axis=0, tiled=True)  5.28 us
  transfers between devices with their start and end apart: 13, of which 5 were waited for; matrix products, arithmetic and copies ran while one was open for 30% of the time, Pallas kernels for 0%

profile of v8, /device:TPU:1, one launch (start us, length us, event | category | flops | bytes accessed | tf_op | source)
XLA Modules:
  0.0 139.1 jit_solution(17205340632284985192)
XLA Ops:
  0.7 1.8 %fusion.86 = (bf16[8,4,8,8,128]{4,3,2,1,0:T(8,128)(2,1)S(1)}, f32[1,8,32,1024]{3,2,1,0:T(8,128)S(1)}) fusion(f32[1,8,32,1024]{3,2,1,0:T(8,128)} %param.13, f32[1,8,32,1024]{3,2,1,0:T(8,128)} %param.14, pred[]{:T(512)S(6)} %eq.84), kind=kLoop, calls=%fused_computation.103 | loop fusion | flops 524288 | bytes 3670017
  3.3 3.9 %collective-permute-start = (f32[2,8,2,1024]{3,2,1,0:T(2,128)}, f32[2,8,2,1024]{3,2,1,0:T(2,128)S(1)}, u32[]{:S(2)}, u32[]{:S(2)}) collective-permute-start(f32[2,8,2,1024]{3,2,1,0:T(2,128)} %get-tuple-element.12), channel_id=1, source_target_pairs={{0,1},{1,2},{2,3},{3,4},{4,5},{5,6},{6,7},{7,8},{8,9},{9,10},{10,1... | collective-permute-start | bytes 393224 | tf_op jit(solution)/shard_map/ppermute | solution.py:18
  7.2 1.3 collective-permute-start.1
  10.1 12.0 %all-to-all-start = ((s32[64,2,128]{2,1,0:T(2,128)}), s32[64,2,128]{2,1,0:T(2,128)S(1)}, u32[]{:S(2)}, u32[]{:S(2)}) async-start(s32[64,2,128]{2,1,0:T(2,128)} %bitcast.9), calls=%async_computation | async-start | bytes 131072 | tf_op jit(solution)/shard_map/all_to_all | solution.py:119
  22.1 2.8 %fusion.15 = bf16[16,1,1024]{2,1,0:T(2,128)(2,1)S(1)} fusion(bf16[1,16,128,1024]{3,2,1,0:T(8,128)(2,1)} %param.23, bf16[16,128,1]{1,0,2:T(8,128)(2,1)S(1)} %bitcast.250), kind=kOutput, calls=%fused_computation.13 | convolution fusion | flops 4194304 | bytes 4231168 | tf_op jit(solution)/shard_map/toj,to->tj/dot_general | solution.py:142
  25.7 4.8 %all-to-all-done = s32[64,2,128]{2,1,0:T(2,128)S(1)} async-done(((s32[64,2,128]{2,1,0:T(2,128)}), s32[64,2,128]{2,1,0:T(2,128)S(1)}, u32[]{:S(2)}, u32[]{:S(2)}) %all-to-all-start) | async-done | bytes 65568 | tf_op jit(solution)/shard_map/all_to_all | solution.py:119
  31.6 3.6 %multiply_reduce_fusion.1 = bf16[128,8,128]{2,1,0:T(8,128)(2,1)S(1)} fusion(s32[128,128]{1,0:T(8,128)S(1)} %get-tuple-element.39, bf16[128,8,8,128]{3,0,2,1:T(8,128)(2,1)S(1)} %fusion.87, bf16[128,8,128]{2,1,0:T(8,128)(2,1)S(1)} %convert_convert_fusion), kind=kOutput, calls=%fused_computation.29 | convolution fusion | flops 272498688 | bytes 2686976 | tf_op jit(solution)/shard_map/slab,sbj->slaj/dot_general | solution.py:56
  36.0 5.0 %all-to-all-start.1 = ((bf16[64,16,256]{2,1,0:T(8,128)(2,1)}), bf16[64,16,256]{2,1,0:T(8,128)(2,1)S(1)}, u32[]{:S(2)}, u32[]{:S(2)}) async-start(bf16[64,16,256]{2,1,0:T(8,128)(2,1)} %pad_maximum_fusion.1), calls=%async_computation.1 | async-start | bytes 1048576 | tf_op jit(solution)/shard_map/all_to_all | solution.py:158
  45.2 1.7 %fusion.69 = f32[8,32,1024]{2,1,0:T(8,128)} fusion(f32[8,34,1024]{2,1,0:T(8,128)S(1)} %multiply_multiply_fusion.1, f32[8,32,1023]{2,1,0:T(8,128)S(1)} %get-tuple-element.23, f32[8,32,1]{2,1,0:T(8,128)S(1)} %get-tuple-element.25, f32[8,32,1]{2,1,0:T(8,128)S(1)} %get-tuple-element.24, f32[8,32,1023]{2,1,0:T(8,128)S(1)} %get-tuple-element.22, ...), kind=kLoop, calls=%fused_computation.73 | loop fusion | flops 2621440 | bytes 7340064 | tf_op jit(solution)/shard_map/mul | solution.py:44
  46.9 2.3 %collective-permute-start.2 = (f32[8,32,1024]{2,1,0:T(8,128)}, f32[8,32,1024]{2,1,0:T(8,128)}, u32[]{:S(2)}, u32[]{:S(2)}) collective-permute-start(f32[8,32,1024]{2,1,0:T(8,128)} %fusion.69), channel_id=1, source_target_pairs={{0,64},{64,0},{1,65},{65,1},{2,66},{66,2},{3,67},{67,3},{4,68},{68... | collective-permute-start | bytes 3145736 | tf_op jit(solution)/shard_map/ppermute | solution.py:182
  49.2 2.9 %all-to-all-done.1 = bf16[64,16,256]{2,1,0:T(8,128)(2,1)S(1)} async-done(((bf16[64,16,256]{2,1,0:T(8,128)(2,1)}), bf16[64,16,256]{2,1,0:T(8,128)(2,1)S(1)}, u32[]{:S(2)}, u32[]{:S(2)}) %all-to-all-start.1) | async-done | bytes 524320 | tf_op jit(solution)/shard_map/all_to_all | solution.py:158
  52.9 2.9 %fusion.5 = bf16[128,8,8,128]{3,2,1,0:T(8,128)(2,1)S(1)} fusion(s32[128,128]{1,0:T(8,128)S(1)} %copy-done.20, bf16[128,8,128]{2,1,0:T(8,128)(2,1)S(1)} %bitcast.246, bf16[128,8,128]{2,1,0:T(8,128)(2,1)S(1)} %convert_convert_fusion), kind=kOutput, calls=%fused_computation.5 | convolution fusion | flops 271581184 | bytes 2686976 | tf_op jit(solution)/shard_map/slaj,sbj->slab/dot_general | solution.py:66
  55.8 1.3 fusion.37
  57.4 2.5 %bitcast_multiply_fusion.7 = f32[8,32,1024]{2,1,0:T(8,128)} fusion(f32[1,8,32,1024]{3,2,1,0:T(8,128)S(1)} %copy-done.6, f32[8,8,4,8,128]{4,3,2,1,0:T(8,128)S(1)} %fusion.37, f32[8,32,1024]{2,1,0:T(8,128)} %collective-permute-done.2, f32[]{:T(128)S(6)} %sub.85, f32[1,8,32,1024]{3,2,1,0:T(8,128)S(1)} %copy-done.4), kind=kLoop, calls=%fused_computation.87 | loop fusion | flops 1310720 | bytes 5242884 | tf_op jit(solution)/shard_map/mul | solution.py:186
  59.9 6.1 %collective-permute-start.3 = (f32[8,32,1024]{2,1,0:T(8,128)}, f32[8,32,1024]{2,1,0:T(8,128)}, u32[]{:S(2)}, u32[]{:S(2)}) collective-permute-start(f32[8,32,1024]{2,1,0:T(8,128)} %bitcast_multiply_fusion.7), channel_id=1, source_target_pairs={{64,0},{65,1},{66,2},{67,3},{68,4},{69,5},{70,6},{71,7},{72,8},{73... | collective-permute-start | bytes 3145736 | tf_op jit(solution)/shard_map/ppermute | solution.py:29
  69.2 4.4 %fusion.72 = f32[8,32,1024]{2,1,0:T(8,128)} fusion(f32[1,8,32,1024]{3,2,1,0:T(8,128)} %param.17, f32[1,8,32,1024]{3,2,1,0:T(8,128)} %param.16, f32[1,8,32,1024]{3,2,1,0:T(8,128)} %param.13, f32[1,8,32,1024]{3,2,1,0:T(8,128)S(1)} %copy-done.4, f32[8,32,1024]{2,1,0:T(8,128)} %collective-permute-done.2, f32[]{:T(128)S(6)} %sub.92, ...), kind=kLoop, calls=%fused_computation.80 | loop fusion | flops 3145728 | bytes 8388616 | tf_op jit(solution)/shard_map/sub | solution.py:209
  73.6 1.6 %collective-permute-start.4 = (f32[8,32,1024]{2,1,0:T(8,128)}, f32[8,32,1024]{2,1,0:T(8,128)}, u32[]{:S(2)}, u32[]{:S(2)}) collective-permute-start(f32[8,32,1024]{2,1,0:T(8,128)} %fusion.72), channel_id=1, source_target_pairs={{0,64},{1,65},{2,66},{3,67},{4,68},{5,69},{6,70},{7,71},{8,72},{9,... | collective-permute-start | bytes 3145736 | tf_op jit(solution)/shard_map/ppermute | solution.py:29
  78.6 4.6 %broadcast_select_fusion = (f32[8,32,1024]{2,1,0:T(8,128)S(1)}, f32[8,32,1024]{2,1,0:T(8,128)S(1)}, f32[8,32,1024]{2,1,0:T(8,128)}) fusion(pred[]{:T(512)S(6)} %eq.84, f32[8,32,1024]{2,1,0:T(8,128)} %fusion.72, f32[8,32,1024]{2,1,0:T(8,128)} %collective-permute-done.4, f32[1,8,32,1024]{3,2,1,0:T(8,128)} %param.18, f32[1,8,32,1024]{3,2,1,0:T(8,128)} %param.13, ...), kind=kLoop, calls=%fused_computation.115 | loop fusion | flops 2621440 | bytes 11534341 | tf_op jit(solution)/shard_map/jit(_where)/select_n | solution.py:175
  85.0 3.0 %multiply_reduce_fusion = bf16[128,8,128]{2,1,0:T(8,128)(2,1)S(1)} fusion(s32[128,128]{1,0:T(8,128)S(1)} %copy-done.20, bf16[128,8,8,128]{3,2,0,1:T(8,128)(2,1)S(1)} %bitcast.235, bf16[128,8,128]{2,1,0:T(8,128)(2,1)S(1)} %copy-done.16), kind=kOutput, calls=%fused_computation.27 | convolution fusion | flops 272498688 | bytes 2686976 | tf_op jit(solution)/shard_map/slab,sbj->slaj/dot_general | solution.py:56
  88.7 2.9 %collective-permute-start.5 = (f32[8,2,1024]{2,1,0:T(2,128)}, f32[8,2,1024]{2,1,0:T(2,128)}, u32[]{:S(2)}, u32[]{:S(2)}) collective-permute-start(f32[8,2,1024]{2,1,0:T(2,128)} %get-tuple-element.30), channel_id=1, source_target_pairs={{0,1},{1,2},{2,3},{3,4},{4,5},{5,6},{6,7},{7,8},{8,9},{9,10},{10,1... | collective-permute-start | bytes 196616 | tf_op jit(solution)/shard_map/ppermute | solution.py:18
  93.8 8.6 %all-to-all-start.2 = ((bf16[64,16,256]{2,1,0:T(8,128)(2,1)}), bf16[64,16,256]{2,1,0:T(8,128)(2,1)}, u32[]{:S(2)}, u32[]{:S(2)}) async-start(bf16[64,16,256]{2,1,0:T(8,128)(2,1)} %pad_maximum_fusion.2), calls=%async_computation.2 | async-start | bytes 1048576 | tf_op jit(solution)/shard_map/all_to_all | solution.py:158
  102.5 1.7 %maximum_multiply_fusion = f32[8,36,1024]{2,1,0:T(8,128)S(1)} fusion(f32[8,2,1024]{2,1,0:T(2,128)} %collective-permute-done.6, f32[8,32,1024]{2,1,0:T(8,128)S(1)} %copy-done.10, f32[8,2,1024]{2,1,0:T(2,128)} %collective-permute-done.5, f32[2,8,36,1024]{3,2,1,0:T(8,128)} %copy-done.3), kind=kLoop, calls=%fused_computation.49 | loop fusion | flops 884736 | bytes 3538944 | tf_op jit(solution)/shard_map/mul | solution.py:35
  106.5 1.7 %fusion.63 = f32[8,32,1024]{2,1,0:T(8,128)} fusion(f32[8,34,1024]{2,1,0:T(8,128)S(1)} %multiply_multiply_fusion, f32[8,32,1023]{2,1,0:T(8,128)S(1)} %get-tuple-element.15, f32[8,32,1]{2,1,0:T(8,128)S(1)} %get-tuple-element.17, f32[8,32,1]{2,1,0:T(8,128)S(1)} %get-tuple-element.16, f32[8,32,1023]{2,1,0:T(8,128)S(1)} %get-tuple-element.14, ...), kind=kLoop, calls=%fused_computation.66 | loop fusion | flops 2621440 | bytes 7340064 | tf_op jit(solution)/shard_map/mul | solution.py:44
  108.2 2.7 %collective-permute-start.7 = (f32[8,32,1024]{2,1,0:T(8,128)}, f32[8,32,1024]{2,1,0:T(8,128)S(1)}, u32[]{:S(2)}, u32[]{:S(2)}) collective-permute-start(f32[8,32,1024]{2,1,0:T(8,128)} %fusion.63), channel_id=1, source_target_pairs={{0,64},{64,0},{1,65},{65,1},{2,66},{66,2},{3,67},{67,3},{4,68},{68... | collective-permute-start | bytes 3145736 | tf_op jit(solution)/shard_map/ppermute | solution.py:182
  110.9 2.4 %all-to-all-done.2 = bf16[64,16,256]{2,1,0:T(8,128)(2,1)} async-done(((bf16[64,16,256]{2,1,0:T(8,128)(2,1)}), bf16[64,16,256]{2,1,0:T(8,128)(2,1)}, u32[]{:S(2)}, u32[]{:S(2)}) %all-to-all-start.2) | async-done | bytes 524320 | tf_op jit(solution)/shard_map/all_to_all | solution.py:158
  114.7 2.9 %fusion.1 = bf16[128,8,8,128]{3,2,1,0:T(8,128)(2,1)S(1)} fusion(s32[128,128]{1,0:T(8,128)S(1)} %copy-done.20, bf16[128,8,128]{2,1,0:T(8,128)(2,1)S(1)} %bitcast.244, bf16[128,8,128]{2,1,0:T(8,128)(2,1)S(1)} %copy-done.17), kind=kOutput, calls=%fused_computation.3 | convolution fusion | flops 271581184 | bytes 2686976 | tf_op jit(solution)/shard_map/slaj,sbj->slab/dot_general | solution.py:66
  117.7 1.3 fusion.40
  120.0 5.8 %collective-permute-start.8 = (f32[8,32,1024]{2,1,0:T(8,128)S(1)}, f32[8,32,1024]{2,1,0:T(8,128)S(1)}, u32[]{:S(2)}, u32[]{:S(2)}) collective-permute-start(f32[8,32,1024]{2,1,0:T(8,128)S(1)} %bitcast_multiply_fusion.5), channel_id=1, source_target_pairs={{64,0},{65,1},{66,2},{67,3},{68,4},{69,5},{70,6},{71,7},{72,8},{73... | collective-permute-start | bytes 3145736 | tf_op jit(solution)/shard_map/ppermute | solution.py:29
  125.8 2.2 %collective-permute-done.8 = f32[8,32,1024]{2,1,0:T(8,128)S(1)} collective-permute-done((f32[8,32,1024]{2,1,0:T(8,128)S(1)}, f32[8,32,1024]{2,1,0:T(8,128)S(1)}, u32[]{:S(2)}, u32[]{:S(2)}) %collective-permute-start.8) | collective-permute-done | bytes 1048608 | tf_op jit(solution)/shard_map/ppermute | solution.py:29
  128.0 3.0 %fusion.75 = (f32[8,32,1024]{2,1,0:T(8,128)S(1)}, f32[1,8,32,1024]{3,2,1,0:T(8,128)}) fusion(f32[8,32,1024]{2,1,0:T(8,128)S(1)} %copy-done.8, f32[1,8,32,1024]{3,2,1,0:T(8,128)S(1)} %copy-done.11, f32[1,8,32,1024]{3,2,1,0:T(8,128)S(1)} %copy-done.12, f32[8,32,1024]{2,1,0:T(8,128)S(1)} %get-tuple-element.8, f32[8,32,1024]{2,1,0:T(8,128)} %copy-done.14, ...), kind=kLoop, calls=%fused_computation.83 | loop fusion | flops 3407872 | bytes 9437192 | tf_op jit(solution)/shard_map/sub | solution.py:209
  132.5 3.4 %fusion.9 = f32[16,1,128]{2,1,0:T(1,128)S(1)} fusion(bf16[16,1024,1]{1,2,0:T(2,128)(2,1)S(1)} %copy.53, bf16[1,16,128,1024]{3,2,1,0:T(8,128)(2,1)} %param.23), kind=kOutput, calls=%fused_computation.7 | convolution fusion | flops 4194304 | bytes 4235264 | tf_op jit(solution)/shard_map/toj,tj->to/dot_general | solution.py:189
  136.5 2.6 %fusion.80 = f32[1,8,32,1024]{3,2,1,0:T(8,128)} fusion(f32[8,32,1024]{2,1,0:T(8,128)S(1)} %get-tuple-element.8, f32[8,32,1024]{2,1,0:T(8,128)S(1)} %get-tuple-element.10, f32[8,32,1024]{2,1,0:T(8,128)} %collective-permute-done.9, f32[1,8,32,1024]{3,2,1,0:T(8,128)S(1)} %copy-done.7), kind=kLoop, calls=%fused_computation.92 | loop fusion | flops 786432 | bytes 5242880 | tf_op jit(solution)/shard_map/broadcast_in_dim | solution.py:214
  (127 shorter events, 27.8 us)
Async XLA Ops:
  0.6 8.2 %copy-start = (s32[1,16,128]{2,1,0:T(8,128)S(1)}, s32[1,16,128]{2,1,0:T(8,128)}, u32[]{:S(2)}) copy-start(s32[1,16,128]{2,1,0:T(8,128)} %param.22) | copy-start | bytes 24580
  2.5 6.0 %copy-start.32 = (s32[1,16]{1,0:T(1,128)S(1)}, s32[1,16]{1,0:T(1,128)}, u32[]{:S(2)}) copy-start(s32[1,16]{1,0:T(1,128)} %param.21) | copy-start | bytes 196
  2.5 19.6 %copy-start.18 = (bf16[1,16,128]{2,1,0:T(8,128)(2,1)S(1)}, bf16[1,16,128]{2,1,0:T(8,128)(2,1)}, u32[]{:S(2)}) copy-start(bf16[1,16,128]{2,1,0:T(8,128)(2,1)} %param.15) | copy-start | bytes 12292
  3.3 37.7 %collective-permute-start = (f32[2,8,2,1024]{3,2,1,0:T(2,128)}, f32[2,8,2,1024]{3,2,1,0:T(2,128)S(1)}, u32[]{:S(2)}, u32[]{:S(2)}) collective-permute-start(f32[2,8,2,1024]{3,2,1,0:T(2,128)} %get-tuple-element.12), channel_id=1, source_target_pairs={{0,1},{1,2},{2,3},{3,4},{4,5},{5,6},{6,7},{7,8},{8,9},{9,10},{10,1... | collective-permute-start | bytes 393224 | tf_op jit(solution)/shard_map/ppermute | solution.py:18
  7.2 33.8 %collective-permute-start.1 = (f32[2,8,2,1024]{3,2,1,0:T(2,128)S(1)}, f32[2,8,2,1024]{3,2,1,0:T(2,128)S(1)}, u32[]{:S(2)}, u32[]{:S(2)}) collective-permute-start(f32[2,8,2,1024]{3,2,1,0:T(2,128)S(1)} %get-tuple-element.13), channel_id=1, source_target_pairs={{1,0},{2,1},{3,2},{4,3},{5,4},{6,5},{7,6},{8,7},{9,8},{10,9},{11,1... | collective-permute-start | bytes 393224 | tf_op jit(solution)/shard_map/ppermute | solution.py:20
  10.1 20.4 %all-to-all-start = ((s32[64,2,128]{2,1,0:T(2,128)}), s32[64,2,128]{2,1,0:T(2,128)S(1)}, u32[]{:S(2)}, u32[]{:S(2)}) async-start(s32[64,2,128]{2,1,0:T(2,128)} %bitcast.9), calls=%async_computation | async-start | bytes 131072 | tf_op jit(solution)/shard_map/all_to_all | solution.py:119
  22.1 43.9 %copy-start.29 = (s32[16]{0:T(128)}, s32[16]{0:T(128)S(1)}, u32[]{:S(2)}) copy-start(s32[16]{0:T(128)S(1)} %multiply_add_fusion) | copy-start | bytes 196
  30.6 25.2 %copy-start.24 = (s32[128]{0:T(128)}, s32[128]{0:T(128)S(1)}, u32[]{:S(2)}) copy-start(s32[128]{0:T(128)S(1)} %fusion.99) | copy-start | bytes 1540
  30.8 22.1 %copy-start.15 = (bf16[128,8,128]{2,1,0:T(8,128)(2,1)}, bf16[128,8,128]{2,1,0:T(8,128)(2,1)S(1)}, u32[]{:S(2)}) copy-start(bf16[128,8,128]{2,1,0:T(8,128)(2,1)S(1)} %convert_convert_fusion) | copy-start | bytes 786436
  36.0 16.1 %all-to-all-start.1 = ((bf16[64,16,256]{2,1,0:T(8,128)(2,1)}), bf16[64,16,256]{2,1,0:T(8,128)(2,1)S(1)}, u32[]{:S(2)}, u32[]{:S(2)}) async-start(bf16[64,16,256]{2,1,0:T(8,128)(2,1)} %pad_maximum_fusion.1), calls=%async_computation.1 | async-start | bytes 1048576 | tf_op jit(solution)/shard_map/all_to_all | solution.py:158
  45.2 7.7 %copy-start.20 = (s32[128,128]{1,0:T(8,128)S(1)}, s32[128,128]{1,0:T(8,128)}, u32[]{:S(2)}) copy-start(s32[128,128]{1,0:T(8,128)} %copy-done.19) | copy-start | bytes 196612
  46.9 10.3 %collective-permute-start.2 = (f32[8,32,1024]{2,1,0:T(8,128)}, f32[8,32,1024]{2,1,0:T(8,128)}, u32[]{:S(2)}, u32[]{:S(2)}) collective-permute-start(f32[8,32,1024]{2,1,0:T(8,128)} %fusion.69), channel_id=1, source_target_pairs={{0,64},{64,0},{1,65},{65,1},{2,66},{66,2},{3,67},{67,3},{4,68},{68... | collective-permute-start | bytes 3145736 | tf_op jit(solution)/shard_map/ppermute | solution.py:182
  59.9 9.3 %collective-permute-start.3 = (f32[8,32,1024]{2,1,0:T(8,128)}, f32[8,32,1024]{2,1,0:T(8,128)}, u32[]{:S(2)}, u32[]{:S(2)}) collective-permute-start(f32[8,32,1024]{2,1,0:T(8,128)} %bitcast_multiply_fusion.7), channel_id=1, source_target_pairs={{64,0},{65,1},{66,2},{67,3},{68,4},{69,5},{70,6},{71,7},{72,8},{73... | collective-permute-start | bytes 3145736 | tf_op jit(solution)/shard_map/ppermute | solution.py:29
  69.2 6.1 %copy-start.2 = (bf16[1,16,128,1024]{3,2,1,0:T(8,128)(2,1)S(1)}, bf16[1,16,128,1024]{3,2,1,0:T(8,128)(2,1)}, u32[]{:S(2)}) copy-start(bf16[1,16,128,1024]{3,2,1,0:T(8,128)(2,1)} %param.23) | copy-start | bytes 12582916
  73.6 2.8 %copy-start.21 = (bf16[1,16,128]{2,1,0:T(8,128)(2,1)S(1)}, bf16[1,16,128]{2,1,0:T(8,128)(2,1)}, u32[]{:S(2)}) copy-start(bf16[1,16,128]{2,1,0:T(8,128)(2,1)} %param.25) | copy-start | bytes 12292
  73.6 2.8 %copy-start.22 = (bf16[1,16,128]{2,1,0:T(8,128)(2,1)S(1)}, bf16[1,16,128]{2,1,0:T(8,128)(2,1)}, u32[]{:S(2)}) copy-start(bf16[1,16,128]{2,1,0:T(8,128)(2,1)} %param.24) | copy-start | bytes 12292
  73.6 5.0 %collective-permute-start.4 = (f32[8,32,1024]{2,1,0:T(8,128)}, f32[8,32,1024]{2,1,0:T(8,128)}, u32[]{:S(2)}, u32[]{:S(2)}) collective-permute-start(f32[8,32,1024]{2,1,0:T(8,128)} %fusion.72), channel_id=1, source_target_pairs={{0,64},{1,65},{2,66},{3,67},{4,68},{5,69},{6,70},{7,71},{8,72},{9,... | collective-permute-start | bytes 3145736 | tf_op jit(solution)/shard_map/ppermute | solution.py:29
  77.9 5.4 %copy-start.25 = (s32[128]{0:T(128)S(1)}, s32[128]{0:T(128)}, u32[]{:S(2)}) copy-start(s32[128]{0:T(128)} %copy-done.24) | copy-start | bytes 1540
  83.3 4.7 %copy-start.9 = (f32[8,32,1024]{2,1,0:T(8,128)}, f32[8,32,1024]{2,1,0:T(8,128)S(1)}, u32[]{:S(2)}) copy-start(f32[8,32,1024]{2,1,0:T(8,128)S(1)} %get-tuple-element.7) | copy-start | bytes 3145732
  88.7 13.8 %copy-start.10 = (f32[8,32,1024]{2,1,0:T(8,128)S(1)}, f32[8,32,1024]{2,1,0:T(8,128)}, u32[]{:S(2)}) copy-start(f32[8,32,1024]{2,1,0:T(8,128)} %copy-done.9) | copy-start | bytes 3145732
  88.7 13.7 %collective-permute-start.5 = (f32[8,2,1024]{2,1,0:T(2,128)}, f32[8,2,1024]{2,1,0:T(2,128)}, u32[]{:S(2)}, u32[]{:S(2)}) collective-permute-start(f32[8,2,1024]{2,1,0:T(2,128)} %get-tuple-element.30), channel_id=1, source_target_pairs={{0,1},{1,2},{2,3},{3,4},{4,5},{5,6},{6,7},{7,8},{8,9},{9,10},{10,1... | collective-permute-start | bytes 196616 | tf_op jit(solution)/shard_map/ppermute | solution.py:18
  91.7 10.8 %collective-permute-start.6 = (f32[8,2,1024]{2,1,0:T(2,128)S(1)}, f32[8,2,1024]{2,1,0:T(2,128)}, u32[]{:S(2)}, u32[]{:S(2)}) collective-permute-start(f32[8,2,1024]{2,1,0:T(2,128)S(1)} %get-tuple-element.31), channel_id=1, source_target_pairs={{1,0},{2,1},{3,2},{4,3},{5,4},{6,5},{7,6},{8,7},{9,8},{10,9},{11,1... | collective-permute-start | bytes 196616 | tf_op jit(solution)/shard_map/ppermute | solution.py:20
  93.8 19.4 %all-to-all-start.2 = ((bf16[64,16,256]{2,1,0:T(8,128)(2,1)}), bf16[64,16,256]{2,1,0:T(8,128)(2,1)}, u32[]{:S(2)}, u32[]{:S(2)}) async-start(bf16[64,16,256]{2,1,0:T(8,128)(2,1)} %pad_maximum_fusion.2), calls=%async_computation.2 | async-start | bytes 1048576 | tf_op jit(solution)/shard_map/all_to_all | solution.py:158
  106.5 7.8 %copy-start.31 = (s32[16]{0:T(128)S(1)}, s32[16]{0:T(128)}, u32[]{:S(2)}) copy-start(s32[16]{0:T(128)} %copy-done.29) | copy-start | bytes 196
  108.2 6.5 %copy-start.17 = (bf16[128,8,128]{2,1,0:T(8,128)(2,1)S(1)}, bf16[128,8,128]{2,1,0:T(8,128)(2,1)}, u32[]{:S(2)}) copy-start(bf16[128,8,128]{2,1,0:T(8,128)(2,1)} %copy-done.15) | copy-start | bytes 786436
  108.2 10.8 %collective-permute-start.7 = (f32[8,32,1024]{2,1,0:T(8,128)}, f32[8,32,1024]{2,1,0:T(8,128)S(1)}, u32[]{:S(2)}, u32[]{:S(2)}) collective-permute-start(f32[8,32,1024]{2,1,0:T(8,128)} %fusion.63), channel_id=1, source_target_pairs={{0,64},{64,0},{1,65},{65,1},{2,66},{66,2},{3,67},{67,3},{4,68},{68... | collective-permute-start | bytes 3145736 | tf_op jit(solution)/shard_map/ppermute | solution.py:182
  114.7 2.9 %copy-start.26 = (s32[128]{0:T(128)S(1)}, s32[128]{0:T(128)}, u32[]{:S(2)}) copy-start(s32[128]{0:T(128)} %copy-done.24) | copy-start | bytes 1540
  119.2 8.8 %copy-start.11 = (f32[1,8,32,1024]{3,2,1,0:T(8,128)S(1)}, f32[1,8,32,1024]{3,2,1,0:T(8,128)}, u32[]{:S(2)}) copy-start(f32[1,8,32,1024]{3,2,1,0:T(8,128)} %param.17) | copy-start | bytes 3145732
  119.2 8.8 %copy-start.12 = (f32[1,8,32,1024]{3,2,1,0:T(8,128)S(1)}, f32[1,8,32,1024]{3,2,1,0:T(8,128)}, u32[]{:S(2)}) copy-start(f32[1,8,32,1024]{3,2,1,0:T(8,128)} %param.16) | copy-start | bytes 3145732
  120.0 8.0 %collective-permute-start.8 = (f32[8,32,1024]{2,1,0:T(8,128)S(1)}, f32[8,32,1024]{2,1,0:T(8,128)S(1)}, u32[]{:S(2)}, u32[]{:S(2)}) collective-permute-start(f32[8,32,1024]{2,1,0:T(8,128)S(1)} %bitcast_multiply_fusion.5), channel_id=1, source_target_pairs={{64,0},{65,1},{66,2},{67,3},{68,4},{69,5},{70,6},{71,7},{72,8},{73... | collective-permute-start | bytes 3145736 | tf_op jit(solution)/shard_map/ppermute | solution.py:29
  131.0 5.5 %collective-permute-start.9 = (f32[8,32,1024]{2,1,0:T(8,128)S(1)}, f32[8,32,1024]{2,1,0:T(8,128)}, u32[]{:S(2)}, u32[]{:S(2)}) collective-permute-start(f32[8,32,1024]{2,1,0:T(8,128)S(1)} %get-tuple-element.10), channel_id=1, source_target_pairs={{0,64},{1,65},{2,66},{3,67},{4,68},{5,69},{6,70},{7,71},{8,72},{9,... | collective-permute-start | bytes 3145736 | tf_op jit(solution)/shard_map/ppermute | solution.py:29
  132.5 3.4 %copy-start.23 = (bf16[1,16,128]{2,1,0:T(8,128)(2,1)S(1)}, bf16[1,16,128]{2,1,0:T(8,128)(2,1)}, u32[]{:S(2)}) copy-start(bf16[1,16,128]{2,1,0:T(8,128)(2,1)} %param.24) | copy-start | bytes 12292
  (14 other events, 18.2 us)
